TPU v7x, 256 devices: a whole 4x4x8 slice. The times are simulated.
256 devices in a mesh: row: 8 (over y_lo, x), col: 32 (over y_hi, z, core).
Axes of the slice: x: 4, y: 4 (y_hi: 2, y_lo: 2; y = y_hi * 2 + y_lo), z: 8, core: 2. Of those that a mesh axis runs over, the one named last changes fastest.
Arguments:
- features: bfloat16 [65536, 256], P(('col', 'row')), may hold values from -6 to 6
- weight: bfloat16 [256, 256], replicated, may hold values from -0.375 to 0.375
- cotangent: bfloat16 [65536, 256], P(('row', 'col')), may hold values from -6 to 6
- tile_rows: int32 [8, 32, 176], P('row', 'col'), may hold values from 0 to 63
- tile_cols: int32 [8, 32, 176], P('row', 'col'), may hold values from 0 to 15
- tile_weights: int32 [8, 32, 176, 128, 128], P('row', 'col'), may hold values from 0 to 3, as said below
- tile_count: int32 [8, 32], P('row', 'col'), may hold values from 44 to 176, as said below
Outputs:
- hidden: bfloat16 [65536, 256], P(('row', 'col'))
- weight_grad: float32 [256, 256], replicated
- feature_grad: bfloat16 [65536, 256], P(('col', 'row'))
Inputs may be any that keep to these rules, and one draw needn't show every extreme that they name: `tile_count`: one row group and column group has all 176 slots live, another a quarter of them. `tile_weights`: about one entry in 128 is nonzero.
All inputs are finite; a program needn't handle non-finite values.
Results may differ from a plain program's by a relative error of at most 0.006.
Values may be sent and summed in bfloat16 or wider, within the bound.
No kernel may reach another device: no remote copies, remote signals or barrier semaphores. Data moves between devices by JAX's collectives and lax.ppermute only.
A program may use at most 128 MiB of HBM per device.

v0:
```python
import math

import jax
import jax.numpy as jnp
from jax import lax
from jax.sharding import PartitionSpec as P

SPARSITY = 128


def slot_pass(
    tiles_all, slot_order, begin_pos, end_pos, fetcher, placer, accum, per_block, transpose
):
    slot_total = slot_order.shape[0]

    def block_step(block_id, summed):
        positions = begin_pos + block_id * per_block + jnp.arange(per_block, dtype=jnp.int32)
        usable = positions < end_pos
        chosen = slot_order[jnp.minimum(positions, slot_total - 1)]
        tile_vals = jnp.take(tiles_all, chosen, axis=0).astype(jnp.bfloat16)
        pieces = fetcher(chosen)
        if transpose:
            product = jnp.einsum(
                "sji,sjf->sif", tile_vals, pieces, preferred_element_type=jnp.float32
            )
        else:
            product = jnp.einsum(
                "sij,sjf->sif", tile_vals, pieces, preferred_element_type=jnp.float32
            )
        product = jnp.where(usable[:, None, None], product, 0.0)
        targets = jnp.where(usable, placer(chosen), 0)
        return summed.at[targets].add(product)

    blocks = (end_pos - begin_pos + per_block - 1) // per_block
    return lax.fori_loop(0, blocks, block_step, accum)


def dense_layer(aggregate, weight, cotangent):
    preact = jnp.dot(aggregate, weight, preferred_element_type=jnp.float32)
    hidden = jax.nn.silu(preact).astype(jnp.bfloat16)
    sigma = jax.nn.sigmoid(preact)
    grad_pre = (cotangent.astype(jnp.float32) * sigma * (1.0 + preact * (1.0 - sigma))).astype(
        jnp.bfloat16
    )
    return (hidden, grad_pre)


def on_device(features, weight, cotangent, tile_rows, tile_cols, tile_weights, tile_count):
    node_dev = cotangent.shape[0]
    width = features.shape[1]
    slot_total = tile_weights.shape[2]
    tile_len = tile_weights.shape[-1]
    sparsity_value = SPARSITY
    fan_value = slot_total * tile_len * tile_len // (node_dev * sparsity_value)
    scale = 1.0 / math.sqrt(2.0 * fan_value)
    row_len = node_dev * lax.axis_size("col")
    col_len = node_dev * lax.axis_size("row")
    row_tiles = row_len // tile_len
    col_tiles = col_len // tile_len
    nodes_all = row_len * lax.axis_size("row")
    per_block = math.gcd(slot_total, 16)
    row_ids = tile_rows[0, 0]
    col_ids = tile_cols[0, 0]
    weights_all = tile_weights[0, 0]
    live = tile_count[0, 0]
    slot_index = jnp.arange(slot_total, dtype=jnp.int32)
    source = lax.all_gather(features, "row", axis=0, tiled=True)
    source_tiles = source.reshape(col_tiles, tile_len, width)

    def feature_pieces(chosen):
        return jnp.take(source_tiles, col_ids[chosen], axis=0)

    def row_place(chosen):
        return row_ids[chosen]

    empty = jnp.zeros((row_tiles, tile_len, width), jnp.float32)
    summed = slot_pass(
        weights_all, slot_index, 0, live, feature_pieces, row_place, empty, per_block, False
    )
    partial_value = summed.reshape(row_len, width) * scale
    aggregate = lax.psum_scatter(partial_value, "col", scatter_dimension=0, tiled=True).astype(
        jnp.bfloat16
    )
    hidden, grad_own = dense_layer(aggregate, weight, cotangent)
    weight_part = lax.dot_general(
        aggregate, grad_own, (((0,), (0,)), ((), ())), preferred_element_type=jnp.float32
    )
    grad_agg = jnp.dot(grad_own, weight.T, preferred_element_type=jnp.float32).astype(jnp.bfloat16)
    weight_grad = lax.psum(weight_part, ("row", "col")) / math.sqrt(nodes_all)

    def col_place(chosen):
        return col_ids[chosen]

    back_empty = jnp.zeros((col_tiles, tile_len, width), jnp.float32)
    grad_source = lax.all_gather(grad_agg, "col", axis=0, tiled=True)
    grad_tiles = grad_source.reshape(row_tiles, tile_len, width)

    def grad_pieces_all(chosen):
        return jnp.take(grad_tiles, row_ids[chosen], axis=0)

    back_summed = slot_pass(
        weights_all, slot_index, 0, live, grad_pieces_all, col_place, back_empty, per_block, True
    )
    back_partial = back_summed.reshape(col_len, width) * scale
    feature_grad = lax.psum_scatter(back_partial, "row", scatter_dimension=0, tiled=True).astype(
        jnp.bfloat16
    )
    return (hidden, weight_grad, feature_grad)


def solution(mesh):
    in_specs = (
        P(("col", "row"), None),
        P(),
        P(("row", "col"), None),
        P("row", "col", None),
        P("row", "col", None),
        P("row", "col", None, None, None),
        P("row", "col"),
    )
    out_specs = (P(("row", "col"), None), P(), P(("col", "row"), None))
    return jax.shard_map(
        on_device, mesh=mesh, in_specs=in_specs, out_specs=out_specs, check_vma=False
    )
```

profile of v0, /device:TPU:8, one launch (start us, length us, event | category | flops | bytes accessed | tf_op | source)
XLA Modules:
  0.0 809.5 jit_solution(17250384771919868959)
XLA Ops:
  8.6 44.4 %all-gather.3.cloned.1.call-done = bf16[2048,256]{1,0:T(8,128)(2,1)} async-done(((bf16[256,256]{1,0:T(8,128)(2,1)}), bf16[2048,256]{1,0:T(8,128)(2,1)}) %all-gather.3.cloned.1.call-update) | async-done | bytes 1048592 | tf_op jit(solution)/shard_map/all_gather | solution.py:67
  53.0 4.3 broadcast_in_dim.68
  57.3 88.1 %while.22 = (s32[]{:T(128)}, f32[64,128,256]{2,1,0:T(8,128)}, s32[]{:T(128)}, s32[]{:T(128)}, s32[176]{0:T(256)S(1)}, /*index=5*/s32[176,128,128]{2,1,0:T(8,128)...) while((s32[]{:T(128)}, f32[64,128,256]{2,1,0:T(8,128)}, s32[]{:T(128)}, ...), condition=%wide.region_2.4_spmd.clone, body=%wide.region_0.3_spmd.clone.sunk | while | flops 136319520 | bytes 14699109 | solution.py:35
  60.6 5.9 gather_fusion.4
  70.2 4.6 scatter_fusion
  78.2 5.9 gather_fusion.4
  87.8 4.6 scatter_fusion
  95.7 5.9 gather_fusion.4
  105.3 4.6 scatter_fusion
  113.2 5.9 gather_fusion.4
  122.8 4.5 scatter_fusion
  130.6 5.9 gather_fusion.4
  140.3 5.1 scatter_fusion
  145.4 8.1 broadcast_multiply_fusion
  153.5 256.0 %reduce-scatter.3.cloned.1.call-done = f32[256,256]{1,0:T(8,128)} async-done(((f32[8192,256]{1,0:T(8,128)}), f32[256,256]{1,0:T(8,128)}) %reduce-scatter.3.cloned.1.call-update) | async-done | bytes 262160 | tf_op jit(solution)/shard_map/reduce_scatter | solution.py:81
  413.5 84.1 %all-gather.5.cloned.1.call-done = bf16[8192,256]{1,0:T(8,128)(2,1)} async-done(((bf16[256,256]{1,0:T(8,128)(2,1)}), bf16[8192,256]{1,0:T(8,128)(2,1)}) %all-gather.5.cloned.1.call-update) | async-done | bytes 4194320 | tf_op jit(solution)/shard_map/all_gather | solution.py:95
  499.1 92.8 %while.23 = (s32[]{:T(128)}, f32[16,128,256]{2,1,0:T(8,128)}, s32[]{:T(128)}, s32[]{:T(128)}, s32[176]{0:T(256)S(1)}, /*index=5*/s32[176,128,128]{2,1,0:T(8,128)...) while((s32[]{:T(128)}, f32[16,128,256]{2,1,0:T(8,128)}, s32[]{:T(128)}, ...), condition=%wide.region_7.9_spmd.clone, body=%wide.region_5.8_spmd.clone.sunk | while | flops 136319520 | bytes 14699109 | solution.py:35
  503.4 5.9 gather_fusion.9
  513.2 4.4 scatter_fusion.1
  519.0 2.8 gather_fusion.8
  521.8 5.9 gather_fusion.9
  531.7 4.4 scatter_fusion.1
  537.5 2.8 gather_fusion.8
  540.4 5.9 gather_fusion.9
  550.3 4.4 scatter_fusion.1
  559.0 5.9 gather_fusion.9
  568.8 4.4 scatter_fusion.1
  577.5 5.9 gather_fusion.9
  587.3 4.6 scatter_fusion.1
  591.9 3.2 broadcast_multiply_fusion.1
  595.1 160.4 %all-reduce.2.cloned.1.call-done = f32[256,256]{1,0:T(8,128)} async-done(((f32[256,256]{1,0:T(8,128)}), f32[256,256]{1,0:T(8,128)}) %all-reduce.2.cloned.1.call-update) | async-done | bytes 262160 | tf_op jit(solution)/shard_map/psum | solution.py:89
  757.2 44.2 %reduce-scatter.5.cloned.1.call-done = f32[256,256]{1,0:T(8,128)} async-done(((f32[2048,256]{1,0:T(8,128)}), f32[256,256]{1,0:T(8,128)}) %reduce-scatter.5.cloned.1.call-update) | async-done | bytes 262160 | tf_op jit(solution)/shard_map/reduce_scatter | solution.py:105
  (194 shorter events, 79.2 us)
Async XLA Ops:
  7.2 402.4 %copy-start = (bf16[256,256]{1,0:T(8,128)(2,1)S(1)}, bf16[256,256]{1,0:T(8,128)(2,1)}, u32[]{:S(2)}) copy-start(bf16[256,256]{1,0:T(8,128)(2,1)} %param.14) | copy-start | bytes 393220
  7.2 45.8 %all-gather.3.cloned.1.call-start = ((), (), s32[]{:S(2)}) async-start(), calls=%async_computation.2 | async-start | bytes 1179648 | tf_op jit(solution)/shard_map/all_gather | solution.py:67
  7.9 401.6 %reduce-scatter.3.cloned.1.call-start = ((), (), s32[]{:S(2)}) async-start(), calls=%async_computation.3 | async-start | bytes 8650752 | tf_op jit(solution)/shard_map/reduce_scatter | solution.py:81
  53.0 4.3 copy-start.1
  53.0 4.3 copy-start.2
  153.5 256.1 %copy-start.4 = (bf16[256,256]{1,0:T(8,128)(2,1)S(1)}, bf16[256,256]{1,0:T(8,128)(2,1)}, u32[]{:S(2)}) copy-start(bf16[256,256]{1,0:T(8,128)(2,1)} %param.15) | copy-start | bytes 393220
  153.5 344.1 %all-gather.5.cloned.1.call-start = ((), (), s32[]{:S(2)}) async-start(), calls=%async_computation.5 | async-start | bytes 4325376 | tf_op jit(solution)/shard_map/all_gather | solution.py:95
  409.6 2.9 copy-start.3
  412.4 343.1 %all-reduce.2.cloned.1.call-start = ((), (), s32[]{:S(2)}) async-start(), calls=%async_computation.4 | async-start | bytes 524288 | tf_op jit(solution)/shard_map/psum | solution.py:89
  413.4 387.9 %reduce-scatter.5.cloned.1.call-start = ((), (), s32[]{:S(2)}) async-start(), calls=%async_computation.6 | async-start | bytes 2359296 | tf_op jit(solution)/shard_map/reduce_scatter | solution.py:105
Sparse Core Ops, SparseCore 0:
  9.8 43.1 all-gather.2
  153.6 255.8 reduce-scatter.2
  412.9 84.6 all-gather.4
  503.5 252.0 all-reduce.1
  757.9 43.3 reduce-scatter.4
where the time goes:
time: 814 us; the launch traced here: 809 us
  waiting for transfers between devices  590 us (72%)
  local copies, waits for them, and re-layouts  108 us (13%)
  other arithmetic  73.9 us (9%)
  matrix products  22.1 us (3%)
  between operations  14.5 us (2%)
    reduce_scatter x1, waiting for transfers between devices, on_device(): lax.psum_scatter(partial_value, 'col', scatter_dimension=0, tiled=True)  256 us
    psum x1, waiting for transfers between devices, on_device(): weight_grad = lax.psum(weight_part, ('row', 'col')) / math.sqrt(nodes_all)  160 us
    all_gather x1, waiting for transfers between devices, on_device(): grad_source = lax.all_gather(grad_agg, 'col', axis=0, tiled=True)  84.1 us
    gather x10, local copies, waits for them, and re-layouts, block_step(): tile_vals = jnp.take(tiles_all, chosen, axis=0).astype(jnp.bfloat16)  59.1 us
    scatter-add x10, other arithmetic, block_step(): return summed.at[targets].add(product)  45.7 us
    all_gather x1, waiting for transfers between devices, on_device(): source = lax.all_gather(features, 'row', axis=0, tiled=True)  44.4 us
    reduce_scatter x1, waiting for transfers between devices, on_device(): lax.psum_scatter(back_partial, 'row', scatter_dimension=0, tiled=True)  44.2 us
    gather x10, local copies, waits for them, and re-layouts, grad_pieces_all(): return jnp.take(grad_tiles, row_ids[chosen], axis=0)  17.4 us
  transfers between devices with their start and end apart: 5, of which 5 were waited for; matrix products, arithmetic and copies ran while one was open for 12% of the time, Pallas kernels for 0%

commit v1 on v0

v1 whole, which is shorter than its diff:
```python
import functools
import math

import jax
import jax.numpy as jnp
from jax import lax
from jax.experimental import pallas as pl
from jax.experimental.pallas import tpu as pltpu
from jax.sharding import PartitionSpec as P

SPARSITY = 128


def slot_kernel(live_ref, rows_ref, cols_ref, tiles_ref, src_ref, out_ref, *, per_block, scale, transpose):
    block_id = pl.program_id(0)

    @pl.when(block_id == 0)
    def _():
        out_ref[...] = jnp.zeros_like(out_ref)

    live = live_ref[0]
    for k in range(per_block):
        slot = block_id * per_block + k

        @pl.when(slot < live)
        def _():
            tile_vals = tiles_ref[k].astype(jnp.bfloat16)
            if transpose:
                piece = src_ref[rows_ref[slot]]
                product = lax.dot_general(
                    tile_vals, piece, (((0,), (0,)), ((), ())), preferred_element_type=jnp.float32
                )
                target = cols_ref[slot]
            else:
                piece = src_ref[cols_ref[slot]]
                product = jnp.dot(tile_vals, piece, preferred_element_type=jnp.float32)
                target = rows_ref[slot]
            out_ref[target] += product

    @pl.when(block_id == pl.num_programs(0) - 1)
    def _():
        out_ref[...] = out_ref[...] * scale


def slot_pass(live, row_ids, col_ids, tiles, source_tiles, out_tiles, scale, transpose):
    slot_total, tile_len, _ = tiles.shape
    width = source_tiles.shape[-1]
    per_block = math.gcd(slot_total, 16)

    def tile_block(block_id, live_ref, rows_ref, cols_ref):
        last = jnp.maximum(live_ref[0] - 1, 0) // per_block
        return (jnp.minimum(block_id, last), 0, 0)

    def whole(block_id, live_ref, rows_ref, cols_ref):
        return (0, 0, 0)

    grid_spec = pltpu.PrefetchScalarGridSpec(
        num_scalar_prefetch=3,
        grid=(slot_total // per_block,),
        in_specs=[
            pl.BlockSpec((per_block, tile_len, tile_len), tile_block),
            pl.BlockSpec(source_tiles.shape, whole),
        ],
        out_specs=pl.BlockSpec((out_tiles, tile_len, width), whole),
    )
    return pl.pallas_call(
        functools.partial(slot_kernel, per_block=per_block, scale=scale, transpose=transpose),
        grid_spec=grid_spec,
        out_shape=jax.ShapeDtypeStruct((out_tiles, tile_len, width), jnp.float32),
        compiler_params=pltpu.CompilerParams(
            dimension_semantics=("arbitrary",), vmem_limit_bytes=48 * 1024 * 1024
        ),
    )(live, row_ids, col_ids, tiles, source_tiles)


def dense_layer(aggregate, weight, cotangent):
    preact = jnp.dot(aggregate, weight, preferred_element_type=jnp.float32)
    hidden = jax.nn.silu(preact).astype(jnp.bfloat16)
    sigma = jax.nn.sigmoid(preact)
    grad_pre = (cotangent.astype(jnp.float32) * sigma * (1.0 + preact * (1.0 - sigma))).astype(
        jnp.bfloat16
    )
    return (hidden, grad_pre)


def on_device(features, weight, cotangent, tile_rows, tile_cols, tile_weights, tile_count):
    node_dev = cotangent.shape[0]
    width = features.shape[1]
    slot_total = tile_weights.shape[2]
    tile_len = tile_weights.shape[-1]
    sparsity_value = SPARSITY
    fan_value = slot_total * tile_len * tile_len // (node_dev * sparsity_value)
    scale = 1.0 / math.sqrt(2.0 * fan_value)
    row_len = node_dev * lax.axis_size("col")
    col_len = node_dev * lax.axis_size("row")
    row_tiles = row_len // tile_len
    col_tiles = col_len // tile_len
    nodes_all = row_len * lax.axis_size("row")
    row_ids = tile_rows[0, 0]
    col_ids = tile_cols[0, 0]
    weights_all = tile_weights[0, 0]
    live = tile_count[0, 0].reshape(1)
    source = lax.all_gather(features, "row", axis=0, tiled=True)
    source_tiles = source.reshape(col_tiles, tile_len, width)
    summed = slot_pass(live, row_ids, col_ids, weights_all, source_tiles, row_tiles, scale, False)
    partial_value = summed.reshape(row_len, width)
    aggregate = lax.psum_scatter(partial_value, "col", scatter_dimension=0, tiled=True).astype(
        jnp.bfloat16
    )
    hidden, grad_own = dense_layer(aggregate, weight, cotangent)
    weight_part = lax.dot_general(
        aggregate, grad_own, (((0,), (0,)), ((), ())), preferred_element_type=jnp.float32
    )
    grad_agg = jnp.dot(grad_own, weight.T, preferred_element_type=jnp.float32).astype(jnp.bfloat16)
    weight_grad = lax.psum(weight_part, ("row", "col")) / math.sqrt(nodes_all)
    grad_source = lax.all_gather(grad_agg, "col", axis=0, tiled=True)
    grad_tiles = grad_source.reshape(row_tiles, tile_len, width)
    back_summed = slot_pass(live, row_ids, col_ids, weights_all, grad_tiles, col_tiles, scale, True)
    back_partial = back_summed.reshape(col_len, width)
    feature_grad = lax.psum_scatter(back_partial, "row", scatter_dimension=0, tiled=True).astype(
        jnp.bfloat16
    )
    return (hidden, weight_grad, feature_grad)


def solution(mesh):
    in_specs = (
        P(("col", "row"), None),
        P(),
        P(("row", "col"), None),
        P("row", "col", None),
        P("row", "col", None),
        P("row", "col", None, None, None),
        P("row", "col"),
    )
    out_specs = (P(("row", "col"), None), P(), P(("col", "row"), None))
    return jax.shard_map(
        on_device, mesh=mesh, in_specs=in_specs, out_specs=out_specs, check_vma=False
    )
```

time: 814 us -> 641 us (0.79)
  local copies, waits for them, and re-layouts: 108 us -> 2.6 us
  other arithmetic: 73.9 us -> 3.29 us
  Pallas kernels: 0 us -> 29.4 us
  matrix products: 22.1 us -> 4.65 us
    gather x50 -> x0, local copies, waits for them, and re-layouts: 102 us -> none  [the longest x10 59.1 us: block_step(): tile_vals = jnp.take(tiles_all, chosen, axis=0).astype(jnp.bfloat16)]
    reduce_scatter x1, waiting for transfers between devices: 256 us -> 171 us  [on_device(): lax.psum_scatter(partial_value, 'col', scatter_dimension=0, tiled=True)]
    psum x1, waiting for transfers between devices: 160 us -> 243 us  [on_device(): weight_grad = lax.psum(weight_part, ('row', 'col')) / math.sqrt(nodes_all)]
    scatter-add x10 -> x0, other arithmetic: 45.7 us -> none  [block_step(): return summed.at[targets].add(product)]
    pallas_call x0 -> x2, Pallas kernels: none -> 29.4 us  [slot_pass(): pl.pallas_call(functools.partial(slot_kernel, per_block=per_block, scale=...]
    dot_general x10 -> x0, matrix products: 18.4 us -> none  [the longest x5 9.71 us: block_step(): jnp.einsum('sji,sjf->sif', tile_vals, pieces, preferred_element_type=jnp....]
    mul x2 -> x0, other arithmetic: 11.2 us -> none  [the longest x1 8.09 us: on_device(): partial_value = summed.reshape(row_len, width) * scale]
  transfers between devices with their start and end apart: 5 -> 5, of which waited for: 5 -> 5; matrix products, arithmetic and copies ran while one was open for 12% -> 1% of each run, Pallas kernels for 0% -> 2%
where the time goes in v1:
time: 641 us
  waiting for transfers between devices  586 us (91%)
  Pallas kernels  29.4 us (5%)
  between operations  14.4 us (2%)
    psum x1, waiting for transfers between devices, on_device(): weight_grad = lax.psum(weight_part, ('row', 'col')) / math.sqrt(nodes_all)  243 us
    reduce_scatter x1, waiting for transfers between devices, on_device(): lax.psum_scatter(partial_value, 'col', scatter_dimension=0, tiled=True)  171 us
    all_gather x1, waiting for transfers between devices, on_device(): grad_source = lax.all_gather(grad_agg, 'col', axis=0, tiled=True)  83.3 us
    all_gather x1, waiting for transfers between devices, on_device(): source = lax.all_gather(features, 'row', axis=0, tiled=True)  44.4 us
    reduce_scatter x1, waiting for transfers between devices, on_device(): lax.psum_scatter(back_partial, 'row', scatter_dimension=0, tiled=True)  44.2 us
    pallas_call x2, Pallas kernels, slot_pass(): pl.pallas_call(functools.partial(slot_kernel, per_block=per_block, scale=...  29.4 us
  transfers between devices with their start and end apart: 5, of which 5 were waited for; matrix products, arithmetic and copies ran while one was open for 1% of the time, Pallas kernels for 2%

profile of v1, /device:TPU:8, one launch (start us, length us, event | category | flops | bytes accessed | tf_op | source)
XLA Modules:
  0.0 640.8 jit_solution(7192114248929590869)
XLA Ops:
  7.2 0.0 copy-start
  7.2 0.0 all-gather.3.cloned.1.call-start
  7.2 0.7 all-gather.3.cloned.1.call-update
  7.9 0.0 reduce-scatter.3.cloned.1.call-start
  8.6 44.4 %all-gather.3.cloned.1.call-done = bf16[2048,256]{1,0:T(8,128)(2,1)} async-done(((bf16[256,256]{1,0:T(8,128)(2,1)}), bf16[2048,256]{1,0:T(8,128)(2,1)}) %all-gather.3.cloned.1.call-update) | async-done | bytes 1048592 | tf_op jit(solution)/shard_map/all_gather | solution.py:103
  53.0 0.0 copy-start.1
  53.0 1.2 copy-done.1
  54.2 0.0 copy-start.2
  54.2 0.7 copy-done.2
  54.9 0.7 copy-done.4
  55.6 14.4 %shard_map.94 = f32[64,128,256]{2,1,0:T(8,128)} custom-call(s32[1]{0:T(128)} %bitcast.12.live_ref, s32[176]{0:T(256)S(1)} %bitcast.15, s32[176]{0:T(256)S(1)} %bitcast.17, s32[176,128,128]{2,1,0:T(8,128)} %bitcast.19, bf16[16,128,256]{2,1,0:T(8,128)(2,1)S(1)} %bitcast.14), custom_call_target="tpu_custom_call" | custom-call | tf_op jit(solution)/shard_map/pallas_call | solution.py:66
  70.0 0.0 reduce-scatter.3.cloned.1.call-update
  70.0 0.0 all-gather.5.cloned.1.call-start
  70.0 170.9 %reduce-scatter.3.cloned.1.call-done = f32[256,256]{1,0:T(8,128)} async-done(((f32[8192,256]{1,0:T(8,128)}), f32[256,256]{1,0:T(8,128)}) %reduce-scatter.3.cloned.1.call-update) | async-done | bytes 262160 | tf_op jit(solution)/shard_map/reduce_scatter | solution.py:107
  240.9 0.0 copy-done
  240.9 0.0 copy-done.6
  240.9 1.9 multiply_convert_fusion
  242.8 0.9 convolution_convert_fusion
  243.7 0.0 all-gather.5.cloned.1.call-update
  243.7 0.0 all-reduce.2.cloned.1.call-start
  243.8 1.9 fusion
  245.7 0.0 all-reduce.2.cloned.1.call-update
  245.7 0.0 reduce-scatter.5.cloned.1.call-start
  245.7 83.3 %all-gather.5.cloned.1.call-done = bf16[8192,256]{1,0:T(8,128)(2,1)} async-done(((bf16[256,256]{1,0:T(8,128)(2,1)}), bf16[8192,256]{1,0:T(8,128)(2,1)}) %all-gather.5.cloned.1.call-update) | async-done | bytes 4194320 | tf_op jit(solution)/shard_map/all_gather | solution.py:116
  329.1 0.0 copy-done.3
  329.1 0.0 copy-done.5
  329.1 15.1 %shard_map.95 = f32[16,128,256]{2,1,0:T(8,128)} custom-call(s32[1]{0:T(128)} %bitcast.13.live_ref, s32[176]{0:T(256)S(1)} %bitcast.16, s32[176]{0:T(256)S(1)} %bitcast.18, s32[176,128,128]{2,1,0:T(8,128)} %bitcast.20, bf16[64,128,256]{2,1,0:T(8,128)(2,1)} %bitcast.22), custom_call_target="tpu_custom_call" | custom-call | tf_op jit(solution)/shard_map/pallas_call | solution.py:66
  344.1 0.0 reduce-scatter.5.cloned.1.call-update
  344.2 242.7 %all-reduce.2.cloned.1.call-done = f32[256,256]{1,0:T(8,128)} async-done(((f32[256,256]{1,0:T(8,128)}), f32[256,256]{1,0:T(8,128)}) %all-reduce.2.cloned.1.call-update) | async-done | bytes 262160 | tf_op jit(solution)/shard_map/psum | solution.py:115
  586.9 1.7 broadcast_multiply_fusion
  588.5 44.2 %reduce-scatter.5.cloned.1.call-done = f32[256,256]{1,0:T(8,128)} async-done(((f32[2048,256]{1,0:T(8,128)}), f32[256,256]{1,0:T(8,128)}) %reduce-scatter.5.cloned.1.call-update) | async-done | bytes 262160 | tf_op jit(solution)/shard_map/reduce_scatter | solution.py:120
  632.7 1.6 convert_element_type.23
  (4 shorter events, 0.0 us)
Async XLA Ops:
  7.2 233.8 %copy-start = (bf16[256,256]{1,0:T(8,128)(2,1)S(1)}, bf16[256,256]{1,0:T(8,128)(2,1)}, u32[]{:S(2)}) copy-start(bf16[256,256]{1,0:T(8,128)(2,1)} %param.8) | copy-start | bytes 393220
  7.2 45.8 %all-gather.3.cloned.1.call-start = ((), (), s32[]{:S(2)}) async-start(), calls=%async_computation.2 | async-start | bytes 1179648 | tf_op jit(solution)/shard_map/all_gather | solution.py:103
  7.9 233.0 %reduce-scatter.3.cloned.1.call-start = ((), (), s32[]{:S(2)}) async-start(), calls=%async_computation.3 | async-start | bytes 8650752 | tf_op jit(solution)/shard_map/reduce_scatter | solution.py:107
  53.0 1.2 copy-start.1
  54.2 0.7 copy-start.2
  54.9 0.7 copy-start.4
  70.0 171.0 %copy-start.6 = (bf16[256,256]{1,0:T(8,128)(2,1)S(1)}, bf16[256,256]{1,0:T(8,128)(2,1)}, u32[]{:S(2)}) copy-start(bf16[256,256]{1,0:T(8,128)(2,1)} %param.9) | copy-start | bytes 393220
  70.0 259.1 %copy-start.3 = (s32[1,1,176]{2,1,0:T(1,128)S(1)}, s32[1,1,176]{2,1,0:T(1,128)}, u32[]{:S(2)}) copy-start(s32[1,1,176]{2,1,0:T(1,128)} %param.10) | copy-start | bytes 2116
  70.0 259.1 %copy-start.5 = (s32[1,1,176]{2,1,0:T(1,128)S(1)}, s32[1,1,176]{2,1,0:T(1,128)}, u32[]{:S(2)}) copy-start(s32[1,1,176]{2,1,0:T(1,128)} %param.11) | copy-start | bytes 2116
  70.0 259.1 %all-gather.5.cloned.1.call-start = ((), (), s32[]{:S(2)}) async-start(), calls=%async_computation.5 | async-start | bytes 4325376 | tf_op jit(solution)/shard_map/all_gather | solution.py:116
  243.7 343.1 %all-reduce.2.cloned.1.call-start = ((), (), s32[]{:S(2)}) async-start(), calls=%async_computation.4 | async-start | bytes 524288 | tf_op jit(solution)/shard_map/psum | solution.py:115
  245.7 387.0 %reduce-scatter.5.cloned.1.call-start = ((), (), s32[]{:S(2)}) async-start(), calls=%async_computation.6 | async-start | bytes 2359296 | tf_op jit(solution)/shard_map/reduce_scatter | solution.py:120
Sparse Core Ops, SparseCore 0:
  9.8 43.1 all-gather.2
  70.1 170.7 reduce-scatter.2
  244.3 84.7 all-gather.4
  334.9 251.8 all-reduce.1
  589.2 43.3 reduce-scatter.4

commit v2 on v1

--- a/solution.py
+++ b/solution.py
@@ -6,6 +6,7 @@
 from jax import lax
 from jax.experimental import pallas as pl
 from jax.experimental.pallas import tpu as pltpu
+from jax.sharding import Mesh
 from jax.sharding import PartitionSpec as P
 
 SPARSITY = 128
@@ -83,7 +84,19 @@
     return (hidden, grad_pre)
 
 
-def on_device(features, weight, cotangent, tile_rows, tile_cols, tile_weights, tile_count):
+def butterfly_sum(value, axes, count):
+    for level in reversed(range(count.bit_length() - 1)):
+        pairs = [(i, i ^ (1 << level)) for i in range(count)]
+        value = value + lax.ppermute(value, axes, pairs)
+    return value
+
+
+def on_device(
+    features, weight, cotangent, tile_rows, tile_cols, tile_weights, tile_count, *, sizes
+):
+    row_n, high_n, mid_n, core_n = sizes
+    col_axes = ("high", "mid", "core")
+    col_n = high_n * mid_n * core_n
     node_dev = cotangent.shape[0]
     width = features.shape[1]
     slot_total = tile_weights.shape[2]
@@ -91,31 +104,41 @@
     sparsity_value = SPARSITY
     fan_value = slot_total * tile_len * tile_len // (node_dev * sparsity_value)
     scale = 1.0 / math.sqrt(2.0 * fan_value)
-    row_len = node_dev * lax.axis_size("col")
-    col_len = node_dev * lax.axis_size("row")
+    row_len = node_dev * col_n
+    col_len = node_dev * row_n
     row_tiles = row_len // tile_len
     col_tiles = col_len // tile_len
-    nodes_all = row_len * lax.axis_size("row")
+    nodes_all = row_len * row_n
+    per_chunk = node_dev // tile_len
     row_ids = tile_rows[0, 0]
     col_ids = tile_cols[0, 0]
+    chunk = row_ids // per_chunk
+    high_i = chunk // (mid_n * core_n)
+    mid_i = (chunk // core_n) % mid_n
+    core_i = chunk % core_n
+    placed = (core_i * mid_n * high_n + mid_i * high_n + high_i) * per_chunk + row_ids % per_chunk
     weights_all = tile_weights[0, 0]
     live = tile_count[0, 0].reshape(1)
     source = lax.all_gather(features, "row", axis=0, tiled=True)
     source_tiles = source.reshape(col_tiles, tile_len, width)
-    summed = slot_pass(live, row_ids, col_ids, weights_all, source_tiles, row_tiles, scale, False)
+    summed = slot_pass(live, placed, col_ids, weights_all, source_tiles, row_tiles, scale, False)
     partial_value = summed.reshape(row_len, width)
-    aggregate = lax.psum_scatter(partial_value, "col", scatter_dimension=0, tiled=True).astype(
-        jnp.bfloat16
-    )
+    partial_value = lax.psum_scatter(partial_value, "core", scatter_dimension=0, tiled=True)
+    partial_value = lax.psum_scatter(partial_value, "mid", scatter_dimension=0, tiled=True)
+    partial_value = lax.psum_scatter(partial_value, "high", scatter_dimension=0, tiled=True)
+    aggregate = partial_value.astype(jnp.bfloat16)
     hidden, grad_own = dense_layer(aggregate, weight, cotangent)
     weight_part = lax.dot_general(
         aggregate, grad_own, (((0,), (0,)), ((), ())), preferred_element_type=jnp.float32
     )
     grad_agg = jnp.dot(grad_own, weight.T, preferred_element_type=jnp.float32).astype(jnp.bfloat16)
-    weight_grad = lax.psum(weight_part, ("row", "col")) / math.sqrt(nodes_all)
-    grad_source = lax.all_gather(grad_agg, "col", axis=0, tiled=True)
+    weight_sum = butterfly_sum(weight_part, ("row",) + col_axes, row_n * col_n)
+    weight_grad = weight_sum / math.sqrt(nodes_all)
+    grad_source = lax.all_gather(grad_agg, "high", axis=0, tiled=True)
+    grad_source = lax.all_gather(grad_source, "mid", axis=0, tiled=True)
+    grad_source = lax.all_gather(grad_source, "core", axis=0, tiled=True)
     grad_tiles = grad_source.reshape(row_tiles, tile_len, width)
-    back_summed = slot_pass(live, row_ids, col_ids, weights_all, grad_tiles, col_tiles, scale, True)
+    back_summed = slot_pass(live, placed, col_ids, weights_all, grad_tiles, col_tiles, scale, True)
     back_partial = back_summed.reshape(col_len, width)
     feature_grad = lax.psum_scatter(back_partial, "row", scatter_dimension=0, tiled=True).astype(
         jnp.bfloat16
@@ -124,16 +147,27 @@
 
 
 def solution(mesh):
+    row_n, col_n = mesh.shape["row"], mesh.shape["col"]
+    core_n = 2
+    high_n = 2
+    mid_n = col_n // (high_n * core_n)
+    sizes = (row_n, high_n, mid_n, core_n)
+    fine = Mesh(mesh.devices.reshape(sizes), ("row", "high", "mid", "core"))
+    col = ("high", "mid", "core")
     in_specs = (
-        P(("col", "row"), None),
+        P(col + ("row",), None),
         P(),
-        P(("row", "col"), None),
-        P("row", "col", None),
-        P("row", "col", None),
-        P("row", "col", None, None, None),
-        P("row", "col"),
+        P(("row",) + col, None),
+        P("row", col, None),
+        P("row", col, None),
+        P("row", col, None, None, None),
+        P("row", col),
     )
-    out_specs = (P(("row", "col"), None), P(), P(("col", "row"), None))
+    out_specs = (P(("row",) + col, None), P(), P(col + ("row",), None))
     return jax.shard_map(
-        on_device, mesh=mesh, in_specs=in_specs, out_specs=out_specs, check_vma=False
+        functools.partial(on_device, sizes=sizes),
+        mesh=fine,
+        in_specs=in_specs,
+        out_specs=out_specs,
+        check_vma=False,
     )

time: 641 us -> 394 us (0.61)
  waiting for transfers between devices: 586 us -> 286 us
  starting transfers between devices: 0.2 us -> 39.3 us
  Pallas kernels: 29.4 us -> 36.9 us
  blocking collectives: 0 us -> 7.35 us
    psum x1 -> x0, waiting for transfers between devices: 243 us -> none  [on_device(): weight_grad = lax.psum(weight_part, ('row', 'col')) / math.sqrt(nodes_all)]
    ppermute x0 -> x8, waiting for transfers between devices: none -> 62.5 us  [butterfly_sum(): value = value + lax.ppermute(value, axes, pairs)]
    reduce_scatter x1 -> x3, waiting for transfers between devices: 171 us -> 118 us  [the longest x1 59.1 us: on_device(): lax.psum_scatter(partial_value, 'mid', scatter_dimension=0, tiled=True)]
    reduce_scatter x1, waiting for transfers between devices: 44.2 us -> 0.01 us  [on_device(): lax.psum_scatter(back_partial, 'row', scatter_dimension=0, tiled=True)]
    ppermute x0 -> x8, starting transfers between devices: none -> 39 us  [butterfly_sum(): value = value + lax.ppermute(value, axes, pairs)]
    all_gather x1 -> x2, waiting for transfers between devices: 83.3 us -> 60.5 us  [the longest x1 41.3 us: on_device(): grad_source = lax.all_gather(grad_source, 'mid', axis=0, tiled=True)]
    pallas_call x2, Pallas kernels: 29.4 us -> 36.9 us  [slot_pass(): pl.pallas_call(functools.partial(slot_kernel, per_block=per_block, scale=...]
    all_gather x0 -> x1, blocking collectives: none -> 7.35 us  [on_device(): grad_source = lax.all_gather(grad_agg, 'high', axis=0, tiled=True)]
  transfers between devices with their start and end apart: 5 -> 15, of which waited for: 5 -> 14; matrix products, arithmetic and copies ran while one was open for 1% -> 0% of each run, Pallas kernels for 2% -> 0%
where the time goes in v2:
time: 394 us; the launch traced here: 392 us
  waiting for transfers between devices  286 us (73%)
  starting transfers between devices  39.3 us (10%)
  Pallas kernels  36.9 us (9%)
  between operations  14.9 us (4%)
  blocking collectives  7.35 us (2%)
    ppermute x8, waiting for transfers between devices, butterfly_sum(): value = value + lax.ppermute(value, axes, pairs)  62.5 us
    reduce_scatter x1, waiting for transfers between devices, on_device(): lax.psum_scatter(partial_value, 'mid', scatter_dimension=0, tiled=True)  59.1 us
    all_gather x1, waiting for transfers between devices, on_device(): source = lax.all_gather(features, 'row', axis=0, tiled=True)  43.7 us
    all_gather x1, waiting for transfers between devices, on_device(): grad_source = lax.all_gather(grad_source, 'mid', axis=0, tiled=True)  41.3 us
    ppermute x8, starting transfers between devices, butterfly_sum(): value = value + lax.ppermute(value, axes, pairs)  39 us
    reduce_scatter x1, waiting for transfers between devices, on_device(): lax.psum_scatter(partial_value, 'core', scatter_dimension=0, tiled=True)  37.8 us
    pallas_call x2, Pallas kernels, slot_pass(): pl.pallas_call(functools.partial(slot_kernel, per_block=per_block, scale=...  36.9 us
    reduce_scatter x1, waiting for transfers between devices, on_device(): lax.psum_scatter(partial_value, 'high', scatter_dimension=0, tiled=True)  21.3 us
  transfers between devices with their start and end apart: 15, of which 14 were waited for; matrix products, arithmetic and copies ran while one was open for 0% of the time, Pallas kernels for 0%

profile of v2, /device:TPU:8, one launch (start us, length us, event | category | flops | bytes accessed | tf_op | source)
XLA Modules:
  0.0 391.7 jit_solution(13302259902165766662)
XLA Ops:
  7.2 0.7 all-gather.4.cloned.1.call-update
  8.6 0.7 fusion.8.rows_ref
  9.3 43.7 %all-gather.4.cloned.1.call-done = bf16[2048,256]{1,0:T(8,128)(2,1)} async-done(((bf16[256,256]{1,0:T(8,128)(2,1)}), bf16[2048,256]{1,0:T(8,128)(2,1)}) %all-gather.4.cloned.1.call-update) | async-done | bytes 1048592 | tf_op jit(solution)/shard_map/all_gather | solution.py:122
  53.0 1.2 copy-done.1
  54.2 0.7 copy-done.2
  54.9 17.6 %shard_map.94 = f32[64,128,256]{2,1,0:T(8,128)} custom-call(s32[1]{0:T(128)} %bitcast.12.live_ref, s32[176]{0:T(256)S(1)} %fusion.8.rows_ref, s32[176]{0:T(256)S(1)} %bitcast.15, s32[176,128,128]{2,1,0:T(8,128)} %bitcast.17, bf16[16,128,256]{2,1,0:T(8,128)(2,1)S(1)} %bitcast.14), custom_call_target="tpu_custom_call" | custom-call | tf_op jit(solution)/shard_map/pallas_call | solution.py:67
  72.6 37.8 %reduce-scatter.5.cloned.1.call-done = f32[4096,256]{1,0:T(8,128)} async-done(((f32[8192,256]{1,0:T(8,128)}), f32[4096,256]{1,0:T(8,128)}) %reduce-scatter.5.cloned.1.call-update) | async-done | bytes 4194320 | tf_op jit(solution)/shard_map/reduce_scatter | solution.py:126
  110.5 59.1 %reduce-scatter.7.cloned.1.call-done = f32[512,256]{1,0:T(8,128)} async-done(((f32[4096,256]{1,0:T(8,128)}), f32[512,256]{1,0:T(8,128)}) %reduce-scatter.7.cloned.1.call-update) | async-done | bytes 524304 | tf_op jit(solution)/shard_map/reduce_scatter | solution.py:127
  169.7 21.3 %reduce-scatter.9.cloned.1.call-done = f32[256,256]{1,0:T(8,128)} async-done(((f32[512,256]{1,0:T(8,128)}), f32[256,256]{1,0:T(8,128)}) %reduce-scatter.9.cloned.1.call-update) | async-done | bytes 262160 | tf_op jit(solution)/shard_map/reduce_scatter | solution.py:128
  191.0 1.9 multiply_convert_fusion
  192.9 0.2 convolution_convert_fusion
  193.1 7.3 %all_gather.13 = bf16[512,256]{1,0:T(8,128)(2,1)} all-gather(bf16[256,256]{1,0:T(8,128)(2,1)S(1)} %convolution_convert_fusion), channel_id=1, replica_groups=mesh['row'=8,'high'=2,'mid'=8,'core'=2] {'high'}, dimensions={0}, use_global_device_ids=true | all-gather | bytes 393216 | tf_op jit(solution)/shard_map/all_gather | solution.py:137
  200.5 41.3 %all-gather.6.cloned.1.call-done = bf16[4096,256]{1,0:T(8,128)(2,1)} async-done(((bf16[512,256]{1,0:T(8,128)(2,1)}), bf16[4096,256]{1,0:T(8,128)(2,1)}) %all-gather.6.cloned.1.call-update) | async-done | bytes 2097168 | tf_op jit(solution)/shard_map/all_gather | solution.py:138
  241.9 19.2 %all-gather.8.cloned.1.call-done = bf16[8192,256]{1,0:T(8,128)(2,1)} async-done(((bf16[4096,256]{1,0:T(8,128)(2,1)}), bf16[8192,256]{1,0:T(8,128)(2,1)}) %all-gather.8.cloned.1.call-update) | async-done | bytes 4194320 | tf_op jit(solution)/shard_map/all_gather | solution.py:139
  261.1 19.3 %shard_map.95 = f32[16,128,256]{2,1,0:T(8,128)} custom-call(s32[1]{0:T(128)} %bitcast.13.live_ref, s32[176]{0:T(256)S(1)} %fusion.8.rows_ref, s32[176]{0:T(256)S(1)} %bitcast.16, s32[176,128,128]{2,1,0:T(8,128)} %bitcast.18, bf16[64,128,256]{2,1,0:T(8,128)(2,1)} %bitcast.20), custom_call_target="tpu_custom_call" | custom-call | tf_op jit(solution)/shard_map/pallas_call | solution.py:67
  280.4 0.2 fusion
  280.8 8.4 %collective-permute-done = f32[256,256]{1,0:T(8,128)S(1)} collective-permute-done((f32[256,256]{1,0:T(8,128)S(1)}, f32[256,256]{1,0:T(8,128)S(1)}, u32[]{:S(2)}, u32[]{:S(2)}) %collective-permute-start) | collective-permute-done | bytes 262176 | tf_op jit(solution)/shard_map/ppermute | solution.py:90
  289.2 4.8 %collective-permute-start.1 = (f32[256,256]{1,0:T(8,128)S(1)}, f32[256,256]{1,0:T(8,128)S(1)}, u32[]{:S(2)}, u32[]{:S(2)}) collective-permute-start(f32[256,256]{1,0:T(8,128)S(1)} %add.74), channel_id=1, source_target_pairs={{0,64},{1,65},{2,66},{3,67},{4,68},{5,69},{6,70},{7,71},{8,72},{9,... | collective-permute-start | bytes 786440 | tf_op jit(solution)/shard_map/ppermute | solution.py:90
  294.1 6.6 %collective-permute-done.1 = f32[256,256]{1,0:T(8,128)S(1)} collective-permute-done((f32[256,256]{1,0:T(8,128)S(1)}, f32[256,256]{1,0:T(8,128)S(1)}, u32[]{:S(2)}, u32[]{:S(2)}) %collective-permute-start.1) | collective-permute-done | bytes 262176 | tf_op jit(solution)/shard_map/ppermute | solution.py:90
  300.7 14.1 %collective-permute-start.2 = (f32[256,256]{1,0:T(8,128)S(1)}, f32[256,256]{1,0:T(8,128)S(1)}, u32[]{:S(2)}, u32[]{:S(2)}) collective-permute-start(f32[256,256]{1,0:T(8,128)S(1)} %add.75), channel_id=1, source_target_pairs={{0,32},{1,33},{2,34},{3,35},{4,36},{5,37},{6,38},{7,39},{8,40},{9,... | collective-permute-start | bytes 786440 | tf_op jit(solution)/shard_map/ppermute | solution.py:90
  314.8 9.8 %collective-permute-done.2 = f32[256,256]{1,0:T(8,128)S(1)} collective-permute-done((f32[256,256]{1,0:T(8,128)S(1)}, f32[256,256]{1,0:T(8,128)S(1)}, u32[]{:S(2)}, u32[]{:S(2)}) %collective-permute-start.2) | collective-permute-done | bytes 262176 | tf_op jit(solution)/shard_map/ppermute | solution.py:90
  324.7 3.7 collective-permute-start.3
  328.4 10.8 %collective-permute-done.3 = f32[256,256]{1,0:T(8,128)S(1)} collective-permute-done((f32[256,256]{1,0:T(8,128)S(1)}, f32[256,256]{1,0:T(8,128)S(1)}, u32[]{:S(2)}, u32[]{:S(2)}) %collective-permute-start.3) | collective-permute-done | bytes 262176 | tf_op jit(solution)/shard_map/ppermute | solution.py:90
  339.2 14.6 %collective-permute-start.4 = (f32[256,256]{1,0:T(8,128)S(1)}, f32[256,256]{1,0:T(8,128)S(1)}, u32[]{:S(2)}, u32[]{:S(2)}) collective-permute-start(f32[256,256]{1,0:T(8,128)S(1)} %add.77), channel_id=1, source_target_pairs={{0,8},{1,9},{2,10},{3,11},{4,12},{5,13},{6,14},{7,15},{8,0},{9,1},... | collective-permute-start | bytes 786440 | tf_op jit(solution)/shard_map/ppermute | solution.py:90
  353.8 7.1 %collective-permute-done.4 = f32[256,256]{1,0:T(8,128)S(1)} collective-permute-done((f32[256,256]{1,0:T(8,128)S(1)}, f32[256,256]{1,0:T(8,128)S(1)}, u32[]{:S(2)}, u32[]{:S(2)}) %collective-permute-start.4) | collective-permute-done | bytes 262176 | tf_op jit(solution)/shard_map/ppermute | solution.py:90
  360.9 1.5 collective-permute-start.5
  362.4 11.9 %collective-permute-done.5 = f32[256,256]{1,0:T(8,128)S(1)} collective-permute-done((f32[256,256]{1,0:T(8,128)S(1)}, f32[256,256]{1,0:T(8,128)S(1)}, u32[]{:S(2)}, u32[]{:S(2)}) %collective-permute-start.5) | collective-permute-done | bytes 262176 | tf_op jit(solution)/shard_map/ppermute | solution.py:90
  374.4 0.1 collective-permute-start.6
  374.5 6.4 %collective-permute-done.6 = f32[256,256]{1,0:T(8,128)S(1)} collective-permute-done((f32[256,256]{1,0:T(8,128)S(1)}, f32[256,256]{1,0:T(8,128)S(1)}, u32[]{:S(2)}, u32[]{:S(2)}) %collective-permute-start.6) | collective-permute-done | bytes 262176 | tf_op jit(solution)/shard_map/ppermute | solution.py:90
  381.0 1.5 collective-permute-done.7
  382.5 0.7 add_multiply_fusion
  383.2 1.6 convert_element_type.23
  (33 shorter events, 0.8 us)
Async XLA Ops:
  7.2 183.8 %copy-start = (bf16[256,256]{1,0:T(8,128)(2,1)S(1)}, bf16[256,256]{1,0:T(8,128)(2,1)}, u32[]{:S(2)}) copy-start(bf16[256,256]{1,0:T(8,128)(2,1)} %param.8) | copy-start | bytes 393220
  7.2 45.8 %all-gather.4.cloned.1.call-start = ((), (), s32[]{:S(2)}) async-start(), calls=%async_computation.4 | async-start | bytes 1179648 | tf_op jit(solution)/shard_map/all_gather | solution.py:122
  7.9 102.5 %reduce-scatter.5.cloned.1.call-start = ((), (), s32[]{:S(2)}) async-start(), calls=%async_computation.5 | async-start | bytes 12582912 | tf_op jit(solution)/shard_map/reduce_scatter | solution.py:126
  53.0 1.2 copy-start.1
  54.2 0.7 copy-start.2
  72.5 118.4 %copy-start.5 = (bf16[256,256]{1,0:T(8,128)(2,1)S(1)}, bf16[256,256]{1,0:T(8,128)(2,1)}, u32[]{:S(2)}) copy-start(bf16[256,256]{1,0:T(8,128)(2,1)} %param.9) | copy-start | bytes 393220
  72.5 97.1 %reduce-scatter.7.cloned.1.call-start = ((), (), s32[]{:S(2)}) async-start(), calls=%async_computation.6 | async-start | bytes 4718592 | tf_op jit(solution)/shard_map/reduce_scatter | solution.py:127
  110.4 150.6 %copy-start.3 = (s32[1,1,176]{2,1,0:T(1,128)S(1)}, s32[1,1,176]{2,1,0:T(1,128)}, u32[]{:S(2)}) copy-start(s32[1,1,176]{2,1,0:T(1,128)} %param.11) | copy-start | bytes 2116
  110.4 80.5 %reduce-scatter.9.cloned.1.call-start = ((), (), s32[]{:S(2)}) async-start(), calls=%async_computation.7 | async-start | bytes 786432 | tf_op jit(solution)/shard_map/reduce_scatter | solution.py:128
  169.6 72.2 %all-gather.6.cloned.1.call-start = ((), (), s32[]{:S(2)}) async-start(), calls=%async_computation.8 | async-start | bytes 2359296 | tf_op jit(solution)/shard_map/all_gather | solution.py:138
  200.5 60.6 %all-gather.8.cloned.1.call-start = ((), (), s32[]{:S(2)}) async-start(), calls=%async_computation.9 | async-start | bytes 6291456 | tf_op jit(solution)/shard_map/all_gather | solution.py:139
  241.8 141.4 %reduce-scatter.11.cloned.1.call-start = ((), (), s32[]{:S(2)}) async-start(), calls=%async_computation.10 | async-start | bytes 2359296 | tf_op jit(solution)/shard_map/reduce_scatter | solution.py:143
  261.1 19.4 %copy-start.4 = (f32[256,256]{1,0:T(8,128)S(1)}, f32[256,256]{1,0:T(8,128)}, u32[]{:S(2)}) copy-start(f32[256,256]{1,0:T(8,128)} %reduce-scatter.9.cloned.1.call-done) | copy-start | bytes 786436
  280.7 8.5 %collective-permute-start = (f32[256,256]{1,0:T(8,128)S(1)}, f32[256,256]{1,0:T(8,128)S(1)}, u32[]{:S(2)}, u32[]{:S(2)}) collective-permute-start(f32[256,256]{1,0:T(8,128)S(1)} %fusion), channel_id=1, source_target_pairs={{0,128},{1,129},{2,130},{3,131},{4,132},{5,133},{6,134},{7,135},{8... | collective-permute-start | bytes 786440 | tf_op jit(solution)/shard_map/ppermute | solution.py:90
  289.2 11.4 %collective-permute-start.1 = (f32[256,256]{1,0:T(8,128)S(1)}, f32[256,256]{1,0:T(8,128)S(1)}, u32[]{:S(2)}, u32[]{:S(2)}) collective-permute-start(f32[256,256]{1,0:T(8,128)S(1)} %add.74), channel_id=1, source_target_pairs={{0,64},{1,65},{2,66},{3,67},{4,68},{5,69},{6,70},{7,71},{8,72},{9,... | collective-permute-start | bytes 786440 | tf_op jit(solution)/shard_map/ppermute | solution.py:90
  300.7 24.0 %collective-permute-start.2 = (f32[256,256]{1,0:T(8,128)S(1)}, f32[256,256]{1,0:T(8,128)S(1)}, u32[]{:S(2)}, u32[]{:S(2)}) collective-permute-start(f32[256,256]{1,0:T(8,128)S(1)} %add.75), channel_id=1, source_target_pairs={{0,32},{1,33},{2,34},{3,35},{4,36},{5,37},{6,38},{7,39},{8,40},{9,... | collective-permute-start | bytes 786440 | tf_op jit(solution)/shard_map/ppermute | solution.py:90
  324.7 14.5 %collective-permute-start.3 = (f32[256,256]{1,0:T(8,128)S(1)}, f32[256,256]{1,0:T(8,128)S(1)}, u32[]{:S(2)}, u32[]{:S(2)}) collective-permute-start(f32[256,256]{1,0:T(8,128)S(1)} %add.76), channel_id=1, source_target_pairs={{0,16},{1,17},{2,18},{3,19},{4,20},{5,21},{6,22},{7,23},{8,24},{9,... | collective-permute-start | bytes 786440 | tf_op jit(solution)/shard_map/ppermute | solution.py:90
  339.2 21.7 %collective-permute-start.4 = (f32[256,256]{1,0:T(8,128)S(1)}, f32[256,256]{1,0:T(8,128)S(1)}, u32[]{:S(2)}, u32[]{:S(2)}) collective-permute-start(f32[256,256]{1,0:T(8,128)S(1)} %add.77), channel_id=1, source_target_pairs={{0,8},{1,9},{2,10},{3,11},{4,12},{5,13},{6,14},{7,15},{8,0},{9,1},... | collective-permute-start | bytes 786440 | tf_op jit(solution)/shard_map/ppermute | solution.py:90
  360.9 13.4 %collective-permute-start.5 = (f32[256,256]{1,0:T(8,128)S(1)}, f32[256,256]{1,0:T(8,128)S(1)}, u32[]{:S(2)}, u32[]{:S(2)}) collective-permute-start(f32[256,256]{1,0:T(8,128)S(1)} %add.78), channel_id=1, source_target_pairs={{0,4},{1,5},{2,6},{3,7},{4,0},{5,1},{6,2},{7,3},{8,12},{9,13},{10,... | collective-permute-start | bytes 786440 | tf_op jit(solution)/shard_map/ppermute | solution.py:90
  374.4 6.5 %collective-permute-start.6 = (f32[256,256]{1,0:T(8,128)S(1)}, f32[256,256]{1,0:T(8,128)S(1)}, u32[]{:S(2)}, u32[]{:S(2)}) collective-permute-start(f32[256,256]{1,0:T(8,128)S(1)} %add.79), channel_id=1, source_target_pairs={{0,2},{1,3},{2,0},{3,1},{4,6},{5,7},{6,4},{7,5},{8,10},{9,11},{10,... | collective-permute-start | bytes 786440 | tf_op jit(solution)/shard_map/ppermute | solution.py:90
  380.9 1.6 collective-permute-start.7
Sparse Core Ops, SparseCore 0:
  9.8 43.1 all-gather.3
  72.6 37.7 reduce-scatter.4
  113.0 56.5 reduce-scatter.6
  172.0 18.9 reduce-scatter.8
  200.6 41.1 all-gather.5
  243.5 17.5 all-gather.7
  280.6 66.7 reduce-scatter.10

commit v3 on v2

--- a/solution.py
+++ b/solution.py
@@ -91,6 +91,22 @@
     return value
 
 
+def pair_scatter(value, axis):
+    half = value.shape[0] // 2
+    own = lax.axis_index(axis)
+    keep = lax.dynamic_slice_in_dim(value, own * half, half, 0)
+    send = lax.dynamic_slice_in_dim(value, (1 - own) * half, half, 0)
+    return keep + lax.ppermute(send, axis, [(0, 1), (1, 0)])
+
+
+def pair_gather(value, axis):
+    own = lax.axis_index(axis)
+    other = lax.ppermute(value, axis, [(0, 1), (1, 0)])
+    first = jnp.where(own == 0, value, other)
+    second = jnp.where(own == 0, other, value)
+    return jnp.concatenate([first, second], axis=0)
+
+
 def on_device(
     features, weight, cotangent, tile_rows, tile_cols, tile_weights, tile_count, *, sizes
 ):
@@ -123,9 +139,9 @@
     source_tiles = source.reshape(col_tiles, tile_len, width)
     summed = slot_pass(live, placed, col_ids, weights_all, source_tiles, row_tiles, scale, False)
     partial_value = summed.reshape(row_len, width)
-    partial_value = lax.psum_scatter(partial_value, "core", scatter_dimension=0, tiled=True)
+    partial_value = pair_scatter(partial_value, "core")
     partial_value = lax.psum_scatter(partial_value, "mid", scatter_dimension=0, tiled=True)
-    partial_value = lax.psum_scatter(partial_value, "high", scatter_dimension=0, tiled=True)
+    partial_value = pair_scatter(partial_value, "high")
     aggregate = partial_value.astype(jnp.bfloat16)
     hidden, grad_own = dense_layer(aggregate, weight, cotangent)
     weight_part = lax.dot_general(
@@ -134,9 +150,9 @@
     grad_agg = jnp.dot(grad_own, weight.T, preferred_element_type=jnp.float32).astype(jnp.bfloat16)
     weight_sum = butterfly_sum(weight_part, ("row",) + col_axes, row_n * col_n)
     weight_grad = weight_sum / math.sqrt(nodes_all)
-    grad_source = lax.all_gather(grad_agg, "high", axis=0, tiled=True)
+    grad_source = pair_gather(grad_agg, "high")
     grad_source = lax.all_gather(grad_source, "mid", axis=0, tiled=True)
-    grad_source = lax.all_gather(grad_source, "core", axis=0, tiled=True)
+    grad_source = pair_gather(grad_source, "core")
     grad_tiles = grad_source.reshape(row_tiles, tile_len, width)
     back_summed = slot_pass(live, placed, col_ids, weights_all, grad_tiles, col_tiles, scale, True)
     back_partial = back_summed.reshape(col_len, width)

time: 394 us -> 359 us (0.911)
  waiting for transfers between devices: 286 us -> 239 us
  other arithmetic: 3.3 us -> 15.1 us
  blocking collectives: 7.35 us -> 0 us
  local copies, waits for them, and re-layouts: 1.93 us -> 7.28 us
    reduce_scatter x2 -> x0, waiting for transfers between devices: 59.1 us -> none  [the longest x1 37.8 us: on_device(): lax.psum_scatter(partial_value, 'core', scatter_dimension=0, tiled=True)]
    ppermute x0 -> x4, waiting for transfers between devices: none -> 23.6 us  [the longest x2 14.9 us: pair_scatter(): return keep + lax.ppermute(send, axis, [(0, 1), (1, 0)])]
    all_gather x1 -> x0, waiting for transfers between devices: 19.2 us -> none  [on_device(): grad_source = lax.all_gather(grad_source, 'core', axis=0, tiled=True)]
    reduce_scatter x1, waiting for transfers between devices: 59.1 us -> 69 us  [on_device(): lax.psum_scatter(partial_value, 'mid', scatter_dimension=0, tiled=True)]
    all_gather x1 -> x0, blocking collectives: 7.35 us -> none  [on_device(): grad_source = lax.all_gather(grad_agg, 'high', axis=0, tiled=True)]
    ppermute x8, starting transfers between devices: 39 us -> 33 us  [butterfly_sum(): value = value + lax.ppermute(value, axes, pairs)]
    add x0 -> x1, other arithmetic: none -> 5.94 us  [pair_scatter(): return keep + lax.ppermute(send, axis, [(0, 1), (1, 0)])]
    dynamic_slice x0 -> x2, local copies, waits for them, and re-layouts: none -> 5.36 us  [pair_scatter(): send = lax.dynamic_slice_in_dim(value, (1 - own) * half, half, 0)]
  transfers between devices with their start and end apart: 15 -> 16, of which waited for: 14 -> 15; matrix products, arithmetic and copies ran while one was open for 0% -> 1% of each run, Pallas kernels for 0% -> 0%
where the time goes in v3:
time: 359 us; the launch traced here: 354 us
  waiting for transfers between devices  239 us (67%)
  Pallas kernels  39 us (11%)
  starting transfers between devices  37.5 us (10%)
  other arithmetic  15.1 us (4%)
  between operations  14.6 us (4%)
  local copies, waits for them, and re-layouts  7.28 us (2%)
    reduce_scatter x1, waiting for transfers between devices, on_device(): lax.psum_scatter(partial_value, 'mid', scatter_dimension=0, tiled=True)  69 us
    ppermute x8, waiting for transfers between devices, butterfly_sum(): value = value + lax.ppermute(value, axes, pairs)  62.1 us
    all_gather x1, waiting for transfers between devices, on_device(): source = lax.all_gather(features, 'row', axis=0, tiled=True)  43.7 us
    all_gather x1, waiting for transfers between devices, on_device(): grad_source = lax.all_gather(grad_source, 'mid', axis=0, tiled=True)  39.6 us
    pallas_call x2, Pallas kernels, slot_pass(): pl.pallas_call(functools.partial(slot_kernel, per_block=per_block, scale=...  39 us
    ppermute x8, starting transfers between devices, butterfly_sum(): value = value + lax.ppermute(value, axes, pairs)  33 us
    ppermute x2, waiting for transfers between devices, pair_scatter(): return keep + lax.ppermute(send, axis, [(0, 1), (1, 0)])  14.9 us
    ppermute x2, waiting for transfers between devices, pair_gather(): other = lax.ppermute(value, axis, [(0, 1), (1, 0)])  8.72 us
  transfers between devices with their start and end apart: 16, of which 15 were waited for; matrix products, arithmetic and copies ran while one was open for 1% of the time, Pallas kernels for 0%

profile of v3, /device:TPU:8, one launch (start us, length us, event | category | flops | bytes accessed | tf_op | source)
XLA Modules:
  0.0 353.6 jit_solution(16332704472064967561)
XLA Ops:
  9.3 43.7 %all-gather.3.cloned.1.call-done = bf16[2048,256]{1,0:T(8,128)(2,1)} async-done(((bf16[256,256]{1,0:T(8,128)(2,1)}), bf16[2048,256]{1,0:T(8,128)(2,1)}) %all-gather.3.cloned.1.call-update) | async-done | bytes 1048592 | tf_op jit(solution)/shard_map/all_gather | solution.py:138
  53.0 1.2 copy-done.1
  54.9 18.5 %shard_map.94 = f32[64,128,256]{2,1,0:T(8,128)} custom-call(s32[1]{0:T(128)} %bitcast.14.live_ref, s32[176]{0:T(256)S(1)} %fusion.4.rows_ref, s32[176]{0:T(256)S(1)} %bitcast.17, s32[176,128,128]{2,1,0:T(8,128)} %bitcast.19, bf16[16,128,256]{2,1,0:T(8,128)(2,1)S(1)} %bitcast.16), custom_call_target="tpu_custom_call" | custom-call | tf_op jit(solution)/shard_map/pallas_call | solution.py:67
  73.4 4.4 %constant_dynamic-slice_fusion.1 = f32[4096,256]{1,0:T(8,128)} fusion(f32[8192,256]{1,0:T(8,128)} %bitcast.21, s32[]{:T(128)S(6)} %select_n.69), kind=kLoop, calls=%fused_computation.36 | loop fusion | bytes 8388612 | tf_op jit(solution)/shard_map/dynamic_slice | solution.py:98
  77.8 7.5 %collective-permute-done = f32[4096,256]{1,0:T(8,128)} collective-permute-done((f32[4096,256]{1,0:T(8,128)}, f32[4096,256]{1,0:T(8,128)}, u32[]{:S(2)}, u32[]{:S(2)}) %collective-permute-start) | collective-permute-done | bytes 4194336 | tf_op jit(solution)/shard_map/ppermute | solution.py:99
  85.3 5.9 %dynamic-slice_add_fusion = f32[4096,256]{1,0:T(8,128)} fusion(f32[4096,256]{1,0:T(8,128)} %collective-permute-done, f32[8192,256]{1,0:T(8,128)} %bitcast.22, s32[]{:T(128)S(6)} %select_n.68), kind=kLoop, calls=%fused_computation.1 | loop fusion | flops 1048576 | bytes 12582916 | tf_op jit(solution)/shard_map/add | solution.py:99
  91.3 69.0 %reduce-scatter.3.cloned.1.call-done = f32[512,256]{1,0:T(8,128)} async-done(((f32[4096,256]{1,0:T(8,128)}), f32[512,256]{1,0:T(8,128)}) %reduce-scatter.3.cloned.1.call-update) | async-done | bytes 524304 | tf_op jit(solution)/shard_map/reduce_scatter | solution.py:143
  160.4 1.0 constant_dynamic-slice_fusion
  161.3 2.2 collective-permute-start.1
  163.5 7.4 %collective-permute-done.1 = f32[256,256]{1,0:T(8,128)S(1)} collective-permute-done((f32[256,256]{1,0:T(8,128)S(1)}, f32[256,256]{1,0:T(8,128)S(1)}, u32[]{:S(2)}, u32[]{:S(2)}) %collective-permute-start.1) | collective-permute-done | bytes 262176 | tf_op jit(solution)/shard_map/ppermute | solution.py:99
  170.9 1.0 add_convert_fusion
  171.9 0.9 multiply_convert_fusion
  173.1 2.2 collective-permute-start.10
  175.3 4.4 %collective-permute-done.10 = bf16[256,256]{1,0:T(8,128)(2,1)S(1)} collective-permute-done((bf16[256,256]{1,0:T(8,128)(2,1)S(1)}, bf16[256,256]{1,0:T(8,128)(2,1)S(1)}, u32[]{:S(2)}, u32[]{:S(2)}) %collective-permute-start.10) | collective-permute-done | bytes 131104 | tf_op jit(solution)/shard_map/ppermute | solution.py:104
  180.5 39.6 %all-gather.5.cloned.1.call-done = bf16[4096,256]{1,0:T(8,128)(2,1)} async-done(((bf16[512,256]{1,0:T(8,128)(2,1)}), bf16[4096,256]{1,0:T(8,128)(2,1)}) %all-gather.5.cloned.1.call-update) | async-done | bytes 2097168 | tf_op jit(solution)/shard_map/all_gather | solution.py:154
  220.1 4.4 %collective-permute-done.11 = bf16[4096,256]{1,0:T(8,128)(2,1)S(1)} collective-permute-done((bf16[4096,256]{1,0:T(8,128)(2,1)}, bf16[4096,256]{1,0:T(8,128)(2,1)S(1)}, u32[]{:S(2)}, u32[]{:S(2)}) %collective-permute-start.11) | collective-permute-done | bytes 2097184 | tf_op jit(solution)/shard_map/ppermute | solution.py:104
  224.4 1.9 broadcast_select_fusion.1
  226.3 2.2 pad_maximum_fusion
  228.5 20.5 %shard_map.95 = f32[16,128,256]{2,1,0:T(8,128)} custom-call(s32[1]{0:T(128)} %bitcast.15.live_ref, s32[176]{0:T(256)S(1)} %fusion.4.rows_ref, s32[176]{0:T(256)S(1)} %bitcast.18, s32[176,128,128]{2,1,0:T(8,128)} %bitcast.20, bf16[64,128,256]{2,1,0:T(8,128)(2,1)} %bitcast.23), custom_call_target="tpu_custom_call" | custom-call | tf_op jit(solution)/shard_map/pallas_call | solution.py:67
  249.4 8.3 %collective-permute-done.2 = f32[256,256]{1,0:T(8,128)S(1)} collective-permute-done((f32[256,256]{1,0:T(8,128)S(1)}, f32[256,256]{1,0:T(8,128)S(1)}, u32[]{:S(2)}, u32[]{:S(2)}) %collective-permute-start.2) | collective-permute-done | bytes 262176 | tf_op jit(solution)/shard_map/ppermute | solution.py:90
  257.8 19.5 %collective-permute-start.3 = (f32[256,256]{1,0:T(8,128)S(1)}, f32[256,256]{1,0:T(8,128)S(1)}, u32[]{:S(2)}, u32[]{:S(2)}) collective-permute-start(f32[256,256]{1,0:T(8,128)S(1)} %add.94), channel_id=1, source_target_pairs={{0,64},{1,65},{2,66},{3,67},{4,68},{5,69},{6,70},{7,71},{8,72},{9,... | collective-permute-start | bytes 786440 | tf_op jit(solution)/shard_map/ppermute | solution.py:90
  277.2 6.9 %collective-permute-done.3 = f32[256,256]{1,0:T(8,128)S(1)} collective-permute-done((f32[256,256]{1,0:T(8,128)S(1)}, f32[256,256]{1,0:T(8,128)S(1)}, u32[]{:S(2)}, u32[]{:S(2)}) %collective-permute-start.3) | collective-permute-done | bytes 262176 | tf_op jit(solution)/shard_map/ppermute | solution.py:90
  284.3 10.0 %collective-permute-done.4 = f32[256,256]{1,0:T(8,128)S(1)} collective-permute-done((f32[256,256]{1,0:T(8,128)S(1)}, f32[256,256]{1,0:T(8,128)S(1)}, u32[]{:S(2)}, u32[]{:S(2)}) %collective-permute-start.4) | collective-permute-done | bytes 262176 | tf_op jit(solution)/shard_map/ppermute | solution.py:90
  294.5 13.8 %collective-permute-done.5 = f32[256,256]{1,0:T(8,128)S(1)} collective-permute-done((f32[256,256]{1,0:T(8,128)S(1)}, f32[256,256]{1,0:T(8,128)S(1)}, u32[]{:S(2)}, u32[]{:S(2)}) %collective-permute-start.5) | collective-permute-done | bytes 262176 | tf_op jit(solution)/shard_map/ppermute | solution.py:90
  308.3 6.8 %collective-permute-start.6 = (f32[256,256]{1,0:T(8,128)S(1)}, f32[256,256]{1,0:T(8,128)S(1)}, u32[]{:S(2)}, u32[]{:S(2)}) collective-permute-start(f32[256,256]{1,0:T(8,128)S(1)} %add.97), channel_id=1, source_target_pairs={{0,8},{1,9},{2,10},{3,11},{4,12},{5,13},{6,14},{7,15},{8,0},{9,1},... | collective-permute-start | bytes 786440 | tf_op jit(solution)/shard_map/ppermute | solution.py:90
  315.2 5.0 %collective-permute-done.6 = f32[256,256]{1,0:T(8,128)S(1)} collective-permute-done((f32[256,256]{1,0:T(8,128)S(1)}, f32[256,256]{1,0:T(8,128)S(1)}, u32[]{:S(2)}, u32[]{:S(2)}) %collective-permute-start.6) | collective-permute-done | bytes 262176 | tf_op jit(solution)/shard_map/ppermute | solution.py:90
  320.2 6.2 %collective-permute-start.7 = (f32[256,256]{1,0:T(8,128)S(1)}, f32[256,256]{1,0:T(8,128)S(1)}, u32[]{:S(2)}, u32[]{:S(2)}) collective-permute-start(f32[256,256]{1,0:T(8,128)S(1)} %add.98), channel_id=1, source_target_pairs={{0,4},{1,5},{2,6},{3,7},{4,0},{5,1},{6,2},{7,3},{8,12},{9,13},{10,... | collective-permute-start | bytes 786440 | tf_op jit(solution)/shard_map/ppermute | solution.py:90
  326.4 10.1 %collective-permute-done.7 = f32[256,256]{1,0:T(8,128)S(1)} collective-permute-done((f32[256,256]{1,0:T(8,128)S(1)}, f32[256,256]{1,0:T(8,128)S(1)}, u32[]{:S(2)}, u32[]{:S(2)}) %collective-permute-start.7) | collective-permute-done | bytes 262176 | tf_op jit(solution)/shard_map/ppermute | solution.py:90
  336.7 6.4 %collective-permute-done.8 = f32[256,256]{1,0:T(8,128)S(1)} collective-permute-done((f32[256,256]{1,0:T(8,128)S(1)}, f32[256,256]{1,0:T(8,128)S(1)}, u32[]{:S(2)}, u32[]{:S(2)}) %collective-permute-start.8) | collective-permute-done | bytes 262176 | tf_op jit(solution)/shard_map/ppermute | solution.py:90
  343.1 1.5 collective-permute-done.9
  344.7 0.7 add_multiply_fusion
  345.4 1.6 convert_element_type.23
  (37 shorter events, 4.2 us)
Async XLA Ops:
  7.2 164.7 %copy-start = (bf16[256,256]{1,0:T(8,128)(2,1)S(1)}, bf16[256,256]{1,0:T(8,128)(2,1)}, u32[]{:S(2)}) copy-start(bf16[256,256]{1,0:T(8,128)(2,1)} %param.8) | copy-start | bytes 393220
  7.2 45.8 %all-gather.3.cloned.1.call-start = ((), (), s32[]{:S(2)}) async-start(), calls=%async_computation.2 | async-start | bytes 1179648 | tf_op jit(solution)/shard_map/all_gather | solution.py:138
  7.9 152.4 %reduce-scatter.3.cloned.1.call-start = ((), (), s32[]{:S(2)}) async-start(), calls=%async_computation.3 | async-start | bytes 4718592 | tf_op jit(solution)/shard_map/reduce_scatter | solution.py:143
  53.0 1.2 copy-start.1
  54.2 0.7 copy-start.2
  77.8 7.5 %collective-permute-start = (f32[4096,256]{1,0:T(8,128)}, f32[4096,256]{1,0:T(8,128)}, u32[]{:S(2)}, u32[]{:S(2)}) collective-permute-start(f32[4096,256]{1,0:T(8,128)} %constant_dynamic-slice_fusion.1), channel_id=1, source_target_pairs={{0,1},{1,0},{2,3},{3,2},{4,5},{5,4},{6,7},{7,6},{8,9},{9,8},{10,11... | collective-permute-start | bytes 12582920 | tf_op jit(solution)/shard_map/ppermute | solution.py:99
  91.2 80.7 %copy-start.4 = (bf16[256,256]{1,0:T(8,128)(2,1)S(1)}, bf16[256,256]{1,0:T(8,128)(2,1)}, u32[]{:S(2)}) copy-start(bf16[256,256]{1,0:T(8,128)(2,1)} %param.9) | copy-start | bytes 393220
  91.3 128.8 %all-gather.5.cloned.1.call-start = ((), (), s32[]{:S(2)}) async-start(), calls=%async_computation.4 | async-start | bytes 2359296 | tf_op jit(solution)/shard_map/all_gather | solution.py:154
  161.3 9.6 %collective-permute-start.1 = (f32[256,256]{1,0:T(8,128)S(1)}, f32[256,256]{1,0:T(8,128)S(1)}, u32[]{:S(2)}, u32[]{:S(2)}) collective-permute-start(f32[256,256]{1,0:T(8,128)S(1)} %constant_dynamic-slice_fusion), channel_id=1, source_target_pairs={{0,16},{16,0},{1,17},{17,1},{2,18},{18,2},{3,19},{19,3},{4,20},{20... | collective-permute-start | bytes 786440 | tf_op jit(solution)/shard_map/ppermute | solution.py:99
  173.1 6.6 %collective-permute-start.10 = (bf16[256,256]{1,0:T(8,128)(2,1)S(1)}, bf16[256,256]{1,0:T(8,128)(2,1)S(1)}, u32[]{:S(2)}, u32[]{:S(2)}) collective-permute-start(bf16[256,256]{1,0:T(8,128)(2,1)S(1)} %convolution_convert_fusion), channel_id=1, source_target_pairs={{0,16},{16,0},{1,17},{17,1},{2,18},{18,2},{3,19},{19,3},{4,20},{20... | collective-permute-start | bytes 393224 | tf_op jit(solution)/shard_map/ppermute | solution.py:104
  180.4 165.0 %reduce-scatter.5.cloned.1.call-start = ((), (), s32[]{:S(2)}) async-start(), calls=%async_computation.5 | async-start | bytes 2359296 | tf_op jit(solution)/shard_map/reduce_scatter | solution.py:159
  220.1 4.4 %collective-permute-start.11 = (bf16[4096,256]{1,0:T(8,128)(2,1)}, bf16[4096,256]{1,0:T(8,128)(2,1)S(1)}, u32[]{:S(2)}, u32[]{:S(2)}) collective-permute-start(bf16[4096,256]{1,0:T(8,128)(2,1)} %all-gather.5.cloned.1.call-done), channel_id=1, source_target_pairs={{0,1},{1,0},{2,3},{3,2},{4,5},{5,4},{6,7},{7,6},{8,9},{9,8},{10,11... | collective-permute-start | bytes 6291464 | tf_op jit(solution)/shard_map/ppermute | solution.py:104
  226.3 2.2 copy-start.3
  249.3 8.4 %collective-permute-start.2 = (f32[256,256]{1,0:T(8,128)S(1)}, f32[256,256]{1,0:T(8,128)S(1)}, u32[]{:S(2)}, u32[]{:S(2)}) collective-permute-start(f32[256,256]{1,0:T(8,128)S(1)} %fusion.6), channel_id=1, source_target_pairs={{0,128},{1,129},{2,130},{3,131},{4,132},{5,133},{6,134},{7,135},{8... | collective-permute-start | bytes 786440 | tf_op jit(solution)/shard_map/ppermute | solution.py:90
  257.8 26.4 %collective-permute-start.3 = (f32[256,256]{1,0:T(8,128)S(1)}, f32[256,256]{1,0:T(8,128)S(1)}, u32[]{:S(2)}, u32[]{:S(2)}) collective-permute-start(f32[256,256]{1,0:T(8,128)S(1)} %add.94), channel_id=1, source_target_pairs={{0,64},{1,65},{2,66},{3,67},{4,68},{5,69},{6,70},{7,71},{8,72},{9,... | collective-permute-start | bytes 786440 | tf_op jit(solution)/shard_map/ppermute | solution.py:90
  284.2 10.1 %collective-permute-start.4 = (f32[256,256]{1,0:T(8,128)S(1)}, f32[256,256]{1,0:T(8,128)S(1)}, u32[]{:S(2)}, u32[]{:S(2)}) collective-permute-start(f32[256,256]{1,0:T(8,128)S(1)} %add.95), channel_id=1, source_target_pairs={{0,32},{1,33},{2,34},{3,35},{4,36},{5,37},{6,38},{7,39},{8,40},{9,... | collective-permute-start | bytes 786440 | tf_op jit(solution)/shard_map/ppermute | solution.py:90
  294.4 13.9 %collective-permute-start.5 = (f32[256,256]{1,0:T(8,128)S(1)}, f32[256,256]{1,0:T(8,128)S(1)}, u32[]{:S(2)}, u32[]{:S(2)}) collective-permute-start(f32[256,256]{1,0:T(8,128)S(1)} %add.96), channel_id=1, source_target_pairs={{0,16},{1,17},{2,18},{3,19},{4,20},{5,21},{6,22},{7,23},{8,24},{9,... | collective-permute-start | bytes 786440 | tf_op jit(solution)/shard_map/ppermute | solution.py:90
  308.3 11.9 %collective-permute-start.6 = (f32[256,256]{1,0:T(8,128)S(1)}, f32[256,256]{1,0:T(8,128)S(1)}, u32[]{:S(2)}, u32[]{:S(2)}) collective-permute-start(f32[256,256]{1,0:T(8,128)S(1)} %add.97), channel_id=1, source_target_pairs={{0,8},{1,9},{2,10},{3,11},{4,12},{5,13},{6,14},{7,15},{8,0},{9,1},... | collective-permute-start | bytes 786440 | tf_op jit(solution)/shard_map/ppermute | solution.py:90
  320.2 16.3 %collective-permute-start.7 = (f32[256,256]{1,0:T(8,128)S(1)}, f32[256,256]{1,0:T(8,128)S(1)}, u32[]{:S(2)}, u32[]{:S(2)}) collective-permute-start(f32[256,256]{1,0:T(8,128)S(1)} %add.98), channel_id=1, source_target_pairs={{0,4},{1,5},{2,6},{3,7},{4,0},{5,1},{6,2},{7,3},{8,12},{9,13},{10,... | collective-permute-start | bytes 786440 | tf_op jit(solution)/shard_map/ppermute | solution.py:90
  336.5 6.5 %collective-permute-start.8 = (f32[256,256]{1,0:T(8,128)S(1)}, f32[256,256]{1,0:T(8,128)S(1)}, u32[]{:S(2)}, u32[]{:S(2)}) collective-permute-start(f32[256,256]{1,0:T(8,128)S(1)} %add.99), channel_id=1, source_target_pairs={{0,2},{1,3},{2,0},{3,1},{4,6},{5,7},{6,4},{7,5},{8,10},{9,11},{10,... | collective-permute-start | bytes 786440 | tf_op jit(solution)/shard_map/ppermute | solution.py:90
  343.0 1.6 collective-permute-start.9
Sparse Core Ops, SparseCore 0:
  9.8 43.1 all-gather.2
  91.4 68.9 reduce-scatter.2
  180.5 39.4 all-gather.4
  249.2 64.1 reduce-scatter.4

commit v4 on v3

--- a/solution.py
+++ b/solution.py
@@ -84,10 +84,22 @@
     return (hidden, grad_pre)
 
 
-def butterfly_sum(value, axes, count):
-    for level in reversed(range(count.bit_length() - 1)):
+def butterfly_sum(value, axes, count, levels):
+    for level in levels:
         pairs = [(i, i ^ (1 << level)) for i in range(count)]
         value = value + lax.ppermute(value, axes, pairs)
+    return value
+
+
+def doubling_gather(value, axis, count):
+    own = lax.axis_index(axis)
+    for level in range(count.bit_length() - 1):
+        pairs = [(i, i ^ (1 << level)) for i in range(count)]
+        other = lax.ppermute(value, axis, pairs)
+        low = ((own >> level) & 1) == 0
+        value = jnp.concatenate(
+            [jnp.where(low, value, other), jnp.where(low, other, value)], axis=0
+        )
     return value
 
 
@@ -135,7 +147,7 @@
     placed = (core_i * mid_n * high_n + mid_i * high_n + high_i) * per_chunk + row_ids % per_chunk
     weights_all = tile_weights[0, 0]
     live = tile_count[0, 0].reshape(1)
-    source = lax.all_gather(features, "row", axis=0, tiled=True)
+    source = doubling_gather(features, "row", row_n)
     source_tiles = source.reshape(col_tiles, tile_len, width)
     summed = slot_pass(live, placed, col_ids, weights_all, source_tiles, row_tiles, scale, False)
     partial_value = summed.reshape(row_len, width)
@@ -148,8 +160,9 @@
         aggregate, grad_own, (((0,), (0,)), ((), ())), preferred_element_type=jnp.float32
     )
     grad_agg = jnp.dot(grad_own, weight.T, preferred_element_type=jnp.float32).astype(jnp.bfloat16)
-    weight_sum = butterfly_sum(weight_part, ("row",) + col_axes, row_n * col_n)
-    weight_grad = weight_sum / math.sqrt(nodes_all)
+    every = ("row",) + col_axes
+    levels = list(reversed(range((row_n * col_n).bit_length() - 1)))
+    weight_sum = butterfly_sum(weight_part, every, row_n * col_n, levels)
     grad_source = pair_gather(grad_agg, "high")
     grad_source = lax.all_gather(grad_source, "mid", axis=0, tiled=True)
     grad_source = pair_gather(grad_source, "core")
@@ -159,6 +172,7 @@
     feature_grad = lax.psum_scatter(back_partial, "row", scatter_dimension=0, tiled=True).astype(
         jnp.bfloat16
     )
+    weight_grad = weight_sum / math.sqrt(nodes_all)
     return (hidden, weight_grad, feature_grad)
 
 

time: 359 us -> 341 us (0.950); the launches traced: 354 us -> 342 us
  waiting for transfers between devices: 239 us -> 225 us
    all_gather x1 -> x0, waiting for transfers between devices: 43.7 us -> none  [on_device(): source = lax.all_gather(features, 'row', axis=0, tiled=True)]
    ppermute x0 -> x3, waiting for transfers between devices: none -> 19.1 us  [doubling_gather(): other = lax.ppermute(value, axis, pairs)]
    ppermute x8, waiting for transfers between devices: 62.1 us -> 70.7 us  [butterfly_sum(): value = value + lax.ppermute(value, axes, pairs)]
    ppermute x0 -> x3, starting transfers between devices: none -> 5.84 us  [doubling_gather(): other = lax.ppermute(value, axis, pairs)]
    ppermute x8, starting transfers between devices: 33 us -> 29.3 us  [butterfly_sum(): value = value + lax.ppermute(value, axes, pairs)]
  transfers between devices with their start and end apart: 16 -> 18, of which waited for: 15 -> 17; matrix products, arithmetic and copies ran while one was open for 1% -> 1% of each run, Pallas kernels for 0% -> 0%
where the time goes in v4:
time: 341 us; the launch traced here: 342 us
  waiting for transfers between devices  225 us (66%)
  starting transfers between devices  39.7 us (12%)
  Pallas kernels  39 us (11%)
  other arithmetic  16.7 us (5%)
  between operations  14.6 us (4%)
  local copies, waits for them, and re-layouts  5.39 us (2%)
    reduce_scatter x1, waiting for transfers between devices, on_device(): lax.psum_scatter(partial_value, 'mid', scatter_dimension=0, tiled=True)  71.8 us
    ppermute x8, waiting for transfers between devices, butterfly_sum(): value = value + lax.ppermute(value, axes, pairs)  70.7 us
    all_gather x1, waiting for transfers between devices, on_device(): grad_source = lax.all_gather(grad_source, 'mid', axis=0, tiled=True)  39.6 us
    pallas_call x2, Pallas kernels, slot_pass(): pl.pallas_call(functools.partial(slot_kernel, per_block=per_block, scale=...  39 us
    ppermute x8, starting transfers between devices, butterfly_sum(): value = value + lax.ppermute(value, axes, pairs)  29.3 us
    ppermute x3, waiting for transfers between devices, doubling_gather(): other = lax.ppermute(value, axis, pairs)  19.1 us
    ppermute x2, waiting for transfers between devices, pair_scatter(): return keep + lax.ppermute(send, axis, [(0, 1), (1, 0)])  14.9 us
    ppermute x2, waiting for transfers between devices, pair_gather(): other = lax.ppermute(value, axis, [(0, 1), (1, 0)])  8.73 us
  transfers between devices with their start and end apart: 18, of which 17 were waited for; matrix products, arithmetic and copies ran while one was open for 1% of the time, Pallas kernels for 0%

profile of v4, /device:TPU:8, one launch (start us, length us, event | category | flops | bytes accessed | tf_op | source)
XLA Modules:
  0.0 341.7 jit_solution(17853017819105413783)
XLA Ops:
  7.2 1.6 collective-permute-start
  8.8 4.0 %collective-permute-done = bf16[256,256]{1,0:T(8,128)(2,1)S(1)} collective-permute-done((bf16[256,256]{1,0:T(8,128)(2,1)}, bf16[256,256]{1,0:T(8,128)(2,1)S(1)}, u32[]{:S(2)}, u32[]{:S(2)}) %collective-permute-start) | collective-permute-done | bytes 131104 | tf_op jit(solution)/shard_map/ppermute | solution.py:98
  13.7 3.1 collective-permute-start.1
  16.8 5.7 %collective-permute-done.1 = bf16[512,256]{1,0:T(8,128)(2,1)S(1)} collective-permute-done((bf16[512,256]{1,0:T(8,128)(2,1)S(1)}, bf16[512,256]{1,0:T(8,128)(2,1)S(1)}, u32[]{:S(2)}, u32[]{:S(2)}) %collective-permute-start.1) | collective-permute-done | bytes 262176 | tf_op jit(solution)/shard_map/ppermute | solution.py:98
  22.7 1.2 collective-permute-start.2
  25.2 9.5 %collective-permute-done.2 = bf16[1024,256]{1,0:T(8,128)(2,1)S(1)} collective-permute-done((bf16[1024,256]{1,0:T(8,128)(2,1)S(1)}, bf16[1024,256]{1,0:T(8,128)(2,1)S(1)}, u32[]{:S(2)}, u32[]{:S(2)}) %collective-permute-start.2) | collective-permute-done | bytes 524320 | tf_op jit(solution)/shard_map/ppermute | solution.py:98
  35.0 18.5 %shard_map.94 = f32[64,128,256]{2,1,0:T(8,128)} custom-call(s32[1]{0:T(128)} %bitcast.14.live_ref, s32[176]{0:T(256)S(1)} %fusion.4.rows_ref, s32[176]{0:T(256)S(1)} %bitcast.17, s32[176,128,128]{2,1,0:T(8,128)} %bitcast.19, bf16[16,128,256]{2,1,0:T(8,128)(2,1)S(1)} %bitcast.16), custom_call_target="tpu_custom_call" | custom-call | tf_op jit(solution)/shard_map/pallas_call | solution.py:67
  53.5 4.4 %constant_dynamic-slice_fusion.1 = f32[4096,256]{1,0:T(8,128)} fusion(f32[8192,256]{1,0:T(8,128)} %bitcast.21, s32[]{:T(128)S(6)} %select_n.112), kind=kLoop, calls=%fused_computation.45 | loop fusion | bytes 8388612 | tf_op jit(solution)/shard_map/dynamic_slice | solution.py:110
  57.9 7.5 %collective-permute-done.3 = f32[4096,256]{1,0:T(8,128)} collective-permute-done((f32[4096,256]{1,0:T(8,128)}, f32[4096,256]{1,0:T(8,128)}, u32[]{:S(2)}, u32[]{:S(2)}) %collective-permute-start.3) | collective-permute-done | bytes 4194336 | tf_op jit(solution)/shard_map/ppermute | solution.py:111
  65.4 6.0 %dynamic-slice_add_fusion = f32[4096,256]{1,0:T(8,128)} fusion(f32[4096,256]{1,0:T(8,128)} %collective-permute-done.3, f32[8192,256]{1,0:T(8,128)} %bitcast.22, s32[]{:T(128)S(6)} %select_n.111), kind=kLoop, calls=%fused_computation.1 | loop fusion | flops 1048576 | bytes 12582916 | tf_op jit(solution)/shard_map/add | solution.py:111
  71.4 71.8 %reduce-scatter.3.cloned.1.call-done = f32[512,256]{1,0:T(8,128)} async-done(((f32[4096,256]{1,0:T(8,128)}), f32[512,256]{1,0:T(8,128)}) %reduce-scatter.3.cloned.1.call-update) | async-done | bytes 524304 | tf_op jit(solution)/shard_map/reduce_scatter | solution.py:155
  144.3 2.2 collective-permute-start.4
  146.5 7.4 %collective-permute-done.4 = f32[256,256]{1,0:T(8,128)S(1)} collective-permute-done((f32[256,256]{1,0:T(8,128)S(1)}, f32[256,256]{1,0:T(8,128)S(1)}, u32[]{:S(2)}, u32[]{:S(2)}) %collective-permute-start.4) | collective-permute-done | bytes 262176 | tf_op jit(solution)/shard_map/ppermute | solution.py:111
  153.8 1.0 add_convert_fusion
  156.0 2.2 collective-permute-start.13
  158.2 4.4 %collective-permute-done.13 = bf16[256,256]{1,0:T(8,128)(2,1)S(1)} collective-permute-done((bf16[256,256]{1,0:T(8,128)(2,1)S(1)}, bf16[256,256]{1,0:T(8,128)(2,1)S(1)}, u32[]{:S(2)}, u32[]{:S(2)}) %collective-permute-start.13) | collective-permute-done | bytes 131104 | tf_op jit(solution)/shard_map/ppermute | solution.py:116
  163.4 39.6 %all-gather.2.cloned.1.call-done = bf16[4096,256]{1,0:T(8,128)(2,1)} async-done(((bf16[512,256]{1,0:T(8,128)(2,1)}), bf16[4096,256]{1,0:T(8,128)(2,1)}) %all-gather.2.cloned.1.call-update) | async-done | bytes 2097168 | tf_op jit(solution)/shard_map/all_gather | solution.py:167
  203.0 4.4 %collective-permute-done.14 = bf16[4096,256]{1,0:T(8,128)(2,1)S(1)} collective-permute-done((bf16[4096,256]{1,0:T(8,128)(2,1)}, bf16[4096,256]{1,0:T(8,128)(2,1)S(1)}, u32[]{:S(2)}, u32[]{:S(2)}) %collective-permute-start.14) | collective-permute-done | bytes 2097184 | tf_op jit(solution)/shard_map/ppermute | solution.py:116
  207.3 2.1 broadcast_select_fusion.1
  209.5 2.2 pad_maximum_fusion
  211.7 20.5 %shard_map.95 = f32[16,128,256]{2,1,0:T(8,128)} custom-call(s32[1]{0:T(128)} %bitcast.15.live_ref, s32[176]{0:T(256)S(1)} %fusion.4.rows_ref, s32[176]{0:T(256)S(1)} %bitcast.18, s32[176,128,128]{2,1,0:T(8,128)} %bitcast.20, bf16[64,128,256]{2,1,0:T(8,128)(2,1)} %bitcast.23), custom_call_target="tpu_custom_call" | custom-call | tf_op jit(solution)/shard_map/pallas_call | solution.py:67
  232.6 6.4 %collective-permute-done.5 = f32[256,256]{1,0:T(8,128)S(1)} collective-permute-done((f32[256,256]{1,0:T(8,128)S(1)}, f32[256,256]{1,0:T(8,128)S(1)}, u32[]{:S(2)}, u32[]{:S(2)}) %collective-permute-start.5) | collective-permute-done | bytes 262176 | tf_op jit(solution)/shard_map/ppermute | solution.py:90
  239.0 21.4 %collective-permute-start.6 = (f32[256,256]{1,0:T(8,128)S(1)}, f32[256,256]{1,0:T(8,128)S(1)}, u32[]{:S(2)}, u32[]{:S(2)}) collective-permute-start(f32[256,256]{1,0:T(8,128)S(1)} %add.94), channel_id=1, source_target_pairs={{0,64},{1,65},{2,66},{3,67},{4,68},{5,69},{6,70},{7,71},{8,72},{9,... | collective-permute-start | bytes 786440 | tf_op jit(solution)/shard_map/ppermute | solution.py:90
  260.4 6.7 %collective-permute-done.6 = f32[256,256]{1,0:T(8,128)S(1)} collective-permute-done((f32[256,256]{1,0:T(8,128)S(1)}, f32[256,256]{1,0:T(8,128)S(1)}, u32[]{:S(2)}, u32[]{:S(2)}) %collective-permute-start.6) | collective-permute-done | bytes 262176 | tf_op jit(solution)/shard_map/ppermute | solution.py:90
  267.3 10.5 %collective-permute-done.7 = f32[256,256]{1,0:T(8,128)S(1)} collective-permute-done((f32[256,256]{1,0:T(8,128)S(1)}, f32[256,256]{1,0:T(8,128)S(1)}, u32[]{:S(2)}, u32[]{:S(2)}) %collective-permute-start.7) | collective-permute-done | bytes 262176 | tf_op jit(solution)/shard_map/ppermute | solution.py:90
  277.8 7.3 %collective-permute-start.8 = (f32[256,256]{1,0:T(8,128)S(1)}, f32[256,256]{1,0:T(8,128)S(1)}, u32[]{:S(2)}, u32[]{:S(2)}) collective-permute-start(f32[256,256]{1,0:T(8,128)S(1)} %add.96), channel_id=1, source_target_pairs={{0,16},{1,17},{2,18},{3,19},{4,20},{5,21},{6,22},{7,23},{8,24},{9,... | collective-permute-start | bytes 786440 | tf_op jit(solution)/shard_map/ppermute | solution.py:90
  285.2 13.1 %collective-permute-done.8 = f32[256,256]{1,0:T(8,128)S(1)} collective-permute-done((f32[256,256]{1,0:T(8,128)S(1)}, f32[256,256]{1,0:T(8,128)S(1)}, u32[]{:S(2)}, u32[]{:S(2)}) %collective-permute-start.8) | collective-permute-done | bytes 262176 | tf_op jit(solution)/shard_map/ppermute | solution.py:90
  298.4 14.3 %collective-permute-done.9 = f32[256,256]{1,0:T(8,128)S(1)} collective-permute-done((f32[256,256]{1,0:T(8,128)S(1)}, f32[256,256]{1,0:T(8,128)S(1)}, u32[]{:S(2)}, u32[]{:S(2)}) %collective-permute-start.9) | collective-permute-done | bytes 262176 | tf_op jit(solution)/shard_map/ppermute | solution.py:90
  312.8 10.2 %collective-permute-done.10 = f32[256,256]{1,0:T(8,128)S(1)} collective-permute-done((f32[256,256]{1,0:T(8,128)S(1)}, f32[256,256]{1,0:T(8,128)S(1)}, u32[]{:S(2)}, u32[]{:S(2)}) %collective-permute-start.10) | collective-permute-done | bytes 262176 | tf_op jit(solution)/shard_map/ppermute | solution.py:90
  323.2 8.0 %collective-permute-done.11 = f32[256,256]{1,0:T(8,128)S(1)} collective-permute-done((f32[256,256]{1,0:T(8,128)S(1)}, f32[256,256]{1,0:T(8,128)S(1)}, u32[]{:S(2)}, u32[]{:S(2)}) %collective-permute-start.11) | collective-permute-done | bytes 262176 | tf_op jit(solution)/shard_map/ppermute | solution.py:90
  331.3 1.5 collective-permute-done.12
  333.6 1.6 convert_element_type.23
  (42 shorter events, 6.9 us)
Async XLA Ops:
  7.2 147.7 %copy-start = (bf16[256,256]{1,0:T(8,128)(2,1)S(1)}, bf16[256,256]{1,0:T(8,128)(2,1)}, u32[]{:S(2)}) copy-start(bf16[256,256]{1,0:T(8,128)(2,1)} %param.8) | copy-start | bytes 393220
  7.2 27.8 %copy-start.1 = (s32[1,1,176]{2,1,0:T(1,128)S(1)}, s32[1,1,176]{2,1,0:T(1,128)}, u32[]{:S(2)}) copy-start(s32[1,1,176]{2,1,0:T(1,128)} %param.11) | copy-start | bytes 2116
  7.2 136.1 %reduce-scatter.3.cloned.1.call-start = ((), (), s32[]{:S(2)}) async-start(), calls=%async_computation.2 | async-start | bytes 4718592 | tf_op jit(solution)/shard_map/reduce_scatter | solution.py:155
  7.2 5.5 %collective-permute-start = (bf16[256,256]{1,0:T(8,128)(2,1)}, bf16[256,256]{1,0:T(8,128)(2,1)S(1)}, u32[]{:S(2)}, u32[]{:S(2)}) collective-permute-start(bf16[256,256]{1,0:T(8,128)(2,1)} %param.7), channel_id=1, source_target_pairs={{0,32},{32,0},{64,96},{96,64},{128,160},{160,128},{192,224},{224,1... | collective-permute-start | bytes 393224 | tf_op jit(solution)/shard_map/ppermute | solution.py:98
  13.7 8.8 %collective-permute-start.1 = (bf16[512,256]{1,0:T(8,128)(2,1)S(1)}, bf16[512,256]{1,0:T(8,128)(2,1)S(1)}, u32[]{:S(2)}, u32[]{:S(2)}) collective-permute-start(bf16[512,256]{1,0:T(8,128)(2,1)S(1)} %pad_maximum_fusion.3), channel_id=1, source_target_pairs={{0,64},{32,96},{64,0},{96,32},{128,192},{160,224},{192,128},{224,1... | collective-permute-start | bytes 786440 | tf_op jit(solution)/shard_map/ppermute | solution.py:98
  22.7 12.0 %collective-permute-start.2 = (bf16[1024,256]{1,0:T(8,128)(2,1)S(1)}, bf16[1024,256]{1,0:T(8,128)(2,1)S(1)}, u32[]{:S(2)}, u32[]{:S(2)}) collective-permute-start(bf16[1024,256]{1,0:T(8,128)(2,1)S(1)} %pad_maximum_fusion.2), channel_id=1, source_target_pairs={{0,128},{32,160},{64,192},{96,224},{128,0},{160,32},{192,64},{224,... | collective-permute-start | bytes 1572872 | tf_op jit(solution)/shard_map/ppermute | solution.py:98
  57.9 7.5 %collective-permute-start.3 = (f32[4096,256]{1,0:T(8,128)}, f32[4096,256]{1,0:T(8,128)}, u32[]{:S(2)}, u32[]{:S(2)}) collective-permute-start(f32[4096,256]{1,0:T(8,128)} %constant_dynamic-slice_fusion.1), channel_id=1, source_target_pairs={{0,1},{1,0},{2,3},{3,2},{4,5},{5,4},{6,7},{7,6},{8,9},{9,8},{10,11... | collective-permute-start | bytes 12582920 | tf_op jit(solution)/shard_map/ppermute | solution.py:111
  71.4 83.5 %copy-start.2 = (bf16[256,256]{1,0:T(8,128)(2,1)S(1)}, bf16[256,256]{1,0:T(8,128)(2,1)}, u32[]{:S(2)}) copy-start(bf16[256,256]{1,0:T(8,128)(2,1)} %param.9) | copy-start | bytes 393220
  71.4 131.6 %all-gather.2.cloned.1.call-start = ((), (), s32[]{:S(2)}) async-start(), calls=%async_computation.3 | async-start | bytes 2359296 | tf_op jit(solution)/shard_map/all_gather | solution.py:167
  144.3 9.6 %collective-permute-start.4 = (f32[256,256]{1,0:T(8,128)S(1)}, f32[256,256]{1,0:T(8,128)S(1)}, u32[]{:S(2)}, u32[]{:S(2)}) collective-permute-start(f32[256,256]{1,0:T(8,128)S(1)} %constant_dynamic-slice_fusion), channel_id=1, source_target_pairs={{0,16},{16,0},{1,17},{17,1},{2,18},{18,2},{3,19},{19,3},{4,20},{20... | collective-permute-start | bytes 786440 | tf_op jit(solution)/shard_map/ppermute | solution.py:111
  156.0 6.6 %collective-permute-start.13 = (bf16[256,256]{1,0:T(8,128)(2,1)S(1)}, bf16[256,256]{1,0:T(8,128)(2,1)S(1)}, u32[]{:S(2)}, u32[]{:S(2)}) collective-permute-start(bf16[256,256]{1,0:T(8,128)(2,1)S(1)} %convolution_convert_fusion), channel_id=1, source_target_pairs={{0,16},{16,0},{1,17},{17,1},{2,18},{18,2},{3,19},{19,3},{4,20},{20... | collective-permute-start | bytes 393224 | tf_op jit(solution)/shard_map/ppermute | solution.py:116
  163.3 170.2 %reduce-scatter.5.cloned.1.call-start = ((), (), s32[]{:S(2)}) async-start(), calls=%async_computation.4 | async-start | bytes 2359296 | tf_op jit(solution)/shard_map/reduce_scatter | solution.py:172
  203.0 4.4 %collective-permute-start.14 = (bf16[4096,256]{1,0:T(8,128)(2,1)}, bf16[4096,256]{1,0:T(8,128)(2,1)S(1)}, u32[]{:S(2)}, u32[]{:S(2)}) collective-permute-start(bf16[4096,256]{1,0:T(8,128)(2,1)} %all-gather.2.cloned.1.call-done), channel_id=1, source_target_pairs={{0,1},{1,0},{2,3},{3,2},{4,5},{5,4},{6,7},{7,6},{8,9},{9,8},{10,11... | collective-permute-start | bytes 6291464 | tf_op jit(solution)/shard_map/ppermute | solution.py:116
  232.5 6.5 %collective-permute-start.5 = (f32[256,256]{1,0:T(8,128)S(1)}, f32[256,256]{1,0:T(8,128)S(1)}, u32[]{:S(2)}, u32[]{:S(2)}) collective-permute-start(f32[256,256]{1,0:T(8,128)S(1)} %fusion.6), channel_id=1, source_target_pairs={{0,128},{1,129},{2,130},{3,131},{4,132},{5,133},{6,134},{7,135},{8... | collective-permute-start | bytes 786440 | tf_op jit(solution)/shard_map/ppermute | solution.py:90
  239.0 28.1 %collective-permute-start.6 = (f32[256,256]{1,0:T(8,128)S(1)}, f32[256,256]{1,0:T(8,128)S(1)}, u32[]{:S(2)}, u32[]{:S(2)}) collective-permute-start(f32[256,256]{1,0:T(8,128)S(1)} %add.94), channel_id=1, source_target_pairs={{0,64},{1,65},{2,66},{3,67},{4,68},{5,69},{6,70},{7,71},{8,72},{9,... | collective-permute-start | bytes 786440 | tf_op jit(solution)/shard_map/ppermute | solution.py:90
  267.2 10.6 %collective-permute-start.7 = (f32[256,256]{1,0:T(8,128)S(1)}, f32[256,256]{1,0:T(8,128)S(1)}, u32[]{:S(2)}, u32[]{:S(2)}) collective-permute-start(f32[256,256]{1,0:T(8,128)S(1)} %add.95), channel_id=1, source_target_pairs={{0,32},{1,33},{2,34},{3,35},{4,36},{5,37},{6,38},{7,39},{8,40},{9,... | collective-permute-start | bytes 786440 | tf_op jit(solution)/shard_map/ppermute | solution.py:90
  277.8 20.4 %collective-permute-start.8 = (f32[256,256]{1,0:T(8,128)S(1)}, f32[256,256]{1,0:T(8,128)S(1)}, u32[]{:S(2)}, u32[]{:S(2)}) collective-permute-start(f32[256,256]{1,0:T(8,128)S(1)} %add.96), channel_id=1, source_target_pairs={{0,16},{1,17},{2,18},{3,19},{4,20},{5,21},{6,22},{7,23},{8,24},{9,... | collective-permute-start | bytes 786440 | tf_op jit(solution)/shard_map/ppermute | solution.py:90
  298.3 14.4 %collective-permute-start.9 = (f32[256,256]{1,0:T(8,128)S(1)}, f32[256,256]{1,0:T(8,128)S(1)}, u32[]{:S(2)}, u32[]{:S(2)}) collective-permute-start(f32[256,256]{1,0:T(8,128)S(1)} %add.97), channel_id=1, source_target_pairs={{0,8},{1,9},{2,10},{3,11},{4,12},{5,13},{6,14},{7,15},{8,0},{9,1},... | collective-permute-start | bytes 786440 | tf_op jit(solution)/shard_map/ppermute | solution.py:90
  312.7 10.3 %collective-permute-start.10 = (f32[256,256]{1,0:T(8,128)S(1)}, f32[256,256]{1,0:T(8,128)S(1)}, u32[]{:S(2)}, u32[]{:S(2)}) collective-permute-start(f32[256,256]{1,0:T(8,128)S(1)} %add.98), channel_id=1, source_target_pairs={{0,4},{1,5},{2,6},{3,7},{4,0},{5,1},{6,2},{7,3},{8,12},{9,13},{10,... | collective-permute-start | bytes 786440 | tf_op jit(solution)/shard_map/ppermute | solution.py:90
  323.1 8.1 %collective-permute-start.11 = (f32[256,256]{1,0:T(8,128)S(1)}, f32[256,256]{1,0:T(8,128)S(1)}, u32[]{:S(2)}, u32[]{:S(2)}) collective-permute-start(f32[256,256]{1,0:T(8,128)S(1)} %add.99), channel_id=1, source_target_pairs={{0,2},{1,3},{2,0},{3,1},{4,6},{5,7},{6,4},{7,5},{8,10},{9,11},{10,... | collective-permute-start | bytes 786440 | tf_op jit(solution)/shard_map/ppermute | solution.py:90
  331.2 1.6 collective-permute-start.12
Sparse Core Ops, SparseCore 0:
  71.5 71.7 reduce-scatter.2
  163.5 39.4 all-gather.1
  232.4 63.2 reduce-scatter.4

commit v5 on v4

--- a/solution.py
+++ b/solution.py
@@ -161,7 +161,7 @@
     )
     grad_agg = jnp.dot(grad_own, weight.T, preferred_element_type=jnp.float32).astype(jnp.bfloat16)
     every = ("row",) + col_axes
-    levels = list(reversed(range((row_n * col_n).bit_length() - 1)))
+    levels = list(range((row_n * col_n).bit_length() - 1))
     weight_sum = butterfly_sum(weight_part, every, row_n * col_n, levels)
     grad_source = pair_gather(grad_agg, "high")
     grad_source = lax.all_gather(grad_source, "mid", axis=0, tiled=True)

time: 341 us -> 335 us (0.982)
  waiting for transfers between devices: 225 us -> 216 us
  Pallas kernels: 39 us -> 42.8 us
    ppermute x8, waiting for transfers between devices: 70.7 us -> 62.9 us  [butterfly_sum(): value = value + lax.ppermute(value, axes, pairs)]
    pallas_call x2, Pallas kernels: 39 us -> 42.8 us  [slot_pass(): pl.pallas_call(functools.partial(slot_kernel, per_block=per_block, scale=...]
where the time goes in v5:
time: 335 us; the launch traced here: 334 us
  waiting for transfers between devices  216 us (64%)
  Pallas kernels  42.8 us (13%)
  starting transfers between devices  37.3 us (11%)
  other arithmetic  16.7 us (5%)
  between operations  14.6 us (4%)
  local copies, waits for them, and re-layouts  5.39 us (2%)
    reduce_scatter x1, waiting for transfers between devices, on_device(): lax.psum_scatter(partial_value, 'mid', scatter_dimension=0, tiled=True)  70.7 us
    ppermute x8, waiting for transfers between devices, butterfly_sum(): value = value + lax.ppermute(value, axes, pairs)  62.9 us
    pallas_call x2, Pallas kernels, slot_pass(): pl.pallas_call(functools.partial(slot_kernel, per_block=per_block, scale=...  42.8 us
    all_gather x1, waiting for transfers between devices, on_device(): grad_source = lax.all_gather(grad_source, 'mid', axis=0, tiled=True)  39.6 us
    ppermute x8, starting transfers between devices, butterfly_sum(): value = value + lax.ppermute(value, axes, pairs)  26.9 us
    ppermute x3, waiting for transfers between devices, doubling_gather(): other = lax.ppermute(value, axis, pairs)  19.1 us
    ppermute x2, waiting for transfers between devices, pair_scatter(): return keep + lax.ppermute(send, axis, [(0, 1), (1, 0)])  14.9 us
    ppermute x2, waiting for transfers between devices, pair_gather(): other = lax.ppermute(value, axis, [(0, 1), (1, 0)])  8.71 us
  transfers between devices with their start and end apart: 18, of which 17 were waited for; matrix products, arithmetic and copies ran while one was open for 1% of the time, Pallas kernels for 0%

profile of v5, /device:TPU:8, one launch (start us, length us, event | category | flops | bytes accessed | tf_op | source)
XLA Modules:
  0.0 334.1 jit_solution(14179718262357633027)
XLA Ops:
  7.2 1.6 collective-permute-start
  8.8 4.0 %collective-permute-done = bf16[256,256]{1,0:T(8,128)(2,1)S(1)} collective-permute-done((bf16[256,256]{1,0:T(8,128)(2,1)}, bf16[256,256]{1,0:T(8,128)(2,1)S(1)}, u32[]{:S(2)}, u32[]{:S(2)}) %collective-permute-start) | collective-permute-done | bytes 131104 | tf_op jit(solution)/shard_map/ppermute | solution.py:98
  13.7 3.1 collective-permute-start.1
  16.8 5.7 %collective-permute-done.1 = bf16[512,256]{1,0:T(8,128)(2,1)S(1)} collective-permute-done((bf16[512,256]{1,0:T(8,128)(2,1)S(1)}, bf16[512,256]{1,0:T(8,128)(2,1)S(1)}, u32[]{:S(2)}, u32[]{:S(2)}) %collective-permute-start.1) | collective-permute-done | bytes 262176 | tf_op jit(solution)/shard_map/ppermute | solution.py:98
  25.2 9.5 %collective-permute-done.2 = bf16[1024,256]{1,0:T(8,128)(2,1)S(1)} collective-permute-done((bf16[1024,256]{1,0:T(8,128)(2,1)S(1)}, bf16[1024,256]{1,0:T(8,128)(2,1)S(1)}, u32[]{:S(2)}, u32[]{:S(2)}) %collective-permute-start.2) | collective-permute-done | bytes 524320 | tf_op jit(solution)/shard_map/ppermute | solution.py:98
  35.0 20.1 %shard_map.94 = f32[64,128,256]{2,1,0:T(8,128)} custom-call(s32[1]{0:T(128)} %bitcast.14.live_ref, s32[176]{0:T(256)S(1)} %fusion.4.rows_ref, s32[176]{0:T(256)S(1)} %bitcast.17, s32[176,128,128]{2,1,0:T(8,128)} %bitcast.19, bf16[16,128,256]{2,1,0:T(8,128)(2,1)S(1)} %bitcast.16), custom_call_target="tpu_custom_call" | custom-call | tf_op jit(solution)/shard_map/pallas_call | solution.py:67
  55.1 4.4 %constant_dynamic-slice_fusion.1 = f32[4096,256]{1,0:T(8,128)} fusion(f32[8192,256]{1,0:T(8,128)} %bitcast.21, s32[]{:T(128)S(6)} %select_n.112), kind=kLoop, calls=%fused_computation.45 | loop fusion | bytes 8388612 | tf_op jit(solution)/shard_map/dynamic_slice | solution.py:110
  59.5 7.5 %collective-permute-done.3 = f32[4096,256]{1,0:T(8,128)} collective-permute-done((f32[4096,256]{1,0:T(8,128)}, f32[4096,256]{1,0:T(8,128)}, u32[]{:S(2)}, u32[]{:S(2)}) %collective-permute-start.3) | collective-permute-done | bytes 4194336 | tf_op jit(solution)/shard_map/ppermute | solution.py:111
  67.0 6.0 %dynamic-slice_add_fusion = f32[4096,256]{1,0:T(8,128)} fusion(f32[4096,256]{1,0:T(8,128)} %collective-permute-done.3, f32[8192,256]{1,0:T(8,128)} %bitcast.22, s32[]{:T(128)S(6)} %select_n.111), kind=kLoop, calls=%fused_computation.1 | loop fusion | flops 1048576 | bytes 12582916 | tf_op jit(solution)/shard_map/add | solution.py:111
  73.0 70.7 %reduce-scatter.3.cloned.1.call-done = f32[512,256]{1,0:T(8,128)} async-done(((f32[4096,256]{1,0:T(8,128)}), f32[512,256]{1,0:T(8,128)}) %reduce-scatter.3.cloned.1.call-update) | async-done | bytes 524304 | tf_op jit(solution)/shard_map/reduce_scatter | solution.py:155
  144.7 2.2 collective-permute-start.4
  146.9 7.4 %collective-permute-done.4 = f32[256,256]{1,0:T(8,128)S(1)} collective-permute-done((f32[256,256]{1,0:T(8,128)S(1)}, f32[256,256]{1,0:T(8,128)S(1)}, u32[]{:S(2)}, u32[]{:S(2)}) %collective-permute-start.4) | collective-permute-done | bytes 262176 | tf_op jit(solution)/shard_map/ppermute | solution.py:111
  156.4 2.2 collective-permute-start.13
  158.7 4.3 %collective-permute-done.13 = bf16[256,256]{1,0:T(8,128)(2,1)S(1)} collective-permute-done((bf16[256,256]{1,0:T(8,128)(2,1)S(1)}, bf16[256,256]{1,0:T(8,128)(2,1)S(1)}, u32[]{:S(2)}, u32[]{:S(2)}) %collective-permute-start.13) | collective-permute-done | bytes 131104 | tf_op jit(solution)/shard_map/ppermute | solution.py:116
  163.8 39.6 %all-gather.2.cloned.1.call-done = bf16[4096,256]{1,0:T(8,128)(2,1)} async-done(((bf16[512,256]{1,0:T(8,128)(2,1)}), bf16[4096,256]{1,0:T(8,128)(2,1)}) %all-gather.2.cloned.1.call-update) | async-done | bytes 2097168 | tf_op jit(solution)/shard_map/all_gather | solution.py:167
  203.4 4.4 %collective-permute-done.14 = bf16[4096,256]{1,0:T(8,128)(2,1)S(1)} collective-permute-done((bf16[4096,256]{1,0:T(8,128)(2,1)}, bf16[4096,256]{1,0:T(8,128)(2,1)S(1)}, u32[]{:S(2)}, u32[]{:S(2)}) %collective-permute-start.14) | collective-permute-done | bytes 2097184 | tf_op jit(solution)/shard_map/ppermute | solution.py:116
  207.8 2.1 broadcast_select_fusion.1
  209.9 2.2 pad_maximum_fusion
  212.1 22.7 %shard_map.95 = f32[16,128,256]{2,1,0:T(8,128)} custom-call(s32[1]{0:T(128)} %bitcast.15.live_ref, s32[176]{0:T(256)S(1)} %fusion.4.rows_ref, s32[176]{0:T(256)S(1)} %bitcast.18, s32[176,128,128]{2,1,0:T(8,128)} %bitcast.20, bf16[64,128,256]{2,1,0:T(8,128)(2,1)} %bitcast.23), custom_call_target="tpu_custom_call" | custom-call | tf_op jit(solution)/shard_map/pallas_call | solution.py:67
  235.2 1.5 collective-permute-done.5
  236.7 19.1 %collective-permute-start.6 = (f32[256,256]{1,0:T(8,128)S(1)}, f32[256,256]{1,0:T(8,128)S(1)}, u32[]{:S(2)}, u32[]{:S(2)}) collective-permute-start(f32[256,256]{1,0:T(8,128)S(1)} %add.94), channel_id=1, source_target_pairs={{0,2},{1,3},{2,0},{3,1},{4,6},{5,7},{6,4},{7,5},{8,10},{9,11},{10,... | collective-permute-start | bytes 786440 | tf_op jit(solution)/shard_map/ppermute | solution.py:90
  255.8 6.6 %collective-permute-done.6 = f32[256,256]{1,0:T(8,128)S(1)} collective-permute-done((f32[256,256]{1,0:T(8,128)S(1)}, f32[256,256]{1,0:T(8,128)S(1)}, u32[]{:S(2)}, u32[]{:S(2)}) %collective-permute-start.6) | collective-permute-done | bytes 262176 | tf_op jit(solution)/shard_map/ppermute | solution.py:90
  262.6 14.3 %collective-permute-done.7 = f32[256,256]{1,0:T(8,128)S(1)} collective-permute-done((f32[256,256]{1,0:T(8,128)S(1)}, f32[256,256]{1,0:T(8,128)S(1)}, u32[]{:S(2)}, u32[]{:S(2)}) %collective-permute-start.7) | collective-permute-done | bytes 262176 | tf_op jit(solution)/shard_map/ppermute | solution.py:90
  276.9 2.5 collective-permute-start.8
  279.3 13.6 %collective-permute-done.8 = f32[256,256]{1,0:T(8,128)S(1)} collective-permute-done((f32[256,256]{1,0:T(8,128)S(1)}, f32[256,256]{1,0:T(8,128)S(1)}, u32[]{:S(2)}, u32[]{:S(2)}) %collective-permute-start.8) | collective-permute-done | bytes 262176 | tf_op jit(solution)/shard_map/ppermute | solution.py:90
  292.9 1.8 collective-permute-start.9
  294.7 8.0 %collective-permute-done.9 = f32[256,256]{1,0:T(8,128)S(1)} collective-permute-done((f32[256,256]{1,0:T(8,128)S(1)}, f32[256,256]{1,0:T(8,128)S(1)}, u32[]{:S(2)}, u32[]{:S(2)}) %collective-permute-start.9) | collective-permute-done | bytes 262176 | tf_op jit(solution)/shard_map/ppermute | solution.py:90
  302.9 7.4 %collective-permute-done.10 = f32[256,256]{1,0:T(8,128)S(1)} collective-permute-done((f32[256,256]{1,0:T(8,128)S(1)}, f32[256,256]{1,0:T(8,128)S(1)}, u32[]{:S(2)}, u32[]{:S(2)}) %collective-permute-start.10) | collective-permute-done | bytes 262176 | tf_op jit(solution)/shard_map/ppermute | solution.py:90
  310.3 3.2 collective-permute-start.11
  313.5 5.2 %collective-permute-done.11 = f32[256,256]{1,0:T(8,128)S(1)} collective-permute-done((f32[256,256]{1,0:T(8,128)S(1)}, f32[256,256]{1,0:T(8,128)S(1)}, u32[]{:S(2)}, u32[]{:S(2)}) %collective-permute-start.11) | collective-permute-done | bytes 262176 | tf_op jit(solution)/shard_map/ppermute | solution.py:90
  318.8 6.4 %collective-permute-done.12 = f32[256,256]{1,0:T(8,128)S(1)} collective-permute-done((f32[256,256]{1,0:T(8,128)S(1)}, f32[256,256]{1,0:T(8,128)S(1)}, u32[]{:S(2)}, u32[]{:S(2)}) %collective-permute-start.12) | collective-permute-done | bytes 262176 | tf_op jit(solution)/shard_map/ppermute | solution.py:90
  325.9 1.6 convert_element_type.23
  (42 shorter events, 8.9 us)
Async XLA Ops:
  7.2 148.1 %copy-start = (bf16[256,256]{1,0:T(8,128)(2,1)S(1)}, bf16[256,256]{1,0:T(8,128)(2,1)}, u32[]{:S(2)}) copy-start(bf16[256,256]{1,0:T(8,128)(2,1)} %param.8) | copy-start | bytes 393220
  7.2 27.8 %copy-start.1 = (s32[1,1,176]{2,1,0:T(1,128)S(1)}, s32[1,1,176]{2,1,0:T(1,128)}, u32[]{:S(2)}) copy-start(s32[1,1,176]{2,1,0:T(1,128)} %param.11) | copy-start | bytes 2116
  7.2 136.5 %reduce-scatter.3.cloned.1.call-start = ((), (), s32[]{:S(2)}) async-start(), calls=%async_computation.2 | async-start | bytes 4718592 | tf_op jit(solution)/shard_map/reduce_scatter | solution.py:155
  7.2 5.5 %collective-permute-start = (bf16[256,256]{1,0:T(8,128)(2,1)}, bf16[256,256]{1,0:T(8,128)(2,1)S(1)}, u32[]{:S(2)}, u32[]{:S(2)}) collective-permute-start(bf16[256,256]{1,0:T(8,128)(2,1)} %param.7), channel_id=1, source_target_pairs={{0,32},{32,0},{64,96},{96,64},{128,160},{160,128},{192,224},{224,1... | collective-permute-start | bytes 393224 | tf_op jit(solution)/shard_map/ppermute | solution.py:98
  13.7 8.8 %collective-permute-start.1 = (bf16[512,256]{1,0:T(8,128)(2,1)S(1)}, bf16[512,256]{1,0:T(8,128)(2,1)S(1)}, u32[]{:S(2)}, u32[]{:S(2)}) collective-permute-start(bf16[512,256]{1,0:T(8,128)(2,1)S(1)} %pad_maximum_fusion.3), channel_id=1, source_target_pairs={{0,64},{32,96},{64,0},{96,32},{128,192},{160,224},{192,128},{224,1... | collective-permute-start | bytes 786440 | tf_op jit(solution)/shard_map/ppermute | solution.py:98
  22.7 12.0 %collective-permute-start.2 = (bf16[1024,256]{1,0:T(8,128)(2,1)S(1)}, bf16[1024,256]{1,0:T(8,128)(2,1)S(1)}, u32[]{:S(2)}, u32[]{:S(2)}) collective-permute-start(bf16[1024,256]{1,0:T(8,128)(2,1)S(1)} %pad_maximum_fusion.2), channel_id=1, source_target_pairs={{0,128},{32,160},{64,192},{96,224},{128,0},{160,32},{192,64},{224,... | collective-permute-start | bytes 1572872 | tf_op jit(solution)/shard_map/ppermute | solution.py:98
  59.5 7.5 %collective-permute-start.3 = (f32[4096,256]{1,0:T(8,128)}, f32[4096,256]{1,0:T(8,128)}, u32[]{:S(2)}, u32[]{:S(2)}) collective-permute-start(f32[4096,256]{1,0:T(8,128)} %constant_dynamic-slice_fusion.1), channel_id=1, source_target_pairs={{0,1},{1,0},{2,3},{3,2},{4,5},{5,4},{6,7},{7,6},{8,9},{9,8},{10,11... | collective-permute-start | bytes 12582920 | tf_op jit(solution)/shard_map/ppermute | solution.py:111
  73.0 82.3 %copy-start.2 = (bf16[256,256]{1,0:T(8,128)(2,1)S(1)}, bf16[256,256]{1,0:T(8,128)(2,1)}, u32[]{:S(2)}) copy-start(bf16[256,256]{1,0:T(8,128)(2,1)} %param.9) | copy-start | bytes 393220
  73.0 130.4 %all-gather.2.cloned.1.call-start = ((), (), s32[]{:S(2)}) async-start(), calls=%async_computation.3 | async-start | bytes 2359296 | tf_op jit(solution)/shard_map/all_gather | solution.py:167
  144.7 9.6 %collective-permute-start.4 = (f32[256,256]{1,0:T(8,128)S(1)}, f32[256,256]{1,0:T(8,128)S(1)}, u32[]{:S(2)}, u32[]{:S(2)}) collective-permute-start(f32[256,256]{1,0:T(8,128)S(1)} %constant_dynamic-slice_fusion), channel_id=1, source_target_pairs={{0,16},{16,0},{1,17},{17,1},{2,18},{18,2},{3,19},{19,3},{4,20},{20... | collective-permute-start | bytes 786440 | tf_op jit(solution)/shard_map/ppermute | solution.py:111
  156.4 6.6 %collective-permute-start.13 = (bf16[256,256]{1,0:T(8,128)(2,1)S(1)}, bf16[256,256]{1,0:T(8,128)(2,1)S(1)}, u32[]{:S(2)}, u32[]{:S(2)}) collective-permute-start(bf16[256,256]{1,0:T(8,128)(2,1)S(1)} %convolution_convert_fusion), channel_id=1, source_target_pairs={{0,16},{16,0},{1,17},{17,1},{2,18},{18,2},{3,19},{19,3},{4,20},{20... | collective-permute-start | bytes 393224 | tf_op jit(solution)/shard_map/ppermute | solution.py:116
  163.8 162.2 %reduce-scatter.5.cloned.1.call-start = ((), (), s32[]{:S(2)}) async-start(), calls=%async_computation.4 | async-start | bytes 2359296 | tf_op jit(solution)/shard_map/reduce_scatter | solution.py:172
  203.4 4.4 %collective-permute-start.14 = (bf16[4096,256]{1,0:T(8,128)(2,1)}, bf16[4096,256]{1,0:T(8,128)(2,1)S(1)}, u32[]{:S(2)}, u32[]{:S(2)}) collective-permute-start(bf16[4096,256]{1,0:T(8,128)(2,1)} %all-gather.2.cloned.1.call-done), channel_id=1, source_target_pairs={{0,1},{1,0},{2,3},{3,2},{4,5},{5,4},{6,7},{7,6},{8,9},{9,8},{10,11... | collective-permute-start | bytes 6291464 | tf_op jit(solution)/shard_map/ppermute | solution.py:116
  235.1 1.6 collective-permute-start.5
  236.7 25.7 %collective-permute-start.6 = (f32[256,256]{1,0:T(8,128)S(1)}, f32[256,256]{1,0:T(8,128)S(1)}, u32[]{:S(2)}, u32[]{:S(2)}) collective-permute-start(f32[256,256]{1,0:T(8,128)S(1)} %add.94), channel_id=1, source_target_pairs={{0,2},{1,3},{2,0},{3,1},{4,6},{5,7},{6,4},{7,5},{8,10},{9,11},{10,... | collective-permute-start | bytes 786440 | tf_op jit(solution)/shard_map/ppermute | solution.py:90
  262.5 14.4 %collective-permute-start.7 = (f32[256,256]{1,0:T(8,128)S(1)}, f32[256,256]{1,0:T(8,128)S(1)}, u32[]{:S(2)}, u32[]{:S(2)}) collective-permute-start(f32[256,256]{1,0:T(8,128)S(1)} %add.95), channel_id=1, source_target_pairs={{0,4},{1,5},{2,6},{3,7},{4,0},{5,1},{6,2},{7,3},{8,12},{9,13},{10,... | collective-permute-start | bytes 786440 | tf_op jit(solution)/shard_map/ppermute | solution.py:90
  276.9 16.0 %collective-permute-start.8 = (f32[256,256]{1,0:T(8,128)S(1)}, f32[256,256]{1,0:T(8,128)S(1)}, u32[]{:S(2)}, u32[]{:S(2)}) collective-permute-start(f32[256,256]{1,0:T(8,128)S(1)} %add.96), channel_id=1, source_target_pairs={{0,8},{1,9},{2,10},{3,11},{4,12},{5,13},{6,14},{7,15},{8,0},{9,1},... | collective-permute-start | bytes 786440 | tf_op jit(solution)/shard_map/ppermute | solution.py:90
  292.9 9.8 %collective-permute-start.9 = (f32[256,256]{1,0:T(8,128)S(1)}, f32[256,256]{1,0:T(8,128)S(1)}, u32[]{:S(2)}, u32[]{:S(2)}) collective-permute-start(f32[256,256]{1,0:T(8,128)S(1)} %add.97), channel_id=1, source_target_pairs={{0,16},{1,17},{2,18},{3,19},{4,20},{5,21},{6,22},{7,23},{8,24},{9,... | collective-permute-start | bytes 786440 | tf_op jit(solution)/shard_map/ppermute | solution.py:90
  302.8 7.5 %collective-permute-start.10 = (f32[256,256]{1,0:T(8,128)S(1)}, f32[256,256]{1,0:T(8,128)S(1)}, u32[]{:S(2)}, u32[]{:S(2)}) collective-permute-start(f32[256,256]{1,0:T(8,128)S(1)} %add.98), channel_id=1, source_target_pairs={{0,32},{1,33},{2,34},{3,35},{4,36},{5,37},{6,38},{7,39},{8,40},{9,... | collective-permute-start | bytes 786440 | tf_op jit(solution)/shard_map/ppermute | solution.py:90
  310.3 8.4 %collective-permute-start.11 = (f32[256,256]{1,0:T(8,128)S(1)}, f32[256,256]{1,0:T(8,128)S(1)}, u32[]{:S(2)}, u32[]{:S(2)}) collective-permute-start(f32[256,256]{1,0:T(8,128)S(1)} %add.99), channel_id=1, source_target_pairs={{0,64},{1,65},{2,66},{3,67},{4,68},{5,69},{6,70},{7,71},{8,72},{9,... | collective-permute-start | bytes 786440 | tf_op jit(solution)/shard_map/ppermute | solution.py:90
  318.7 6.5 %collective-permute-start.12 = (f32[256,256]{1,0:T(8,128)S(1)}, f32[256,256]{1,0:T(8,128)S(1)}, u32[]{:S(2)}, u32[]{:S(2)}) collective-permute-start(f32[256,256]{1,0:T(8,128)S(1)} %add.100), channel_id=1, source_target_pairs={{0,128},{1,129},{2,130},{3,131},{4,132},{5,133},{6,134},{7,135},{8... | collective-permute-start | bytes 786440 | tf_op jit(solution)/shard_map/ppermute | solution.py:90
Sparse Core Ops, SparseCore 0:
  73.1 70.5 reduce-scatter.2
  163.9 39.4 all-gather.1
  235.0 60.0 reduce-scatter.4

commit v6 on v5

--- a/solution.py
+++ b/solution.py
@@ -116,6 +116,16 @@
     other = lax.ppermute(value, axis, [(0, 1), (1, 0)])
     first = jnp.where(own == 0, value, other)
     second = jnp.where(own == 0, other, value)
+    return jnp.concatenate([first, second], axis=0)
+
+
+def split_scatter(value, axis, count):
+    chunk = value.shape[0] // count
+    blocks = value.reshape(count, chunk, value.shape[1])
+    first = blocks[:, : chunk // 2].reshape(count * (chunk // 2), value.shape[1])
+    second = blocks[:, chunk // 2 :]
+    first = lax.psum_scatter(first, axis, scatter_dimension=0, tiled=True)
+    second = lax.all_to_all(second, axis, 0, 0, tiled=False).sum(0)
     return jnp.concatenate([first, second], axis=0)
 
 
@@ -152,7 +162,7 @@
     summed = slot_pass(live, placed, col_ids, weights_all, source_tiles, row_tiles, scale, False)
     partial_value = summed.reshape(row_len, width)
     partial_value = pair_scatter(partial_value, "core")
-    partial_value = lax.psum_scatter(partial_value, "mid", scatter_dimension=0, tiled=True)
+    partial_value = split_scatter(partial_value, "mid", mid_n)
     partial_value = pair_scatter(partial_value, "high")
     aggregate = partial_value.astype(jnp.bfloat16)
     hidden, grad_own = dense_layer(aggregate, weight, cotangent)

time: 335 us -> 356 us (1.063)
  Pallas kernels: 42.8 us -> 73.7 us
  starting transfers between devices: 37.3 us -> 31 us
  waiting for transfers between devices: 216 us -> 212 us
    reduce_scatter x1, waiting for transfers between devices: 70.7 us -> 1.47 us  [split_scatter(): first = lax.psum_scatter(first, axis, scatter_dimension=0, tiled=True)]
    all_to_all x0 -> x1, waiting for transfers between devices: none -> 67.9 us  [split_scatter(): second = lax.all_to_all(second, axis, 0, 0, tiled=False).sum(0)]
    pallas_call x2, Pallas kernels: 42.8 us -> 73.7 us  [slot_pass(): pl.pallas_call(functools.partial(slot_kernel, per_block=per_block, scale=...]
    ppermute x8, starting transfers between devices: 26.9 us -> 11.5 us  [butterfly_sum(): value = value + lax.ppermute(value, axes, pairs)]
    all_to_all x0 -> x1, starting transfers between devices: none -> 4.69 us  [split_scatter(): second = lax.all_to_all(second, axis, 0, 0, tiled=False).sum(0)]
    ppermute x2, starting transfers between devices: 2.2 us -> 6.49 us  [pair_scatter(): return keep + lax.ppermute(send, axis, [(0, 1), (1, 0)])]
  transfers between devices with their start and end apart: 18 -> 19, of which waited for: 17 -> 18; matrix products, arithmetic and copies ran while one was open for 1% -> 1% of each run, Pallas kernels for 0% -> 0%
where the time goes in v6:
time: 356 us; the launch traced here: 355 us
  waiting for transfers between devices  212 us (60%)
  Pallas kernels  73.7 us (21%)
  starting transfers between devices  31 us (9%)
  other arithmetic  15 us (4%)
  between operations  14.6 us (4%)
  local copies, waits for them, and re-layouts  6.8 us (2%)
    pallas_call x2, Pallas kernels, slot_pass(): pl.pallas_call(functools.partial(slot_kernel, per_block=per_block, scale=...  73.7 us
    all_to_all x1, waiting for transfers between devices, split_scatter(): second = lax.all_to_all(second, axis, 0, 0, tiled=False).sum(0)  67.9 us
    ppermute x8, waiting for transfers between devices, butterfly_sum(): value = value + lax.ppermute(value, axes, pairs)  61 us
    all_gather x1, waiting for transfers between devices, on_device(): grad_source = lax.all_gather(grad_source, 'mid', axis=0, tiled=True)  40.7 us
    ppermute x3, waiting for transfers between devices, doubling_gather(): other = lax.ppermute(value, axis, pairs)  19.1 us
    ppermute x2, waiting for transfers between devices, pair_scatter(): return keep + lax.ppermute(send, axis, [(0, 1), (1, 0)])  13.5 us
    ppermute x8, starting transfers between devices, butterfly_sum(): value = value + lax.ppermute(value, axes, pairs)  11.5 us
    ppermute x2, waiting for transfers between devices, pair_gather(): other = lax.ppermute(value, axis, [(0, 1), (1, 0)])  8.54 us
  transfers between devices with their start and end apart: 19, of which 18 were waited for; matrix products, arithmetic and copies ran while one was open for 1% of the time, Pallas kernels for 0%

profile of v6, /device:TPU:8, one launch (start us, length us, event | category | flops | bytes accessed | tf_op | source)
XLA Modules:
  0.0 354.8 jit_solution(5176934917027679618)
XLA Ops:
  8.8 4.0 %collective-permute-done = bf16[256,256]{1,0:T(8,128)(2,1)S(1)} collective-permute-done((bf16[256,256]{1,0:T(8,128)(2,1)}, bf16[256,256]{1,0:T(8,128)(2,1)S(1)}, u32[]{:S(2)}, u32[]{:S(2)}) %collective-permute-start) | collective-permute-done | bytes 131104 | tf_op jit(solution)/shard_map/ppermute | solution.py:98
  13.7 3.1 collective-permute-start.1
  16.8 5.7 %collective-permute-done.1 = bf16[512,256]{1,0:T(8,128)(2,1)S(1)} collective-permute-done((bf16[512,256]{1,0:T(8,128)(2,1)S(1)}, bf16[512,256]{1,0:T(8,128)(2,1)S(1)}, u32[]{:S(2)}, u32[]{:S(2)}) %collective-permute-start.1) | collective-permute-done | bytes 262176 | tf_op jit(solution)/shard_map/ppermute | solution.py:98
  25.2 9.5 %collective-permute-done.2 = bf16[1024,256]{1,0:T(8,128)(2,1)S(1)} collective-permute-done((bf16[1024,256]{1,0:T(8,128)(2,1)S(1)}, bf16[1024,256]{1,0:T(8,128)(2,1)S(1)}, u32[]{:S(2)}, u32[]{:S(2)}) %collective-permute-start.2) | collective-permute-done | bytes 524320 | tf_op jit(solution)/shard_map/ppermute | solution.py:98
  35.0 33.3 %shard_map.94 = f32[64,128,256]{2,1,0:T(8,128)} custom-call(s32[1]{0:T(128)} %bitcast.16.live_ref, s32[176]{0:T(256)S(1)} %fusion.8.rows_ref, s32[176]{0:T(256)S(1)} %bitcast.19, s32[176,128,128]{2,1,0:T(8,128)} %bitcast.21, bf16[16,128,256]{2,1,0:T(8,128)(2,1)S(1)} %bitcast.18), custom_call_target="tpu_custom_call" | custom-call | tf_op jit(solution)/shard_map/pallas_call | solution.py:67
  68.4 4.4 %constant_dynamic-slice_fusion = f32[4096,256]{1,0:T(8,128)} fusion(f32[8192,256]{1,0:T(8,128)} %bitcast.23, s32[]{:T(128)S(6)} %select_n.112), kind=kLoop, calls=%fused_computation.45 | loop fusion | bytes 8388612 | tf_op jit(solution)/shard_map/dynamic_slice | solution.py:110
  72.8 7.5 %collective-permute-done.3 = f32[4096,256]{1,0:T(8,128)} collective-permute-done((f32[4096,256]{1,0:T(8,128)}, f32[4096,256]{1,0:T(8,128)}, u32[]{:S(2)}, u32[]{:S(2)}) %collective-permute-start.3) | collective-permute-done | bytes 4194336 | tf_op jit(solution)/shard_map/ppermute | solution.py:111
  80.3 4.0 %dynamic-slice_add_fusion = f32[4096,256]{1,0:T(8,128)S(1)} fusion(f32[4096,256]{1,0:T(8,128)} %collective-permute-done.3, f32[8192,256]{1,0:T(8,128)} %bitcast.24, s32[]{:T(128)S(6)} %select_n.111), kind=kLoop, calls=%fused_computation.1 | loop fusion | flops 1048576 | bytes 12582916 | tf_op jit(solution)/shard_map/add | solution.py:111
  84.3 2.4 fusion.10
  86.7 4.7 %all-to-all-start = ((f32[8,256,256]{2,1,0:T(8,128)}), f32[8,256,256]{2,1,0:T(8,128)S(1)}, u32[]{:S(2)}, u32[]{:S(2)}) async-start(f32[8,256,256]{2,1,0:T(8,128)} %get-tuple-element.5), calls=%async_computation.1 | async-start | bytes 4194304 | tf_op jit(solution)/shard_map/all_to_all | solution.py:128
  91.4 67.9 %all-to-all-done = f32[8,256,256]{2,1,0:T(8,128)S(1)} async-done(((f32[8,256,256]{2,1,0:T(8,128)}), f32[8,256,256]{2,1,0:T(8,128)S(1)}, u32[]{:S(2)}, u32[]{:S(2)}) %all-to-all-start) | async-done | bytes 2097184 | tf_op jit(solution)/shard_map/all_to_all | solution.py:128
  161.0 6.5 %collective-permute-start.4 = (f32[256,256]{1,0:T(8,128)S(1)}, f32[256,256]{1,0:T(8,128)S(1)}, u32[]{:S(2)}, u32[]{:S(2)}) collective-permute-start(f32[256,256]{1,0:T(8,128)S(1)} %fusion), channel_id=1, source_target_pairs={{0,16},{16,0},{1,17},{17,1},{2,18},{18,2},{3,19},{19,3},{4,20},{20... | collective-permute-start | bytes 786440 | tf_op jit(solution)/shard_map/ppermute | solution.py:111
  167.5 6.0 %collective-permute-done.4 = f32[256,256]{1,0:T(8,128)S(1)} collective-permute-done((f32[256,256]{1,0:T(8,128)S(1)}, f32[256,256]{1,0:T(8,128)S(1)}, u32[]{:S(2)}, u32[]{:S(2)}) %collective-permute-start.4) | collective-permute-done | bytes 262176 | tf_op jit(solution)/shard_map/ppermute | solution.py:111
  175.7 2.4 collective-permute-start.13
  178.1 4.2 %collective-permute-done.13 = bf16[256,256]{1,0:T(8,128)(2,1)S(1)} collective-permute-done((bf16[256,256]{1,0:T(8,128)(2,1)S(1)}, bf16[256,256]{1,0:T(8,128)(2,1)S(1)}, u32[]{:S(2)}, u32[]{:S(2)}) %collective-permute-start.13) | collective-permute-done | bytes 131104 | tf_op jit(solution)/shard_map/ppermute | solution.py:116
  183.1 40.7 %all-gather.2.cloned.1.call-done = bf16[4096,256]{1,0:T(8,128)(2,1)} async-done(((bf16[512,256]{1,0:T(8,128)(2,1)}), bf16[4096,256]{1,0:T(8,128)(2,1)}) %all-gather.2.cloned.1.call-update) | async-done | bytes 2097168 | tf_op jit(solution)/shard_map/all_gather | solution.py:177
  223.8 4.4 %collective-permute-done.14 = bf16[4096,256]{1,0:T(8,128)(2,1)S(1)} collective-permute-done((bf16[4096,256]{1,0:T(8,128)(2,1)}, bf16[4096,256]{1,0:T(8,128)(2,1)S(1)}, u32[]{:S(2)}, u32[]{:S(2)}) %collective-permute-start.14) | collective-permute-done | bytes 2097184 | tf_op jit(solution)/shard_map/ppermute | solution.py:116
  228.2 2.1 broadcast_select_fusion.1
  230.3 2.2 pad_maximum_fusion
  232.5 40.4 %shard_map.95 = f32[16,128,256]{2,1,0:T(8,128)} custom-call(s32[1]{0:T(128)} %bitcast.17.live_ref, s32[176]{0:T(256)S(1)} %fusion.8.rows_ref, s32[176]{0:T(256)S(1)} %bitcast.20, s32[176,128,128]{2,1,0:T(8,128)} %bitcast.22, bf16[64,128,256]{2,1,0:T(8,128)(2,1)} %bitcast.26), custom_call_target="tpu_custom_call" | custom-call | tf_op jit(solution)/shard_map/pallas_call | solution.py:67
  274.9 8.3 %collective-permute-done.6 = f32[256,256]{1,0:T(8,128)S(1)} collective-permute-done((f32[256,256]{1,0:T(8,128)S(1)}, f32[256,256]{1,0:T(8,128)S(1)}, u32[]{:S(2)}, u32[]{:S(2)}) %collective-permute-start.6) | collective-permute-done | bytes 262176 | tf_op jit(solution)/shard_map/ppermute | solution.py:90
  284.7 12.8 %collective-permute-done.7 = f32[256,256]{1,0:T(8,128)S(1)} collective-permute-done((f32[256,256]{1,0:T(8,128)S(1)}, f32[256,256]{1,0:T(8,128)S(1)}, u32[]{:S(2)}, u32[]{:S(2)}) %collective-permute-start.7) | collective-permute-done | bytes 262176 | tf_op jit(solution)/shard_map/ppermute | solution.py:90
  297.6 2.1 collective-permute-start.8
  299.7 13.6 %collective-permute-done.8 = f32[256,256]{1,0:T(8,128)S(1)} collective-permute-done((f32[256,256]{1,0:T(8,128)S(1)}, f32[256,256]{1,0:T(8,128)S(1)}, u32[]{:S(2)}, u32[]{:S(2)}) %collective-permute-start.8) | collective-permute-done | bytes 262176 | tf_op jit(solution)/shard_map/ppermute | solution.py:90
  313.4 1.7 collective-permute-start.9
  315.1 7.9 %collective-permute-done.9 = f32[256,256]{1,0:T(8,128)S(1)} collective-permute-done((f32[256,256]{1,0:T(8,128)S(1)}, f32[256,256]{1,0:T(8,128)S(1)}, u32[]{:S(2)}, u32[]{:S(2)}) %collective-permute-start.9) | collective-permute-done | bytes 262176 | tf_op jit(solution)/shard_map/ppermute | solution.py:90
  323.1 2.3 collective-permute-start.10
  325.4 5.6 %collective-permute-done.10 = f32[256,256]{1,0:T(8,128)S(1)} collective-permute-done((f32[256,256]{1,0:T(8,128)S(1)}, f32[256,256]{1,0:T(8,128)S(1)}, u32[]{:S(2)}, u32[]{:S(2)}) %collective-permute-start.10) | collective-permute-done | bytes 262176 | tf_op jit(solution)/shard_map/ppermute | solution.py:90
  331.1 2.9 collective-permute-start.11
  334.0 5.4 %collective-permute-done.11 = f32[256,256]{1,0:T(8,128)S(1)} collective-permute-done((f32[256,256]{1,0:T(8,128)S(1)}, f32[256,256]{1,0:T(8,128)S(1)}, u32[]{:S(2)}, u32[]{:S(2)}) %collective-permute-start.11) | collective-permute-done | bytes 262176 | tf_op jit(solution)/shard_map/ppermute | solution.py:90
  340.2 5.7 %collective-permute-done.12 = f32[256,256]{1,0:T(8,128)S(1)} collective-permute-done((f32[256,256]{1,0:T(8,128)S(1)}, f32[256,256]{1,0:T(8,128)S(1)}, u32[]{:S(2)}, u32[]{:S(2)}) %collective-permute-start.12) | collective-permute-done | bytes 262176 | tf_op jit(solution)/shard_map/ppermute | solution.py:90
  346.7 1.6 convert_element_type.23
  (46 shorter events, 14.7 us)
Async XLA Ops:
  7.2 167.4 %copy-start = (bf16[256,256]{1,0:T(8,128)(2,1)S(1)}, bf16[256,256]{1,0:T(8,128)(2,1)}, u32[]{:S(2)}) copy-start(bf16[256,256]{1,0:T(8,128)(2,1)} %param.8) | copy-start | bytes 393220
  7.2 27.8 %copy-start.1 = (s32[1,1,176]{2,1,0:T(1,128)S(1)}, s32[1,1,176]{2,1,0:T(1,128)}, u32[]{:S(2)}) copy-start(s32[1,1,176]{2,1,0:T(1,128)} %param.11) | copy-start | bytes 2116
  7.2 153.8 %reduce-scatter.3.cloned.1.call-start = ((), (), s32[]{:S(2)}) async-start(), calls=%async_computation.3 | async-start | bytes 2359296 | tf_op jit(solution)/shard_map/reduce_scatter | solution.py:127
  7.2 5.5 %collective-permute-start = (bf16[256,256]{1,0:T(8,128)(2,1)}, bf16[256,256]{1,0:T(8,128)(2,1)S(1)}, u32[]{:S(2)}, u32[]{:S(2)}) collective-permute-start(bf16[256,256]{1,0:T(8,128)(2,1)} %param.7), channel_id=1, source_target_pairs={{0,32},{32,0},{64,96},{96,64},{128,160},{160,128},{192,224},{224,1... | collective-permute-start | bytes 393224 | tf_op jit(solution)/shard_map/ppermute | solution.py:98
  13.7 8.8 %collective-permute-start.1 = (bf16[512,256]{1,0:T(8,128)(2,1)S(1)}, bf16[512,256]{1,0:T(8,128)(2,1)S(1)}, u32[]{:S(2)}, u32[]{:S(2)}) collective-permute-start(bf16[512,256]{1,0:T(8,128)(2,1)S(1)} %pad_maximum_fusion.3), channel_id=1, source_target_pairs={{0,64},{32,96},{64,0},{96,32},{128,192},{160,224},{192,128},{224,1... | collective-permute-start | bytes 786440 | tf_op jit(solution)/shard_map/ppermute | solution.py:98
  22.7 12.0 %collective-permute-start.2 = (bf16[1024,256]{1,0:T(8,128)(2,1)S(1)}, bf16[1024,256]{1,0:T(8,128)(2,1)S(1)}, u32[]{:S(2)}, u32[]{:S(2)}) collective-permute-start(bf16[1024,256]{1,0:T(8,128)(2,1)S(1)} %pad_maximum_fusion.2), channel_id=1, source_target_pairs={{0,128},{32,160},{64,192},{96,224},{128,0},{160,32},{192,64},{224,... | collective-permute-start | bytes 1572872 | tf_op jit(solution)/shard_map/ppermute | solution.py:98
  72.8 7.5 %collective-permute-start.3 = (f32[4096,256]{1,0:T(8,128)}, f32[4096,256]{1,0:T(8,128)}, u32[]{:S(2)}, u32[]{:S(2)}) collective-permute-start(f32[4096,256]{1,0:T(8,128)} %constant_dynamic-slice_fusion), channel_id=1, source_target_pairs={{0,1},{1,0},{2,3},{3,2},{4,5},{5,4},{6,7},{7,6},{8,9},{9,8},{10,11... | collective-permute-start | bytes 12582920 | tf_op jit(solution)/shard_map/ppermute | solution.py:111
  86.7 87.9 %copy-start.2 = (bf16[256,256]{1,0:T(8,128)(2,1)S(1)}, bf16[256,256]{1,0:T(8,128)(2,1)}, u32[]{:S(2)}) copy-start(bf16[256,256]{1,0:T(8,128)(2,1)} %param.9) | copy-start | bytes 393220
  86.7 72.6 %all-to-all-start = ((f32[8,256,256]{2,1,0:T(8,128)}), f32[8,256,256]{2,1,0:T(8,128)S(1)}, u32[]{:S(2)}, u32[]{:S(2)}) async-start(f32[8,256,256]{2,1,0:T(8,128)} %get-tuple-element.5), calls=%async_computation.1 | async-start | bytes 4194304 | tf_op jit(solution)/shard_map/all_to_all | solution.py:128
  91.4 132.4 %all-gather.2.cloned.1.call-start = ((), (), s32[]{:S(2)}) async-start(), calls=%async_computation.4 | async-start | bytes 2359296 | tf_op jit(solution)/shard_map/all_gather | solution.py:177
  161.0 12.5 %collective-permute-start.4 = (f32[256,256]{1,0:T(8,128)S(1)}, f32[256,256]{1,0:T(8,128)S(1)}, u32[]{:S(2)}, u32[]{:S(2)}) collective-permute-start(f32[256,256]{1,0:T(8,128)S(1)} %fusion), channel_id=1, source_target_pairs={{0,16},{16,0},{1,17},{17,1},{2,18},{18,2},{3,19},{19,3},{4,20},{20... | collective-permute-start | bytes 786440 | tf_op jit(solution)/shard_map/ppermute | solution.py:111
  175.7 6.6 %collective-permute-start.13 = (bf16[256,256]{1,0:T(8,128)(2,1)S(1)}, bf16[256,256]{1,0:T(8,128)(2,1)S(1)}, u32[]{:S(2)}, u32[]{:S(2)}) collective-permute-start(bf16[256,256]{1,0:T(8,128)(2,1)S(1)} %convolution_convert_fusion), channel_id=1, source_target_pairs={{0,16},{16,0},{1,17},{17,1},{2,18},{18,2},{3,19},{19,3},{4,20},{20... | collective-permute-start | bytes 393224 | tf_op jit(solution)/shard_map/ppermute | solution.py:116
  183.1 163.6 %reduce-scatter.5.cloned.1.call-start = ((), (), s32[]{:S(2)}) async-start(), calls=%async_computation.5 | async-start | bytes 2359296 | tf_op jit(solution)/shard_map/reduce_scatter | solution.py:182
  223.8 4.4 %collective-permute-start.14 = (bf16[4096,256]{1,0:T(8,128)(2,1)}, bf16[4096,256]{1,0:T(8,128)(2,1)S(1)}, u32[]{:S(2)}, u32[]{:S(2)}) collective-permute-start(bf16[4096,256]{1,0:T(8,128)(2,1)} %all-gather.2.cloned.1.call-done), channel_id=1, source_target_pairs={{0,1},{1,0},{2,3},{3,2},{4,5},{5,4},{6,7},{7,6},{8,9},{9,8},{10,11... | collective-permute-start | bytes 6291464 | tf_op jit(solution)/shard_map/ppermute | solution.py:116
  273.1 1.6 collective-permute-start.5
  274.8 8.4 %collective-permute-start.6 = (f32[256,256]{1,0:T(8,128)S(1)}, f32[256,256]{1,0:T(8,128)S(1)}, u32[]{:S(2)}, u32[]{:S(2)}) collective-permute-start(f32[256,256]{1,0:T(8,128)S(1)} %add.94), channel_id=1, source_target_pairs={{0,2},{1,3},{2,0},{3,1},{4,6},{5,7},{6,4},{7,5},{8,10},{9,11},{10,... | collective-permute-start | bytes 786440 | tf_op jit(solution)/shard_map/ppermute | solution.py:90
  283.3 14.3 %collective-permute-start.7 = (f32[256,256]{1,0:T(8,128)S(1)}, f32[256,256]{1,0:T(8,128)S(1)}, u32[]{:S(2)}, u32[]{:S(2)}) collective-permute-start(f32[256,256]{1,0:T(8,128)S(1)} %add.95), channel_id=1, source_target_pairs={{0,4},{1,5},{2,6},{3,7},{4,0},{5,1},{6,2},{7,3},{8,12},{9,13},{10,... | collective-permute-start | bytes 786440 | tf_op jit(solution)/shard_map/ppermute | solution.py:90
  297.6 15.7 %collective-permute-start.8 = (f32[256,256]{1,0:T(8,128)S(1)}, f32[256,256]{1,0:T(8,128)S(1)}, u32[]{:S(2)}, u32[]{:S(2)}) collective-permute-start(f32[256,256]{1,0:T(8,128)S(1)} %add.96), channel_id=1, source_target_pairs={{0,8},{1,9},{2,10},{3,11},{4,12},{5,13},{6,14},{7,15},{8,0},{9,1},... | collective-permute-start | bytes 786440 | tf_op jit(solution)/shard_map/ppermute | solution.py:90
  313.4 9.7 %collective-permute-start.9 = (f32[256,256]{1,0:T(8,128)S(1)}, f32[256,256]{1,0:T(8,128)S(1)}, u32[]{:S(2)}, u32[]{:S(2)}) collective-permute-start(f32[256,256]{1,0:T(8,128)S(1)} %add.97), channel_id=1, source_target_pairs={{0,16},{1,17},{2,18},{3,19},{4,20},{5,21},{6,22},{7,23},{8,24},{9,... | collective-permute-start | bytes 786440 | tf_op jit(solution)/shard_map/ppermute | solution.py:90
  323.1 8.0 %collective-permute-start.10 = (f32[256,256]{1,0:T(8,128)S(1)}, f32[256,256]{1,0:T(8,128)S(1)}, u32[]{:S(2)}, u32[]{:S(2)}) collective-permute-start(f32[256,256]{1,0:T(8,128)S(1)} %add.98), channel_id=1, source_target_pairs={{0,32},{1,33},{2,34},{3,35},{4,36},{5,37},{6,38},{7,39},{8,40},{9,... | collective-permute-start | bytes 786440 | tf_op jit(solution)/shard_map/ppermute | solution.py:90
  331.1 8.4 %collective-permute-start.11 = (f32[256,256]{1,0:T(8,128)S(1)}, f32[256,256]{1,0:T(8,128)S(1)}, u32[]{:S(2)}, u32[]{:S(2)}) collective-permute-start(f32[256,256]{1,0:T(8,128)S(1)} %add.99), channel_id=1, source_target_pairs={{0,64},{1,65},{2,66},{3,67},{4,68},{5,69},{6,70},{7,71},{8,72},{9,... | collective-permute-start | bytes 786440 | tf_op jit(solution)/shard_map/ppermute | solution.py:90
  339.5 6.5 %collective-permute-start.12 = (f32[256,256]{1,0:T(8,128)S(1)}, f32[256,256]{1,0:T(8,128)S(1)}, u32[]{:S(2)}, u32[]{:S(2)}) collective-permute-start(f32[256,256]{1,0:T(8,128)S(1)} %add.100), channel_id=1, source_target_pairs={{0,128},{1,129},{2,130},{3,131},{4,132},{5,133},{6,134},{7,135},{8... | collective-permute-start | bytes 786440 | tf_op jit(solution)/shard_map/ppermute | solution.py:90
Sparse Core Ops, SparseCore 0:
  86.8 74.0 reduce-scatter.2
  183.2 40.5 all-gather.1
  273.0 42.8 reduce-scatter.4

commit v7 on v5

--- a/solution.py
+++ b/solution.py
@@ -145,13 +145,18 @@
     mid_i = (chunk // core_n) % mid_n
     core_i = chunk % core_n
     placed = (core_i * mid_n * high_n + mid_i * high_n + high_i) * per_chunk + row_ids % per_chunk
+    kept = (core_i == lax.axis_index("core")).astype(jnp.int32)
+    fwd_placed = (kept * mid_n * high_n + mid_i * high_n + high_i) * per_chunk + row_ids % per_chunk
     weights_all = tile_weights[0, 0]
     live = tile_count[0, 0].reshape(1)
     source = doubling_gather(features, "row", row_n)
     source_tiles = source.reshape(col_tiles, tile_len, width)
-    summed = slot_pass(live, placed, col_ids, weights_all, source_tiles, row_tiles, scale, False)
+    summed = slot_pass(live, fwd_placed, col_ids, weights_all, source_tiles, row_tiles, scale, False)
     partial_value = summed.reshape(row_len, width)
-    partial_value = pair_scatter(partial_value, "core")
+    half = row_len // 2
+    partial_value = partial_value[half:] + lax.ppermute(
+        partial_value[:half], "core", [(0, 1), (1, 0)]
+    )
     partial_value = lax.psum_scatter(partial_value, "mid", scatter_dimension=0, tiled=True)
     partial_value = pair_scatter(partial_value, "high")
     aggregate = partial_value.astype(jnp.bfloat16)

time: 335 us -> 331 us (0.988)
  Pallas kernels: 42.8 us -> 34.3 us
  waiting for transfers between devices: 216 us -> 224 us
    pallas_call x2, Pallas kernels: 42.8 us -> 34.3 us  [slot_pass(): pl.pallas_call(functools.partial(slot_kernel, per_block=per_block, scale=...]
    ppermute x2 -> x1, waiting for transfers between devices: 14.9 us -> 7.37 us  [pair_scatter(): return keep + lax.ppermute(send, axis, [(0, 1), (1, 0)])]
    ppermute x0 -> x1, waiting for transfers between devices: none -> 7.15 us  [on_device(): lax.ppermute(partial_value[:half], 'core', [(0, 1), (1, 0)])]
    ppermute x8, waiting for transfers between devices: 62.9 us -> 68 us  [butterfly_sum(): value = value + lax.ppermute(value, axes, pairs)]
    dynamic_slice x2 -> x1, local copies, waits for them, and re-layouts: 5.37 us -> 0.97 us  [pair_scatter(): send = lax.dynamic_slice_in_dim(value, (1 - own) * half, half, 0)]
    slice x0 -> x1, local copies, waits for them, and re-layouts: none -> 4.01 us  [on_device(): partial_value[half:]]
    reduce_scatter x1, waiting for transfers between devices: 70.7 us -> 74.6 us  [on_device(): lax.psum_scatter(partial_value, 'mid', scatter_dimension=0, tiled=True)]
where the time goes in v7:
time: 331 us
  waiting for transfers between devices  224 us (68%)
  starting transfers between devices  37.6 us (11%)
  Pallas kernels  34.3 us (10%)
  between operations  14.6 us (4%)
  other arithmetic  14.4 us (4%)
  local copies, waits for them, and re-layouts  4.99 us (2%)
    reduce_scatter x1, waiting for transfers between devices, on_device(): lax.psum_scatter(partial_value, 'mid', scatter_dimension=0, tiled=True)  74.6 us
    ppermute x8, waiting for transfers between devices, butterfly_sum(): value = value + lax.ppermute(value, axes, pairs)  68 us
    all_gather x1, waiting for transfers between devices, on_device(): grad_source = lax.all_gather(grad_source, 'mid', axis=0, tiled=True)  39.6 us
    pallas_call x2, Pallas kernels, slot_pass(): pl.pallas_call(functools.partial(slot_kernel, per_block=per_block, scale=...  34.3 us
    ppermute x8, starting transfers between devices, butterfly_sum(): value = value + lax.ppermute(value, axes, pairs)  27.1 us
    ppermute x3, waiting for transfers between devices, doubling_gather(): other = lax.ppermute(value, axis, pairs)  18.4 us
    ppermute x2, waiting for transfers between devices, pair_gather(): other = lax.ppermute(value, axis, [(0, 1), (1, 0)])  8.73 us
    ppermute x1, waiting for transfers between devices, pair_scatter(): return keep + lax.ppermute(send, axis, [(0, 1), (1, 0)])  7.37 us
  transfers between devices with their start and end apart: 18, of which 17 were waited for; matrix products, arithmetic and copies ran while one was open for 1% of the time, Pallas kernels for 0%

profile of v7, /device:TPU:8, one launch (start us, length us, event | category | flops | bytes accessed | tf_op | source)
XLA Modules:
  0.0 331.1 jit_solution(1663078282236649973)
XLA Ops:
  7.2 1.6 collective-permute-start
  8.8 4.0 %collective-permute-done = bf16[256,256]{1,0:T(8,128)(2,1)S(1)} collective-permute-done((bf16[256,256]{1,0:T(8,128)(2,1)}, bf16[256,256]{1,0:T(8,128)(2,1)S(1)}, u32[]{:S(2)}, u32[]{:S(2)}) %collective-permute-start) | collective-permute-done | bytes 131104 | tf_op jit(solution)/shard_map/ppermute | solution.py:98
  13.7 3.1 collective-permute-start.1
  16.8 5.7 %collective-permute-done.1 = bf16[512,256]{1,0:T(8,128)(2,1)S(1)} collective-permute-done((bf16[512,256]{1,0:T(8,128)(2,1)S(1)}, bf16[512,256]{1,0:T(8,128)(2,1)S(1)}, u32[]{:S(2)}, u32[]{:S(2)}) %collective-permute-start.1) | collective-permute-done | bytes 262176 | tf_op jit(solution)/shard_map/ppermute | solution.py:98
  22.7 1.2 collective-permute-start.2
  25.9 8.8 %collective-permute-done.2 = bf16[1024,256]{1,0:T(8,128)(2,1)S(1)} collective-permute-done((bf16[1024,256]{1,0:T(8,128)(2,1)S(1)}, bf16[1024,256]{1,0:T(8,128)(2,1)S(1)}, u32[]{:S(2)}, u32[]{:S(2)}) %collective-permute-start.2) | collective-permute-done | bytes 524320 | tf_op jit(solution)/shard_map/ppermute | solution.py:98
  35.0 16.5 %shard_map.94 = f32[64,128,256]{2,1,0:T(8,128)} custom-call(s32[1]{0:T(128)} %bitcast.16.live_ref, s32[176]{0:T(256)S(1)} %multiply_add_fusion.1.rows_ref, s32[176]{0:T(256)S(1)} %bitcast.19, s32[176,128,128]{2,1,0:T(8,128)} %bitcast.21, bf16[16,128,256]{2,1,0:T(8,128)(2,1)S(1)} %bitcast.18), custom_call_target="tpu_custom_call" | custom-call | tf_op jit(solution)/shard_map/pallas_call | solution.py:67
  51.5 4.0 %fusion.6 = (f32[32,128,256]{2,1,0:T(8,128)S(1)}, f32[32,128,256]{2,1,0:T(8,128)S(1)}) fusion(f32[64,128,256]{2,1,0:T(8,128)} %shard_map.94), kind=kLoop, calls=%fused_computation.52 | loop fusion | bytes 16777216 | tf_op jit(solution)/shard_map/slice | solution.py:157
  55.6 7.1 %collective-permute-done.3 = f32[4096,256]{1,0:T(8,128)S(1)} collective-permute-done((f32[4096,256]{1,0:T(8,128)S(1)}, f32[4096,256]{1,0:T(8,128)S(1)}, u32[]{:S(2)}, u32[]{:S(2)}) %collective-permute-start.3) | collective-permute-done | bytes 4194336 | tf_op jit(solution)/shard_map/ppermute | solution.py:157
  62.7 2.9 bitcast_add_fusion
  65.8 74.6 %reduce-scatter.3.cloned.1.call-done = f32[512,256]{1,0:T(8,128)} async-done(((f32[4096,256]{1,0:T(8,128)}), f32[512,256]{1,0:T(8,128)}) %reduce-scatter.3.cloned.1.call-update) | async-done | bytes 524304 | tf_op jit(solution)/shard_map/reduce_scatter | solution.py:160
  141.3 2.2 collective-permute-start.4
  143.5 7.4 %collective-permute-done.4 = f32[256,256]{1,0:T(8,128)S(1)} collective-permute-done((f32[256,256]{1,0:T(8,128)S(1)}, f32[256,256]{1,0:T(8,128)S(1)}, u32[]{:S(2)}, u32[]{:S(2)}) %collective-permute-start.4) | collective-permute-done | bytes 262176 | tf_op jit(solution)/shard_map/ppermute | solution.py:111
  150.9 1.0 add_convert_fusion
  153.1 2.2 collective-permute-start.13
  155.3 4.4 %collective-permute-done.13 = bf16[256,256]{1,0:T(8,128)(2,1)S(1)} collective-permute-done((bf16[256,256]{1,0:T(8,128)(2,1)S(1)}, bf16[256,256]{1,0:T(8,128)(2,1)S(1)}, u32[]{:S(2)}, u32[]{:S(2)}) %collective-permute-start.13) | collective-permute-done | bytes 131104 | tf_op jit(solution)/shard_map/ppermute | solution.py:116
  160.4 39.6 %all-gather.2.cloned.1.call-done = bf16[4096,256]{1,0:T(8,128)(2,1)} async-done(((bf16[512,256]{1,0:T(8,128)(2,1)}), bf16[4096,256]{1,0:T(8,128)(2,1)}) %all-gather.2.cloned.1.call-update) | async-done | bytes 2097168 | tf_op jit(solution)/shard_map/all_gather | solution.py:172
  200.0 4.4 %collective-permute-done.14 = bf16[4096,256]{1,0:T(8,128)(2,1)S(1)} collective-permute-done((bf16[4096,256]{1,0:T(8,128)(2,1)}, bf16[4096,256]{1,0:T(8,128)(2,1)S(1)}, u32[]{:S(2)}, u32[]{:S(2)}) %collective-permute-start.14) | collective-permute-done | bytes 2097184 | tf_op jit(solution)/shard_map/ppermute | solution.py:116
  204.4 2.1 broadcast_select_fusion.1
  206.5 2.2 pad_maximum_fusion
  208.8 17.8 %shard_map.95 = f32[16,128,256]{2,1,0:T(8,128)} custom-call(s32[1]{0:T(128)} %bitcast.17.live_ref, s32[176]{0:T(256)S(1)} %get-tuple-element.3.rows_ref, s32[176]{0:T(256)S(1)} %bitcast.20, s32[176,128,128]{2,1,0:T(8,128)} %bitcast.22, bf16[64,128,256]{2,1,0:T(8,128)(2,1)} %bitcast.23), custom_call_target="tpu_custom_call" | custom-call | tf_op jit(solution)/shard_map/pallas_call | solution.py:67
  226.9 1.5 collective-permute-done.5
  228.5 23.9 %collective-permute-start.6 = (f32[256,256]{1,0:T(8,128)S(1)}, f32[256,256]{1,0:T(8,128)S(1)}, u32[]{:S(2)}, u32[]{:S(2)}) collective-permute-start(f32[256,256]{1,0:T(8,128)S(1)} %add.97), channel_id=1, source_target_pairs={{0,2},{1,3},{2,0},{3,1},{4,6},{5,7},{6,4},{7,5},{8,10},{9,11},{10,... | collective-permute-start | bytes 786440 | tf_op jit(solution)/shard_map/ppermute | solution.py:90
  252.5 6.6 %collective-permute-done.6 = f32[256,256]{1,0:T(8,128)S(1)} collective-permute-done((f32[256,256]{1,0:T(8,128)S(1)}, f32[256,256]{1,0:T(8,128)S(1)}, u32[]{:S(2)}, u32[]{:S(2)}) %collective-permute-start.6) | collective-permute-done | bytes 262176 | tf_op jit(solution)/shard_map/ppermute | solution.py:90
  259.2 14.3 %collective-permute-done.7 = f32[256,256]{1,0:T(8,128)S(1)} collective-permute-done((f32[256,256]{1,0:T(8,128)S(1)}, f32[256,256]{1,0:T(8,128)S(1)}, u32[]{:S(2)}, u32[]{:S(2)}) %collective-permute-start.7) | collective-permute-done | bytes 262176 | tf_op jit(solution)/shard_map/ppermute | solution.py:90
  273.5 2.4 collective-permute-start.8
  275.9 14.4 %collective-permute-done.8 = f32[256,256]{1,0:T(8,128)S(1)} collective-permute-done((f32[256,256]{1,0:T(8,128)S(1)}, f32[256,256]{1,0:T(8,128)S(1)}, u32[]{:S(2)}, u32[]{:S(2)}) %collective-permute-start.8) | collective-permute-done | bytes 262176 | tf_op jit(solution)/shard_map/ppermute | solution.py:90
  290.4 9.7 %collective-permute-done.9 = f32[256,256]{1,0:T(8,128)S(1)} collective-permute-done((f32[256,256]{1,0:T(8,128)S(1)}, f32[256,256]{1,0:T(8,128)S(1)}, u32[]{:S(2)}, u32[]{:S(2)}) %collective-permute-start.9) | collective-permute-done | bytes 262176 | tf_op jit(solution)/shard_map/ppermute | solution.py:90
  300.2 7.5 %collective-permute-done.10 = f32[256,256]{1,0:T(8,128)S(1)} collective-permute-done((f32[256,256]{1,0:T(8,128)S(1)}, f32[256,256]{1,0:T(8,128)S(1)}, u32[]{:S(2)}, u32[]{:S(2)}) %collective-permute-start.10) | collective-permute-done | bytes 262176 | tf_op jit(solution)/shard_map/ppermute | solution.py:90
  307.9 7.9 %collective-permute-done.11 = f32[256,256]{1,0:T(8,128)S(1)} collective-permute-done((f32[256,256]{1,0:T(8,128)S(1)}, f32[256,256]{1,0:T(8,128)S(1)}, u32[]{:S(2)}, u32[]{:S(2)}) %collective-permute-start.11) | collective-permute-done | bytes 262176 | tf_op jit(solution)/shard_map/ppermute | solution.py:90
  316.1 6.1 %collective-permute-done.12 = f32[256,256]{1,0:T(8,128)S(1)} collective-permute-done((f32[256,256]{1,0:T(8,128)S(1)}, f32[256,256]{1,0:T(8,128)S(1)}, u32[]{:S(2)}, u32[]{:S(2)}) %collective-permute-start.12) | collective-permute-done | bytes 262176 | tf_op jit(solution)/shard_map/ppermute | solution.py:90
  323.0 1.6 convert_element_type.24
  (43 shorter events, 8.0 us)
Async XLA Ops:
  7.2 144.7 %copy-start = (bf16[256,256]{1,0:T(8,128)(2,1)S(1)}, bf16[256,256]{1,0:T(8,128)(2,1)}, u32[]{:S(2)}) copy-start(bf16[256,256]{1,0:T(8,128)(2,1)} %param.8) | copy-start | bytes 393220
  7.2 27.8 %copy-start.1 = (s32[1,1,176]{2,1,0:T(1,128)S(1)}, s32[1,1,176]{2,1,0:T(1,128)}, u32[]{:S(2)}) copy-start(s32[1,1,176]{2,1,0:T(1,128)} %param.11) | copy-start | bytes 2116
  7.2 133.2 %reduce-scatter.3.cloned.1.call-start = ((), (), s32[]{:S(2)}) async-start(), calls=%async_computation.2 | async-start | bytes 4718592 | tf_op jit(solution)/shard_map/reduce_scatter | solution.py:160
  7.2 5.5 %collective-permute-start = (bf16[256,256]{1,0:T(8,128)(2,1)}, bf16[256,256]{1,0:T(8,128)(2,1)S(1)}, u32[]{:S(2)}, u32[]{:S(2)}) collective-permute-start(bf16[256,256]{1,0:T(8,128)(2,1)} %param.7), channel_id=1, source_target_pairs={{0,32},{32,0},{64,96},{96,64},{128,160},{160,128},{192,224},{224,1... | collective-permute-start | bytes 393224 | tf_op jit(solution)/shard_map/ppermute | solution.py:98
  13.7 8.8 %collective-permute-start.1 = (bf16[512,256]{1,0:T(8,128)(2,1)S(1)}, bf16[512,256]{1,0:T(8,128)(2,1)S(1)}, u32[]{:S(2)}, u32[]{:S(2)}) collective-permute-start(bf16[512,256]{1,0:T(8,128)(2,1)S(1)} %pad_maximum_fusion.3), channel_id=1, source_target_pairs={{0,64},{32,96},{64,0},{96,32},{128,192},{160,224},{192,128},{224,1... | collective-permute-start | bytes 786440 | tf_op jit(solution)/shard_map/ppermute | solution.py:98
  22.7 12.0 %collective-permute-start.2 = (bf16[1024,256]{1,0:T(8,128)(2,1)S(1)}, bf16[1024,256]{1,0:T(8,128)(2,1)S(1)}, u32[]{:S(2)}, u32[]{:S(2)}) collective-permute-start(bf16[1024,256]{1,0:T(8,128)(2,1)S(1)} %pad_maximum_fusion.2), channel_id=1, source_target_pairs={{0,128},{32,160},{64,192},{96,224},{128,0},{160,32},{192,64},{224,... | collective-permute-start | bytes 1572872 | tf_op jit(solution)/shard_map/ppermute | solution.py:98
  55.5 7.2 %collective-permute-start.3 = (f32[4096,256]{1,0:T(8,128)S(1)}, f32[4096,256]{1,0:T(8,128)S(1)}, u32[]{:S(2)}, u32[]{:S(2)}) collective-permute-start(f32[4096,256]{1,0:T(8,128)S(1)} %bitcast.24), channel_id=1, source_target_pairs={{0,1},{1,0},{2,3},{3,2},{4,5},{5,4},{6,7},{7,6},{8,9},{9,8},{10,11... | collective-permute-start | bytes 12582920 | tf_op jit(solution)/shard_map/ppermute | solution.py:157
  65.7 86.2 %copy-start.2 = (bf16[256,256]{1,0:T(8,128)(2,1)S(1)}, bf16[256,256]{1,0:T(8,128)(2,1)}, u32[]{:S(2)}) copy-start(bf16[256,256]{1,0:T(8,128)(2,1)} %param.9) | copy-start | bytes 393220
  65.7 134.3 %all-gather.2.cloned.1.call-start = ((), (), s32[]{:S(2)}) async-start(), calls=%async_computation.3 | async-start | bytes 2359296 | tf_op jit(solution)/shard_map/all_gather | solution.py:172
  141.3 9.6 %collective-permute-start.4 = (f32[256,256]{1,0:T(8,128)S(1)}, f32[256,256]{1,0:T(8,128)S(1)}, u32[]{:S(2)}, u32[]{:S(2)}) collective-permute-start(f32[256,256]{1,0:T(8,128)S(1)} %constant_dynamic-slice_fusion), channel_id=1, source_target_pairs={{0,16},{16,0},{1,17},{17,1},{2,18},{18,2},{3,19},{19,3},{4,20},{20... | collective-permute-start | bytes 786440 | tf_op jit(solution)/shard_map/ppermute | solution.py:111
  153.1 6.6 %collective-permute-start.13 = (bf16[256,256]{1,0:T(8,128)(2,1)S(1)}, bf16[256,256]{1,0:T(8,128)(2,1)S(1)}, u32[]{:S(2)}, u32[]{:S(2)}) collective-permute-start(bf16[256,256]{1,0:T(8,128)(2,1)S(1)} %convolution_convert_fusion), channel_id=1, source_target_pairs={{0,16},{16,0},{1,17},{17,1},{2,18},{18,2},{3,19},{19,3},{4,20},{20... | collective-permute-start | bytes 393224 | tf_op jit(solution)/shard_map/ppermute | solution.py:116
  160.4 162.6 %reduce-scatter.5.cloned.1.call-start = ((), (), s32[]{:S(2)}) async-start(), calls=%async_computation.4 | async-start | bytes 2359296 | tf_op jit(solution)/shard_map/reduce_scatter | solution.py:177
  200.0 4.4 %collective-permute-start.14 = (bf16[4096,256]{1,0:T(8,128)(2,1)}, bf16[4096,256]{1,0:T(8,128)(2,1)S(1)}, u32[]{:S(2)}, u32[]{:S(2)}) collective-permute-start(bf16[4096,256]{1,0:T(8,128)(2,1)} %all-gather.2.cloned.1.call-done), channel_id=1, source_target_pairs={{0,1},{1,0},{2,3},{3,2},{4,5},{5,4},{6,7},{7,6},{8,9},{9,8},{10,11... | collective-permute-start | bytes 6291464 | tf_op jit(solution)/shard_map/ppermute | solution.py:116
  226.8 1.6 collective-permute-start.5
  228.5 30.6 %collective-permute-start.6 = (f32[256,256]{1,0:T(8,128)S(1)}, f32[256,256]{1,0:T(8,128)S(1)}, u32[]{:S(2)}, u32[]{:S(2)}) collective-permute-start(f32[256,256]{1,0:T(8,128)S(1)} %add.97), channel_id=1, source_target_pairs={{0,2},{1,3},{2,0},{3,1},{4,6},{5,7},{6,4},{7,5},{8,10},{9,11},{10,... | collective-permute-start | bytes 786440 | tf_op jit(solution)/shard_map/ppermute | solution.py:90
  259.1 14.4 %collective-permute-start.7 = (f32[256,256]{1,0:T(8,128)S(1)}, f32[256,256]{1,0:T(8,128)S(1)}, u32[]{:S(2)}, u32[]{:S(2)}) collective-permute-start(f32[256,256]{1,0:T(8,128)S(1)} %add.98), channel_id=1, source_target_pairs={{0,4},{1,5},{2,6},{3,7},{4,0},{5,1},{6,2},{7,3},{8,12},{9,13},{10,... | collective-permute-start | bytes 786440 | tf_op jit(solution)/shard_map/ppermute | solution.py:90
  273.5 16.7 %collective-permute-start.8 = (f32[256,256]{1,0:T(8,128)S(1)}, f32[256,256]{1,0:T(8,128)S(1)}, u32[]{:S(2)}, u32[]{:S(2)}) collective-permute-start(f32[256,256]{1,0:T(8,128)S(1)} %add.99), channel_id=1, source_target_pairs={{0,8},{1,9},{2,10},{3,11},{4,12},{5,13},{6,14},{7,15},{8,0},{9,1},... | collective-permute-start | bytes 786440 | tf_op jit(solution)/shard_map/ppermute | solution.py:90
  290.3 9.8 %collective-permute-start.9 = (f32[256,256]{1,0:T(8,128)S(1)}, f32[256,256]{1,0:T(8,128)S(1)}, u32[]{:S(2)}, u32[]{:S(2)}) collective-permute-start(f32[256,256]{1,0:T(8,128)S(1)} %add.100), channel_id=1, source_target_pairs={{0,16},{1,17},{2,18},{3,19},{4,20},{5,21},{6,22},{7,23},{8,24},{9,... | collective-permute-start | bytes 786440 | tf_op jit(solution)/shard_map/ppermute | solution.py:90
  300.1 7.6 %collective-permute-start.10 = (f32[256,256]{1,0:T(8,128)S(1)}, f32[256,256]{1,0:T(8,128)S(1)}, u32[]{:S(2)}, u32[]{:S(2)}) collective-permute-start(f32[256,256]{1,0:T(8,128)S(1)} %add.101), channel_id=1, source_target_pairs={{0,32},{1,33},{2,34},{3,35},{4,36},{5,37},{6,38},{7,39},{8,40},{9,... | collective-permute-start | bytes 786440 | tf_op jit(solution)/shard_map/ppermute | solution.py:90
  307.8 8.0 %collective-permute-start.11 = (f32[256,256]{1,0:T(8,128)S(1)}, f32[256,256]{1,0:T(8,128)S(1)}, u32[]{:S(2)}, u32[]{:S(2)}) collective-permute-start(f32[256,256]{1,0:T(8,128)S(1)} %add.102), channel_id=1, source_target_pairs={{0,64},{1,65},{2,66},{3,67},{4,68},{5,69},{6,70},{7,71},{8,72},{9,... | collective-permute-start | bytes 786440 | tf_op jit(solution)/shard_map/ppermute | solution.py:90
  315.8 6.5 %collective-permute-start.12 = (f32[256,256]{1,0:T(8,128)S(1)}, f32[256,256]{1,0:T(8,128)S(1)}, u32[]{:S(2)}, u32[]{:S(2)}) collective-permute-start(f32[256,256]{1,0:T(8,128)S(1)} %add.103), channel_id=1, source_target_pairs={{0,128},{1,129},{2,130},{3,131},{4,132},{5,133},{6,134},{7,135},{8... | collective-permute-start | bytes 786440 | tf_op jit(solution)/shard_map/ppermute | solution.py:90
Sparse Core Ops, SparseCore 0:
  65.8 74.4 reduce-scatter.2
  160.5 39.4 all-gather.1
  226.7 65.2 reduce-scatter.4

commit v8 on v7

--- a/solution.py
+++ b/solution.py
@@ -43,6 +43,35 @@
         out_ref[...] = out_ref[...] * scale
 
 
+def back_kernel(
+    live_ref, rows_ref, cols_ref, halves_ref, tiles_ref, own_ref, other_ref, out_ref, *,
+    per_block, scale
+):
+    block_id = pl.program_id(0)
+
+    @pl.when(block_id == 0)
+    def _():
+        out_ref[...] = jnp.zeros_like(out_ref)
+
+    live = live_ref[0]
+    for k in range(per_block):
+        slot = block_id * per_block + k
+        for half, half_ref in ((0, own_ref), (1, other_ref)):
+
+            @pl.when((slot < live) & (halves_ref[slot] == half))
+            def _(half_ref=half_ref):
+                tile_vals = tiles_ref[k].astype(jnp.bfloat16)
+                piece = half_ref[rows_ref[slot]]
+                product = lax.dot_general(
+                    tile_vals, piece, (((0,), (0,)), ((), ())), preferred_element_type=jnp.float32
+                )
+                out_ref[cols_ref[slot]] += product
+
+    @pl.when(block_id == pl.num_programs(0) - 1)
+    def _():
+        out_ref[...] = out_ref[...] * scale
+
+
 def slot_pass(live, row_ids, col_ids, tiles, source_tiles, out_tiles, scale, transpose):
     slot_total, tile_len, _ = tiles.shape
     width = source_tiles.shape[-1]
@@ -72,6 +101,38 @@
             dimension_semantics=("arbitrary",), vmem_limit_bytes=48 * 1024 * 1024
         ),
     )(live, row_ids, col_ids, tiles, source_tiles)
+
+
+def back_pass(live, row_ids, col_ids, halves, tiles, own_tiles, other_tiles, out_tiles, scale):
+    slot_total, tile_len, _ = tiles.shape
+    width = own_tiles.shape[-1]
+    per_block = math.gcd(slot_total, 16)
+
+    def tile_block(block_id, live_ref, rows_ref, cols_ref, halves_ref):
+        last = jnp.maximum(live_ref[0] - 1, 0) // per_block
+        return (jnp.minimum(block_id, last), 0, 0)
+
+    def whole(block_id, live_ref, rows_ref, cols_ref, halves_ref):
+        return (0, 0, 0)
+
+    grid_spec = pltpu.PrefetchScalarGridSpec(
+        num_scalar_prefetch=4,
+        grid=(slot_total // per_block,),
+        in_specs=[
+            pl.BlockSpec((per_block, tile_len, tile_len), tile_block),
+            pl.BlockSpec(own_tiles.shape, whole),
+            pl.BlockSpec(other_tiles.shape, whole),
+        ],
+        out_specs=pl.BlockSpec((out_tiles, tile_len, width), whole),
+    )
+    return pl.pallas_call(
+        functools.partial(back_kernel, per_block=per_block, scale=scale),
+        grid_spec=grid_spec,
+        out_shape=jax.ShapeDtypeStruct((out_tiles, tile_len, width), jnp.float32),
+        compiler_params=pltpu.CompilerParams(
+            dimension_semantics=("arbitrary",), vmem_limit_bytes=48 * 1024 * 1024
+        ),
+    )(live, row_ids, col_ids, halves, tiles, own_tiles, other_tiles)
 
 
 def dense_layer(aggregate, weight, cotangent):
@@ -170,9 +231,15 @@
     weight_sum = butterfly_sum(weight_part, every, row_n * col_n, levels)
     grad_source = pair_gather(grad_agg, "high")
     grad_source = lax.all_gather(grad_source, "mid", axis=0, tiled=True)
-    grad_source = pair_gather(grad_source, "core")
-    grad_tiles = grad_source.reshape(row_tiles, tile_len, width)
-    back_summed = slot_pass(live, placed, col_ids, weights_all, grad_tiles, col_tiles, scale, True)
+    grad_other = lax.ppermute(grad_source, "core", [(0, 1), (1, 0)])
+    half_tiles = row_tiles // core_n
+    own_tiles = grad_source.reshape(half_tiles, tile_len, width)
+    other_tiles = grad_other.reshape(half_tiles, tile_len, width)
+    halves = (core_i != lax.axis_index("core")).astype(jnp.int32)
+    back_summed = back_pass(
+        live, placed % half_tiles, col_ids, halves, weights_all, own_tiles, other_tiles,
+        col_tiles, scale,
+    )
     back_partial = back_summed.reshape(col_len, width)
     feature_grad = lax.psum_scatter(back_partial, "row", scatter_dimension=0, tiled=True).astype(
         jnp.bfloat16

time: 331 us -> 329 us (level)
  Pallas kernels: 34.3 us -> 43.3 us
  waiting for transfers between devices: 224 us -> 215 us
  other arithmetic: 14.4 us -> 10.6 us
    pallas_call x0 -> x1, Pallas kernels: none -> 23.3 us  [back_pass(): pl.pallas_call(functools.partial(back_kernel, per_block=per_block, scale=...]
    pallas_call x2 -> x1, Pallas kernels: 34.3 us -> 19.9 us  [slot_pass(): pl.pallas_call(functools.partial(slot_kernel, per_block=per_block, scale=...]
    reduce_scatter x1, waiting for transfers between devices: 74.6 us -> 69.3 us  [on_device(): lax.psum_scatter(partial_value, 'mid', scatter_dimension=0, tiled=True)]
    ppermute x0 -> x1, waiting for transfers between devices: none -> 4.37 us  [on_device(): grad_other = lax.ppermute(grad_source, 'core', [(0, 1), (1, 0)])]
    ppermute x2 -> x1, waiting for transfers between devices: 8.73 us -> 4.37 us  [pair_gather(): other = lax.ppermute(value, axis, [(0, 1), (1, 0)])]
where the time goes in v8:
time: 329 us; the launch traced here: 328 us
  waiting for transfers between devices  215 us (65%)
  Pallas kernels  43.3 us (13%)
  starting transfers between devices  34.9 us (11%)
  between operations  14.6 us (4%)
  other arithmetic  10.6 us (3%)
  local copies, waits for them, and re-layouts  7.93 us (2%)
    reduce_scatter x1, waiting for transfers between devices, on_device(): lax.psum_scatter(partial_value, 'mid', scatter_dimension=0, tiled=True)  69.3 us
    ppermute x8, waiting for transfers between devices, butterfly_sum(): value = value + lax.ppermute(value, axes, pairs)  65.3 us
    all_gather x1, waiting for transfers between devices, on_device(): grad_source = lax.all_gather(grad_source, 'mid', axis=0, tiled=True)  39.6 us
    ppermute x8, starting transfers between devices, butterfly_sum(): value = value + lax.ppermute(value, axes, pairs)  24.4 us
    pallas_call x1, Pallas kernels, back_pass(): pl.pallas_call(functools.partial(back_kernel, per_block=per_block, scale=...  23.3 us
    pallas_call x1, Pallas kernels, slot_pass(): pl.pallas_call(functools.partial(slot_kernel, per_block=per_block, scale=...  19.9 us
    ppermute x3, waiting for transfers between devices, doubling_gather(): other = lax.ppermute(value, axis, pairs)  17.8 us
    ppermute x1, waiting for transfers between devices, pair_scatter(): return keep + lax.ppermute(send, axis, [(0, 1), (1, 0)])  7.38 us
  transfers between devices with their start and end apart: 18, of which 17 were waited for; matrix products, arithmetic and copies ran while one was open for 1% of the time, Pallas kernels for 0%

profile of v8, /device:TPU:8, one launch (start us, length us, event | category | flops | bytes accessed | tf_op | source)
XLA Modules:
  0.0 327.8 jit_solution(2021117540275893302)
XLA Ops:
  7.2 1.6 collective-permute-start
  8.8 4.0 %collective-permute-done = bf16[256,256]{1,0:T(8,128)(2,1)S(1)} collective-permute-done((bf16[256,256]{1,0:T(8,128)(2,1)}, bf16[256,256]{1,0:T(8,128)(2,1)S(1)}, u32[]{:S(2)}, u32[]{:S(2)}) %collective-permute-start) | collective-permute-done | bytes 131104 | tf_op jit(solution)/shard_map/ppermute | solution.py:159
  13.7 3.1 collective-permute-start.1
  16.8 5.7 %collective-permute-done.1 = bf16[512,256]{1,0:T(8,128)(2,1)S(1)} collective-permute-done((bf16[512,256]{1,0:T(8,128)(2,1)S(1)}, bf16[512,256]{1,0:T(8,128)(2,1)S(1)}, u32[]{:S(2)}, u32[]{:S(2)}) %collective-permute-start.1) | collective-permute-done | bytes 262176 | tf_op jit(solution)/shard_map/ppermute | solution.py:159
  22.7 1.2 collective-permute-start.2
  26.6 8.1 %collective-permute-done.2 = bf16[1024,256]{1,0:T(8,128)(2,1)S(1)} collective-permute-done((bf16[1024,256]{1,0:T(8,128)(2,1)S(1)}, bf16[1024,256]{1,0:T(8,128)(2,1)S(1)}, u32[]{:S(2)}, u32[]{:S(2)}) %collective-permute-start.2) | collective-permute-done | bytes 524320 | tf_op jit(solution)/shard_map/ppermute | solution.py:159
  35.0 19.9 %shard_map.94 = f32[64,128,256]{2,1,0:T(8,128)} custom-call(s32[1]{0:T(128)} %bitcast.17.live_ref, s32[176]{0:T(256)S(1)} %multiply_add_fusion.rows_ref, s32[176]{0:T(256)S(1)} %bitcast.21, s32[176,128,128]{2,1,0:T(8,128)} %bitcast.23, bf16[16,128,256]{2,1,0:T(8,128)(2,1)S(1)} %bitcast.19), custom_call_target="tpu_custom_call" | custom-call | tf_op jit(solution)/shard_map/pallas_call | solution.py:96
  55.0 4.0 %fusion.7 = (f32[32,128,256]{2,1,0:T(8,128)S(1)}, f32[32,128,256]{2,1,0:T(8,128)S(1)}) fusion(f32[64,128,256]{2,1,0:T(8,128)} %shard_map.94), kind=kLoop, calls=%fused_computation.53 | loop fusion | bytes 16777216 | tf_op jit(solution)/shard_map/slice | solution.py:218
  59.1 7.1 %collective-permute-done.3 = f32[4096,256]{1,0:T(8,128)S(1)} collective-permute-done((f32[4096,256]{1,0:T(8,128)S(1)}, f32[4096,256]{1,0:T(8,128)S(1)}, u32[]{:S(2)}, u32[]{:S(2)}) %collective-permute-start.3) | collective-permute-done | bytes 4194336 | tf_op jit(solution)/shard_map/ppermute | solution.py:218
  66.2 2.8 bitcast_add_fusion
  69.1 69.3 %reduce-scatter.3.cloned.1.call-done = f32[512,256]{1,0:T(8,128)} async-done(((f32[4096,256]{1,0:T(8,128)}), f32[512,256]{1,0:T(8,128)}) %reduce-scatter.3.cloned.1.call-update) | async-done | bytes 524304 | tf_op jit(solution)/shard_map/reduce_scatter | solution.py:221
  139.3 2.2 collective-permute-start.4
  141.5 7.4 %collective-permute-done.4 = f32[256,256]{1,0:T(8,128)S(1)} collective-permute-done((f32[256,256]{1,0:T(8,128)S(1)}, f32[256,256]{1,0:T(8,128)S(1)}, u32[]{:S(2)}, u32[]{:S(2)}) %collective-permute-start.4) | collective-permute-done | bytes 262176 | tf_op jit(solution)/shard_map/ppermute | solution.py:172
  151.1 2.2 collective-permute-start.13
  153.3 4.4 %collective-permute-done.13 = bf16[256,256]{1,0:T(8,128)(2,1)S(1)} collective-permute-done((bf16[256,256]{1,0:T(8,128)(2,1)S(1)}, bf16[256,256]{1,0:T(8,128)(2,1)S(1)}, u32[]{:S(2)}, u32[]{:S(2)}) %collective-permute-start.13) | collective-permute-done | bytes 131104 | tf_op jit(solution)/shard_map/ppermute | solution.py:177
  158.5 39.6 %all-gather.2.cloned.1.call-done = bf16[4096,256]{1,0:T(8,128)(2,1)} async-done(((bf16[512,256]{1,0:T(8,128)(2,1)}), bf16[4096,256]{1,0:T(8,128)(2,1)}) %all-gather.2.cloned.1.call-update) | async-done | bytes 2097168 | tf_op jit(solution)/shard_map/all_gather | solution.py:233
  198.1 4.4 %collective-permute-done.14 = bf16[4096,256]{1,0:T(8,128)(2,1)S(1)} collective-permute-done((bf16[4096,256]{1,0:T(8,128)(2,1)}, bf16[4096,256]{1,0:T(8,128)(2,1)S(1)}, u32[]{:S(2)}, u32[]{:S(2)}) %collective-permute-start.14) | collective-permute-done | bytes 2097184 | tf_op jit(solution)/shard_map/ppermute | solution.py:234
  202.4 1.3 copy-done.3
  203.8 1.6 copy-done.1
  205.4 23.3 %shard_map.95 = f32[16,128,256]{2,1,0:T(8,128)} custom-call(s32[1]{0:T(128)} %bitcast.18.live_ref, s32[176]{0:T(256)S(1)} %get-tuple-element.5.rows_ref, s32[176]{0:T(256)S(1)} %bitcast.22, s32[176]{0:T(256)S(1)} %get-tuple-element.3.halves_ref, s32[176,128,128]{2,1,0:T(8,128)} %bitcast.24, bf16[32,128,256]{2,1,0:T(8,128)(2,1)S(1)} %bitcast.20, ...), custom_call_target="tpu_custom_call" | custom-call | tf_op jit(solution)/shard_map/pallas_call | solution.py:128
  229.0 1.5 collective-permute-done.5
  230.7 8.3 %collective-permute-done.6 = f32[256,256]{1,0:T(8,128)S(1)} collective-permute-done((f32[256,256]{1,0:T(8,128)S(1)}, f32[256,256]{1,0:T(8,128)S(1)}, u32[]{:S(2)}, u32[]{:S(2)}) %collective-permute-start.6) | collective-permute-done | bytes 262176 | tf_op jit(solution)/shard_map/ppermute | solution.py:151
  239.1 18.6 %collective-permute-start.7 = (f32[256,256]{1,0:T(8,128)S(1)}, f32[256,256]{1,0:T(8,128)S(1)}, u32[]{:S(2)}, u32[]{:S(2)}) collective-permute-start(f32[256,256]{1,0:T(8,128)S(1)} %add.102), channel_id=1, source_target_pairs={{0,4},{1,5},{2,6},{3,7},{4,0},{5,1},{6,2},{7,3},{8,12},{9,13},{10,... | collective-permute-start | bytes 786440 | tf_op jit(solution)/shard_map/ppermute | solution.py:151
  257.6 11.6 %collective-permute-done.7 = f32[256,256]{1,0:T(8,128)S(1)} collective-permute-done((f32[256,256]{1,0:T(8,128)S(1)}, f32[256,256]{1,0:T(8,128)S(1)}, u32[]{:S(2)}, u32[]{:S(2)}) %collective-permute-start.7) | collective-permute-done | bytes 262176 | tf_op jit(solution)/shard_map/ppermute | solution.py:151
  269.3 3.2 collective-permute-start.8
  272.5 14.4 %collective-permute-done.8 = f32[256,256]{1,0:T(8,128)S(1)} collective-permute-done((f32[256,256]{1,0:T(8,128)S(1)}, f32[256,256]{1,0:T(8,128)S(1)}, u32[]{:S(2)}, u32[]{:S(2)}) %collective-permute-start.8) | collective-permute-done | bytes 262176 | tf_op jit(solution)/shard_map/ppermute | solution.py:151
  286.9 2.2 collective-permute-start.9
  289.1 7.7 %collective-permute-done.9 = f32[256,256]{1,0:T(8,128)S(1)} collective-permute-done((f32[256,256]{1,0:T(8,128)S(1)}, f32[256,256]{1,0:T(8,128)S(1)}, u32[]{:S(2)}, u32[]{:S(2)}) %collective-permute-start.9) | collective-permute-done | bytes 262176 | tf_op jit(solution)/shard_map/ppermute | solution.py:151
  296.9 7.5 %collective-permute-done.10 = f32[256,256]{1,0:T(8,128)S(1)} collective-permute-done((f32[256,256]{1,0:T(8,128)S(1)}, f32[256,256]{1,0:T(8,128)S(1)}, u32[]{:S(2)}, u32[]{:S(2)}) %collective-permute-start.10) | collective-permute-done | bytes 262176 | tf_op jit(solution)/shard_map/ppermute | solution.py:151
  304.5 7.9 %collective-permute-done.11 = f32[256,256]{1,0:T(8,128)S(1)} collective-permute-done((f32[256,256]{1,0:T(8,128)S(1)}, f32[256,256]{1,0:T(8,128)S(1)}, u32[]{:S(2)}, u32[]{:S(2)}) %collective-permute-start.11) | collective-permute-done | bytes 262176 | tf_op jit(solution)/shard_map/ppermute | solution.py:151
  312.6 6.4 %collective-permute-done.12 = f32[256,256]{1,0:T(8,128)S(1)} collective-permute-done((f32[256,256]{1,0:T(8,128)S(1)}, f32[256,256]{1,0:T(8,128)S(1)}, u32[]{:S(2)}, u32[]{:S(2)}) %collective-permute-start.12) | collective-permute-done | bytes 262176 | tf_op jit(solution)/shard_map/ppermute | solution.py:151
  319.7 1.6 convert_element_type.28
  (46 shorter events, 9.3 us)
Async XLA Ops:
  7.2 142.7 %copy-start = (bf16[256,256]{1,0:T(8,128)(2,1)S(1)}, bf16[256,256]{1,0:T(8,128)(2,1)}, u32[]{:S(2)}) copy-start(bf16[256,256]{1,0:T(8,128)(2,1)} %param.8) | copy-start | bytes 393220
  7.2 27.8 %copy-start.2 = (s32[1,1,176]{2,1,0:T(1,128)S(1)}, s32[1,1,176]{2,1,0:T(1,128)}, u32[]{:S(2)}) copy-start(s32[1,1,176]{2,1,0:T(1,128)} %param.11) | copy-start | bytes 2116
  7.2 131.2 %reduce-scatter.3.cloned.1.call-start = ((), (), s32[]{:S(2)}) async-start(), calls=%async_computation.2 | async-start | bytes 4718592 | tf_op jit(solution)/shard_map/reduce_scatter | solution.py:221
  7.2 5.5 %collective-permute-start = (bf16[256,256]{1,0:T(8,128)(2,1)}, bf16[256,256]{1,0:T(8,128)(2,1)S(1)}, u32[]{:S(2)}, u32[]{:S(2)}) collective-permute-start(bf16[256,256]{1,0:T(8,128)(2,1)} %param.7), channel_id=1, source_target_pairs={{0,32},{32,0},{64,96},{96,64},{128,160},{160,128},{192,224},{224,1... | collective-permute-start | bytes 393224 | tf_op jit(solution)/shard_map/ppermute | solution.py:159
  13.7 8.8 %collective-permute-start.1 = (bf16[512,256]{1,0:T(8,128)(2,1)S(1)}, bf16[512,256]{1,0:T(8,128)(2,1)S(1)}, u32[]{:S(2)}, u32[]{:S(2)}) collective-permute-start(bf16[512,256]{1,0:T(8,128)(2,1)S(1)} %pad_maximum_fusion.2), channel_id=1, source_target_pairs={{0,64},{32,96},{64,0},{96,32},{128,192},{160,224},{192,128},{224,1... | collective-permute-start | bytes 786440 | tf_op jit(solution)/shard_map/ppermute | solution.py:159
  22.7 12.0 %collective-permute-start.2 = (bf16[1024,256]{1,0:T(8,128)(2,1)S(1)}, bf16[1024,256]{1,0:T(8,128)(2,1)S(1)}, u32[]{:S(2)}, u32[]{:S(2)}) collective-permute-start(bf16[1024,256]{1,0:T(8,128)(2,1)S(1)} %pad_maximum_fusion.1), channel_id=1, source_target_pairs={{0,128},{32,160},{64,192},{96,224},{128,0},{160,32},{192,64},{224,... | collective-permute-start | bytes 1572872 | tf_op jit(solution)/shard_map/ppermute | solution.py:159
  59.0 7.2 %collective-permute-start.3 = (f32[4096,256]{1,0:T(8,128)S(1)}, f32[4096,256]{1,0:T(8,128)S(1)}, u32[]{:S(2)}, u32[]{:S(2)}) collective-permute-start(f32[4096,256]{1,0:T(8,128)S(1)} %bitcast.25), channel_id=1, source_target_pairs={{0,1},{1,0},{2,3},{3,2},{4,5},{5,4},{6,7},{7,6},{8,9},{9,8},{10,11... | collective-permute-start | bytes 12582920 | tf_op jit(solution)/shard_map/ppermute | solution.py:218
  69.0 80.9 %copy-start.4 = (bf16[256,256]{1,0:T(8,128)(2,1)S(1)}, bf16[256,256]{1,0:T(8,128)(2,1)}, u32[]{:S(2)}) copy-start(bf16[256,256]{1,0:T(8,128)(2,1)} %param.9) | copy-start | bytes 393220
  69.0 129.0 %all-gather.2.cloned.1.call-start = ((), (), s32[]{:S(2)}) async-start(), calls=%async_computation.3 | async-start | bytes 2359296 | tf_op jit(solution)/shard_map/all_gather | solution.py:233
  139.3 9.6 %collective-permute-start.4 = (f32[256,256]{1,0:T(8,128)S(1)}, f32[256,256]{1,0:T(8,128)S(1)}, u32[]{:S(2)}, u32[]{:S(2)}) collective-permute-start(f32[256,256]{1,0:T(8,128)S(1)} %constant_dynamic-slice_fusion), channel_id=1, source_target_pairs={{0,16},{16,0},{1,17},{17,1},{2,18},{18,2},{3,19},{19,3},{4,20},{20... | collective-permute-start | bytes 786440 | tf_op jit(solution)/shard_map/ppermute | solution.py:172
  151.1 6.6 %collective-permute-start.13 = (bf16[256,256]{1,0:T(8,128)(2,1)S(1)}, bf16[256,256]{1,0:T(8,128)(2,1)S(1)}, u32[]{:S(2)}, u32[]{:S(2)}) collective-permute-start(bf16[256,256]{1,0:T(8,128)(2,1)S(1)} %convolution_convert_fusion), channel_id=1, source_target_pairs={{0,16},{16,0},{1,17},{17,1},{2,18},{18,2},{3,19},{19,3},{4,20},{20... | collective-permute-start | bytes 393224 | tf_op jit(solution)/shard_map/ppermute | solution.py:177
  158.4 161.2 %reduce-scatter.5.cloned.1.call-start = ((), (), s32[]{:S(2)}) async-start(), calls=%async_computation.4 | async-start | bytes 2359296 | tf_op jit(solution)/shard_map/reduce_scatter | solution.py:244
  198.0 4.4 %collective-permute-start.14 = (bf16[4096,256]{1,0:T(8,128)(2,1)}, bf16[4096,256]{1,0:T(8,128)(2,1)S(1)}, u32[]{:S(2)}, u32[]{:S(2)}) collective-permute-start(bf16[4096,256]{1,0:T(8,128)(2,1)} %all-gather.2.cloned.1.call-done), channel_id=1, source_target_pairs={{0,1},{1,0},{2,3},{3,2},{4,5},{5,4},{6,7},{7,6},{8,9},{9,8},{10,11... | collective-permute-start | bytes 6291464 | tf_op jit(solution)/shard_map/ppermute | solution.py:234
  202.4 1.3 copy-start.3
  203.8 1.6 copy-start.1
  228.9 1.6 collective-permute-start.5
  230.6 8.4 %collective-permute-start.6 = (f32[256,256]{1,0:T(8,128)S(1)}, f32[256,256]{1,0:T(8,128)S(1)}, u32[]{:S(2)}, u32[]{:S(2)}) collective-permute-start(f32[256,256]{1,0:T(8,128)S(1)} %add.101), channel_id=1, source_target_pairs={{0,2},{1,3},{2,0},{3,1},{4,6},{5,7},{6,4},{7,5},{8,10},{9,11},{10,... | collective-permute-start | bytes 786440 | tf_op jit(solution)/shard_map/ppermute | solution.py:151
  239.1 30.2 %collective-permute-start.7 = (f32[256,256]{1,0:T(8,128)S(1)}, f32[256,256]{1,0:T(8,128)S(1)}, u32[]{:S(2)}, u32[]{:S(2)}) collective-permute-start(f32[256,256]{1,0:T(8,128)S(1)} %add.102), channel_id=1, source_target_pairs={{0,4},{1,5},{2,6},{3,7},{4,0},{5,1},{6,2},{7,3},{8,12},{9,13},{10,... | collective-permute-start | bytes 786440 | tf_op jit(solution)/shard_map/ppermute | solution.py:151
  269.3 17.6 %collective-permute-start.8 = (f32[256,256]{1,0:T(8,128)S(1)}, f32[256,256]{1,0:T(8,128)S(1)}, u32[]{:S(2)}, u32[]{:S(2)}) collective-permute-start(f32[256,256]{1,0:T(8,128)S(1)} %add.103), channel_id=1, source_target_pairs={{0,8},{1,9},{2,10},{3,11},{4,12},{5,13},{6,14},{7,15},{8,0},{9,1},... | collective-permute-start | bytes 786440 | tf_op jit(solution)/shard_map/ppermute | solution.py:151
  286.9 9.8 %collective-permute-start.9 = (f32[256,256]{1,0:T(8,128)S(1)}, f32[256,256]{1,0:T(8,128)S(1)}, u32[]{:S(2)}, u32[]{:S(2)}) collective-permute-start(f32[256,256]{1,0:T(8,128)S(1)} %add.104), channel_id=1, source_target_pairs={{0,16},{1,17},{2,18},{3,19},{4,20},{5,21},{6,22},{7,23},{8,24},{9,... | collective-permute-start | bytes 786440 | tf_op jit(solution)/shard_map/ppermute | solution.py:151
  296.8 7.6 %collective-permute-start.10 = (f32[256,256]{1,0:T(8,128)S(1)}, f32[256,256]{1,0:T(8,128)S(1)}, u32[]{:S(2)}, u32[]{:S(2)}) collective-permute-start(f32[256,256]{1,0:T(8,128)S(1)} %add.105), channel_id=1, source_target_pairs={{0,32},{1,33},{2,34},{3,35},{4,36},{5,37},{6,38},{7,39},{8,40},{9,... | collective-permute-start | bytes 786440 | tf_op jit(solution)/shard_map/ppermute | solution.py:151
  304.4 8.0 %collective-permute-start.11 = (f32[256,256]{1,0:T(8,128)S(1)}, f32[256,256]{1,0:T(8,128)S(1)}, u32[]{:S(2)}, u32[]{:S(2)}) collective-permute-start(f32[256,256]{1,0:T(8,128)S(1)} %add.106), channel_id=1, source_target_pairs={{0,64},{1,65},{2,66},{3,67},{4,68},{5,69},{6,70},{7,71},{8,72},{9,... | collective-permute-start | bytes 786440 | tf_op jit(solution)/shard_map/ppermute | solution.py:151
  312.5 6.5 %collective-permute-start.12 = (f32[256,256]{1,0:T(8,128)S(1)}, f32[256,256]{1,0:T(8,128)S(1)}, u32[]{:S(2)}, u32[]{:S(2)}) collective-permute-start(f32[256,256]{1,0:T(8,128)S(1)} %add.107), channel_id=1, source_target_pairs={{0,128},{1,129},{2,130},{3,131},{4,132},{5,133},{6,134},{7,135},{8... | collective-permute-start | bytes 786440 | tf_op jit(solution)/shard_map/ppermute | solution.py:151
Sparse Core Ops, SparseCore 0:
  69.1 69.1 reduce-scatter.2
  158.5 39.4 all-gather.1
  228.8 58.4 reduce-scatter.4

commit v9 on v8

--- a/solution.py
+++ b/solution.py
@@ -145,9 +145,20 @@
     return (hidden, grad_pre)
 
 
-def butterfly_sum(value, axes, count, levels):
+def butterfly_sum(value, axes, count, levels, ring_bits):
+    low_bit, ring_n = ring_bits
+    label = [p ^ (p >> 1) for p in range(ring_n)]
+    position = {g: p for p, g in enumerate(label)}
+
+    def partner(i, level):
+        if low_bit <= level < low_bit + ring_n.bit_length() - 1:
+            p = (i >> low_bit) % ring_n
+            q = position[label[p] ^ (1 << (level - low_bit))]
+            return i + ((q - p) << low_bit)
+        return i ^ (1 << level)
+
     for level in levels:
-        pairs = [(i, i ^ (1 << level)) for i in range(count)]
+        pairs = [(i, partner(i, level)) for i in range(count)]
         value = value + lax.ppermute(value, axes, pairs)
     return value
 
@@ -228,7 +239,9 @@
     grad_agg = jnp.dot(grad_own, weight.T, preferred_element_type=jnp.float32).astype(jnp.bfloat16)
     every = ("row",) + col_axes
     levels = list(range((row_n * col_n).bit_length() - 1))
-    weight_sum = butterfly_sum(weight_part, every, row_n * col_n, levels)
+    weight_sum = butterfly_sum(
+        weight_part, every, row_n * col_n, levels, ((core_n - 1).bit_length(), mid_n)
+    )
     grad_source = pair_gather(grad_agg, "high")
     grad_source = lax.all_gather(grad_source, "mid", axis=0, tiled=True)
     grad_other = lax.ppermute(grad_source, "core", [(0, 1), (1, 0)])

time: 329 us -> 325 us (0.988)
  waiting for transfers between devices: 215 us -> 202 us
  starting transfers between devices: 34.9 us -> 44.5 us
  Pallas kernels: 43.3 us -> 39.9 us
    ppermute x8, waiting for transfers between devices: 65.3 us -> 49.8 us  [butterfly_sum(): value = value + lax.ppermute(value, axes, pairs)]
    ppermute x8, starting transfers between devices: 24.4 us -> 34.1 us  [butterfly_sum(): value = value + lax.ppermute(value, axes, pairs)]
where the time goes in v9:
time: 325 us; the launch traced here: 321 us
  waiting for transfers between devices  202 us (62%)
  starting transfers between devices  44.5 us (14%)
  Pallas kernels  39.9 us (12%)
  between operations  14.6 us (4%)
  other arithmetic  10.6 us (3%)
  local copies, waits for them, and re-layouts  7.93 us (2%)
    reduce_scatter x1, waiting for transfers between devices, on_device(): lax.psum_scatter(partial_value, 'mid', scatter_dimension=0, tiled=True)  71.3 us
    ppermute x8, waiting for transfers between devices, butterfly_sum(): value = value + lax.ppermute(value, axes, pairs)  49.8 us
    all_gather x1, waiting for transfers between devices, on_device(): grad_source = lax.all_gather(grad_source, 'mid', axis=0, tiled=True)  39.6 us
    ppermute x8, starting transfers between devices, butterfly_sum(): value = value + lax.ppermute(value, axes, pairs)  34.1 us
    pallas_call x1, Pallas kernels, back_pass(): pl.pallas_call(functools.partial(back_kernel, per_block=per_block, scale=...  21.5 us
    pallas_call x1, Pallas kernels, slot_pass(): pl.pallas_call(functools.partial(slot_kernel, per_block=per_block, scale=...  18.5 us
    ppermute x3, waiting for transfers between devices, doubling_gather(): other = lax.ppermute(value, axis, pairs)  17.8 us
    ppermute x1, waiting for transfers between devices, pair_scatter(): return keep + lax.ppermute(send, axis, [(0, 1), (1, 0)])  7.38 us
  transfers between devices with their start and end apart: 18, of which 17 were waited for; matrix products, arithmetic and copies ran while one was open for 1% of the time, Pallas kernels for 0%

profile of v9, /device:TPU:8, one launch (start us, length us, event | category | flops | bytes accessed | tf_op | source)
XLA Modules:
  0.0 320.7 jit_solution(12068615820555619365)
XLA Ops:
  7.2 1.6 collective-permute-start
  8.8 4.0 %collective-permute-done = bf16[256,256]{1,0:T(8,128)(2,1)S(1)} collective-permute-done((bf16[256,256]{1,0:T(8,128)(2,1)}, bf16[256,256]{1,0:T(8,128)(2,1)S(1)}, u32[]{:S(2)}, u32[]{:S(2)}) %collective-permute-start) | collective-permute-done | bytes 131104 | tf_op jit(solution)/shard_map/ppermute | solution.py:170
  13.7 3.1 collective-permute-start.1
  16.8 5.7 %collective-permute-done.1 = bf16[512,256]{1,0:T(8,128)(2,1)S(1)} collective-permute-done((bf16[512,256]{1,0:T(8,128)(2,1)S(1)}, bf16[512,256]{1,0:T(8,128)(2,1)S(1)}, u32[]{:S(2)}, u32[]{:S(2)}) %collective-permute-start.1) | collective-permute-done | bytes 262176 | tf_op jit(solution)/shard_map/ppermute | solution.py:170
  26.6 8.1 %collective-permute-done.2 = bf16[1024,256]{1,0:T(8,128)(2,1)S(1)} collective-permute-done((bf16[1024,256]{1,0:T(8,128)(2,1)S(1)}, bf16[1024,256]{1,0:T(8,128)(2,1)S(1)}, u32[]{:S(2)}, u32[]{:S(2)}) %collective-permute-start.2) | collective-permute-done | bytes 524320 | tf_op jit(solution)/shard_map/ppermute | solution.py:170
  35.0 18.5 %shard_map.94 = f32[64,128,256]{2,1,0:T(8,128)} custom-call(s32[1]{0:T(128)} %bitcast.17.live_ref, s32[176]{0:T(256)S(1)} %multiply_add_fusion.rows_ref, s32[176]{0:T(256)S(1)} %bitcast.21, s32[176,128,128]{2,1,0:T(8,128)} %bitcast.23, bf16[16,128,256]{2,1,0:T(8,128)(2,1)S(1)} %bitcast.19), custom_call_target="tpu_custom_call" | custom-call | tf_op jit(solution)/shard_map/pallas_call | solution.py:96
  53.5 4.0 %fusion.7 = (f32[32,128,256]{2,1,0:T(8,128)S(1)}, f32[32,128,256]{2,1,0:T(8,128)S(1)}) fusion(f32[64,128,256]{2,1,0:T(8,128)} %shard_map.94), kind=kLoop, calls=%fused_computation.53 | loop fusion | bytes 16777216 | tf_op jit(solution)/shard_map/slice | solution.py:229
  57.6 7.1 %collective-permute-done.3 = f32[4096,256]{1,0:T(8,128)S(1)} collective-permute-done((f32[4096,256]{1,0:T(8,128)S(1)}, f32[4096,256]{1,0:T(8,128)S(1)}, u32[]{:S(2)}, u32[]{:S(2)}) %collective-permute-start.3) | collective-permute-done | bytes 4194336 | tf_op jit(solution)/shard_map/ppermute | solution.py:229
  64.8 2.8 bitcast_add_fusion
  67.6 71.3 %reduce-scatter.3.cloned.1.call-done = f32[512,256]{1,0:T(8,128)} async-done(((f32[4096,256]{1,0:T(8,128)}), f32[512,256]{1,0:T(8,128)}) %reduce-scatter.3.cloned.1.call-update) | async-done | bytes 524304 | tf_op jit(solution)/shard_map/reduce_scatter | solution.py:232
  139.9 2.2 collective-permute-start.4
  142.1 7.4 %collective-permute-done.4 = f32[256,256]{1,0:T(8,128)S(1)} collective-permute-done((f32[256,256]{1,0:T(8,128)S(1)}, f32[256,256]{1,0:T(8,128)S(1)}, u32[]{:S(2)}, u32[]{:S(2)}) %collective-permute-start.4) | collective-permute-done | bytes 262176 | tf_op jit(solution)/shard_map/ppermute | solution.py:183
  151.6 2.2 collective-permute-start.13
  153.8 4.4 %collective-permute-done.13 = bf16[256,256]{1,0:T(8,128)(2,1)S(1)} collective-permute-done((bf16[256,256]{1,0:T(8,128)(2,1)S(1)}, bf16[256,256]{1,0:T(8,128)(2,1)S(1)}, u32[]{:S(2)}, u32[]{:S(2)}) %collective-permute-start.13) | collective-permute-done | bytes 131104 | tf_op jit(solution)/shard_map/ppermute | solution.py:188
  159.0 39.6 %all-gather.2.cloned.1.call-done = bf16[4096,256]{1,0:T(8,128)(2,1)} async-done(((bf16[512,256]{1,0:T(8,128)(2,1)}), bf16[4096,256]{1,0:T(8,128)(2,1)}) %all-gather.2.cloned.1.call-update) | async-done | bytes 2097168 | tf_op jit(solution)/shard_map/all_gather | solution.py:246
  198.6 4.4 %collective-permute-done.14 = bf16[4096,256]{1,0:T(8,128)(2,1)S(1)} collective-permute-done((bf16[4096,256]{1,0:T(8,128)(2,1)}, bf16[4096,256]{1,0:T(8,128)(2,1)S(1)}, u32[]{:S(2)}, u32[]{:S(2)}) %collective-permute-start.14) | collective-permute-done | bytes 2097184 | tf_op jit(solution)/shard_map/ppermute | solution.py:247
  204.3 1.6 copy-done.1
  205.9 21.5 %shard_map.95 = f32[16,128,256]{2,1,0:T(8,128)} custom-call(s32[1]{0:T(128)} %bitcast.18.live_ref, s32[176]{0:T(256)S(1)} %get-tuple-element.5.rows_ref, s32[176]{0:T(256)S(1)} %bitcast.22, s32[176]{0:T(256)S(1)} %get-tuple-element.3.halves_ref, s32[176,128,128]{2,1,0:T(8,128)} %bitcast.24, bf16[32,128,256]{2,1,0:T(8,128)(2,1)S(1)} %bitcast.20, ...), custom_call_target="tpu_custom_call" | custom-call | tf_op jit(solution)/shard_map/pallas_call | solution.py:128
  227.7 1.5 collective-permute-done.5
  229.3 3.4 %collective-permute-start.6 = (f32[256,256]{1,0:T(8,128)S(1)}, f32[256,256]{1,0:T(8,128)S(1)}, u32[]{:S(2)}, u32[]{:S(2)}) collective-permute-start(f32[256,256]{1,0:T(8,128)S(1)} %add.101), channel_id=1, source_target_pairs={{0,2},{1,3},{2,0},{3,1},{4,6},{5,7},{6,4},{7,5},{8,10},{9,11},{10,... | collective-permute-start | bytes 786440 | tf_op jit(solution)/shard_map/ppermute | solution.py:162
  232.7 6.6 %collective-permute-done.6 = f32[256,256]{1,0:T(8,128)S(1)} collective-permute-done((f32[256,256]{1,0:T(8,128)S(1)}, f32[256,256]{1,0:T(8,128)S(1)}, u32[]{:S(2)}, u32[]{:S(2)}) %collective-permute-start.6) | collective-permute-done | bytes 262176 | tf_op jit(solution)/shard_map/ppermute | solution.py:162
  239.3 3.9 %collective-permute-start.7 = (f32[256,256]{1,0:T(8,128)S(1)}, f32[256,256]{1,0:T(8,128)S(1)}, u32[]{:S(2)}, u32[]{:S(2)}) collective-permute-start(f32[256,256]{1,0:T(8,128)S(1)} %add.102), channel_id=1, source_target_pairs={{0,6},{1,7},{2,4},{3,5},{4,2},{5,3},{6,0},{7,1},{8,14},{9,15},{10,... | collective-permute-start | bytes 786440 | tf_op jit(solution)/shard_map/ppermute | solution.py:162
  243.2 6.1 %collective-permute-done.7 = f32[256,256]{1,0:T(8,128)S(1)} collective-permute-done((f32[256,256]{1,0:T(8,128)S(1)}, f32[256,256]{1,0:T(8,128)S(1)}, u32[]{:S(2)}, u32[]{:S(2)}) %collective-permute-start.7) | collective-permute-done | bytes 262176 | tf_op jit(solution)/shard_map/ppermute | solution.py:162
  249.4 17.2 %collective-permute-start.8 = (f32[256,256]{1,0:T(8,128)S(1)}, f32[256,256]{1,0:T(8,128)S(1)}, u32[]{:S(2)}, u32[]{:S(2)}) collective-permute-start(f32[256,256]{1,0:T(8,128)S(1)} %add.103), channel_id=1, source_target_pairs={{0,14},{1,15},{2,12},{3,13},{4,10},{5,11},{6,8},{7,9},{8,6},{9,7},... | collective-permute-start | bytes 786440 | tf_op jit(solution)/shard_map/ppermute | solution.py:162
  266.6 5.7 %collective-permute-done.8 = f32[256,256]{1,0:T(8,128)S(1)} collective-permute-done((f32[256,256]{1,0:T(8,128)S(1)}, f32[256,256]{1,0:T(8,128)S(1)}, u32[]{:S(2)}, u32[]{:S(2)}) %collective-permute-start.8) | collective-permute-done | bytes 262176 | tf_op jit(solution)/shard_map/ppermute | solution.py:162
  272.5 14.7 %collective-permute-done.9 = f32[256,256]{1,0:T(8,128)S(1)} collective-permute-done((f32[256,256]{1,0:T(8,128)S(1)}, f32[256,256]{1,0:T(8,128)S(1)}, u32[]{:S(2)}, u32[]{:S(2)}) %collective-permute-start.9) | collective-permute-done | bytes 262176 | tf_op jit(solution)/shard_map/ppermute | solution.py:162
  287.3 6.4 %collective-permute-done.10 = f32[256,256]{1,0:T(8,128)S(1)} collective-permute-done((f32[256,256]{1,0:T(8,128)S(1)}, f32[256,256]{1,0:T(8,128)S(1)}, u32[]{:S(2)}, u32[]{:S(2)}) %collective-permute-start.10) | collective-permute-done | bytes 262176 | tf_op jit(solution)/shard_map/ppermute | solution.py:162
  293.8 6.2 %collective-permute-start.11 = (f32[256,256]{1,0:T(8,128)S(1)}, f32[256,256]{1,0:T(8,128)S(1)}, u32[]{:S(2)}, u32[]{:S(2)}) collective-permute-start(f32[256,256]{1,0:T(8,128)S(1)} %add.106), channel_id=1, source_target_pairs={{0,64},{1,65},{2,66},{3,67},{4,68},{5,69},{6,70},{7,71},{8,72},{9,... | collective-permute-start | bytes 786440 | tf_op jit(solution)/shard_map/ppermute | solution.py:162
  300.0 4.4 %collective-permute-done.11 = f32[256,256]{1,0:T(8,128)S(1)} collective-permute-done((f32[256,256]{1,0:T(8,128)S(1)}, f32[256,256]{1,0:T(8,128)S(1)}, u32[]{:S(2)}, u32[]{:S(2)}) %collective-permute-start.11) | collective-permute-done | bytes 262176 | tf_op jit(solution)/shard_map/ppermute | solution.py:162
  304.4 3.0 collective-permute-start.12
  307.4 4.4 %collective-permute-done.12 = f32[256,256]{1,0:T(8,128)S(1)} collective-permute-done((f32[256,256]{1,0:T(8,128)S(1)}, f32[256,256]{1,0:T(8,128)S(1)}, u32[]{:S(2)}, u32[]{:S(2)}) %collective-permute-start.12) | collective-permute-done | bytes 262176 | tf_op jit(solution)/shard_map/ppermute | solution.py:162
  312.5 1.6 convert_element_type.28
  (46 shorter events, 11.6 us)
Async XLA Ops:
  7.2 143.3 %copy-start = (bf16[256,256]{1,0:T(8,128)(2,1)S(1)}, bf16[256,256]{1,0:T(8,128)(2,1)}, u32[]{:S(2)}) copy-start(bf16[256,256]{1,0:T(8,128)(2,1)} %param.8) | copy-start | bytes 393220
  7.2 27.8 %copy-start.2 = (s32[1,1,176]{2,1,0:T(1,128)S(1)}, s32[1,1,176]{2,1,0:T(1,128)}, u32[]{:S(2)}) copy-start(s32[1,1,176]{2,1,0:T(1,128)} %param.11) | copy-start | bytes 2116
  7.2 131.7 %reduce-scatter.3.cloned.1.call-start = ((), (), s32[]{:S(2)}) async-start(), calls=%async_computation.2 | async-start | bytes 4718592 | tf_op jit(solution)/shard_map/reduce_scatter | solution.py:232
  7.2 5.5 %collective-permute-start = (bf16[256,256]{1,0:T(8,128)(2,1)}, bf16[256,256]{1,0:T(8,128)(2,1)S(1)}, u32[]{:S(2)}, u32[]{:S(2)}) collective-permute-start(bf16[256,256]{1,0:T(8,128)(2,1)} %param.7), channel_id=1, source_target_pairs={{0,32},{32,0},{64,96},{96,64},{128,160},{160,128},{192,224},{224,1... | collective-permute-start | bytes 393224 | tf_op jit(solution)/shard_map/ppermute | solution.py:170
  13.7 8.8 %collective-permute-start.1 = (bf16[512,256]{1,0:T(8,128)(2,1)S(1)}, bf16[512,256]{1,0:T(8,128)(2,1)S(1)}, u32[]{:S(2)}, u32[]{:S(2)}) collective-permute-start(bf16[512,256]{1,0:T(8,128)(2,1)S(1)} %pad_maximum_fusion.2), channel_id=1, source_target_pairs={{0,64},{32,96},{64,0},{96,32},{128,192},{160,224},{192,128},{224,1... | collective-permute-start | bytes 786440 | tf_op jit(solution)/shard_map/ppermute | solution.py:170
  22.7 12.0 %collective-permute-start.2 = (bf16[1024,256]{1,0:T(8,128)(2,1)S(1)}, bf16[1024,256]{1,0:T(8,128)(2,1)S(1)}, u32[]{:S(2)}, u32[]{:S(2)}) collective-permute-start(bf16[1024,256]{1,0:T(8,128)(2,1)S(1)} %pad_maximum_fusion.1), channel_id=1, source_target_pairs={{0,128},{32,160},{64,192},{96,224},{128,0},{160,32},{192,64},{224,... | collective-permute-start | bytes 1572872 | tf_op jit(solution)/shard_map/ppermute | solution.py:170
  57.5 7.2 %collective-permute-start.3 = (f32[4096,256]{1,0:T(8,128)S(1)}, f32[4096,256]{1,0:T(8,128)S(1)}, u32[]{:S(2)}, u32[]{:S(2)}) collective-permute-start(f32[4096,256]{1,0:T(8,128)S(1)} %bitcast.25), channel_id=1, source_target_pairs={{0,1},{1,0},{2,3},{3,2},{4,5},{5,4},{6,7},{7,6},{8,9},{9,8},{10,11... | collective-permute-start | bytes 12582920 | tf_op jit(solution)/shard_map/ppermute | solution.py:229
  67.5 82.9 %copy-start.4 = (bf16[256,256]{1,0:T(8,128)(2,1)S(1)}, bf16[256,256]{1,0:T(8,128)(2,1)}, u32[]{:S(2)}) copy-start(bf16[256,256]{1,0:T(8,128)(2,1)} %param.9) | copy-start | bytes 393220
  67.6 131.0 %all-gather.2.cloned.1.call-start = ((), (), s32[]{:S(2)}) async-start(), calls=%async_computation.3 | async-start | bytes 2359296 | tf_op jit(solution)/shard_map/all_gather | solution.py:246
  139.9 9.6 %collective-permute-start.4 = (f32[256,256]{1,0:T(8,128)S(1)}, f32[256,256]{1,0:T(8,128)S(1)}, u32[]{:S(2)}, u32[]{:S(2)}) collective-permute-start(f32[256,256]{1,0:T(8,128)S(1)} %constant_dynamic-slice_fusion), channel_id=1, source_target_pairs={{0,16},{16,0},{1,17},{17,1},{2,18},{18,2},{3,19},{19,3},{4,20},{20... | collective-permute-start | bytes 786440 | tf_op jit(solution)/shard_map/ppermute | solution.py:183
  151.6 6.6 %collective-permute-start.13 = (bf16[256,256]{1,0:T(8,128)(2,1)S(1)}, bf16[256,256]{1,0:T(8,128)(2,1)S(1)}, u32[]{:S(2)}, u32[]{:S(2)}) collective-permute-start(bf16[256,256]{1,0:T(8,128)(2,1)S(1)} %convolution_convert_fusion), channel_id=1, source_target_pairs={{0,16},{16,0},{1,17},{17,1},{2,18},{18,2},{3,19},{19,3},{4,20},{20... | collective-permute-start | bytes 393224 | tf_op jit(solution)/shard_map/ppermute | solution.py:188
  158.9 153.6 %reduce-scatter.5.cloned.1.call-start = ((), (), s32[]{:S(2)}) async-start(), calls=%async_computation.4 | async-start | bytes 2359296 | tf_op jit(solution)/shard_map/reduce_scatter | solution.py:257
  198.6 4.4 %collective-permute-start.14 = (bf16[4096,256]{1,0:T(8,128)(2,1)}, bf16[4096,256]{1,0:T(8,128)(2,1)S(1)}, u32[]{:S(2)}, u32[]{:S(2)}) collective-permute-start(bf16[4096,256]{1,0:T(8,128)(2,1)} %all-gather.2.cloned.1.call-done), channel_id=1, source_target_pairs={{0,1},{1,0},{2,3},{3,2},{4,5},{5,4},{6,7},{7,6},{8,9},{9,8},{10,11... | collective-permute-start | bytes 6291464 | tf_op jit(solution)/shard_map/ppermute | solution.py:247
  203.0 1.3 copy-start.3
  204.3 1.6 copy-start.1
  227.6 1.6 collective-permute-start.5
  229.3 10.0 %collective-permute-start.6 = (f32[256,256]{1,0:T(8,128)S(1)}, f32[256,256]{1,0:T(8,128)S(1)}, u32[]{:S(2)}, u32[]{:S(2)}) collective-permute-start(f32[256,256]{1,0:T(8,128)S(1)} %add.101), channel_id=1, source_target_pairs={{0,2},{1,3},{2,0},{3,1},{4,6},{5,7},{6,4},{7,5},{8,10},{9,11},{10,... | collective-permute-start | bytes 786440 | tf_op jit(solution)/shard_map/ppermute | solution.py:162
  239.3 10.0 %collective-permute-start.7 = (f32[256,256]{1,0:T(8,128)S(1)}, f32[256,256]{1,0:T(8,128)S(1)}, u32[]{:S(2)}, u32[]{:S(2)}) collective-permute-start(f32[256,256]{1,0:T(8,128)S(1)} %add.102), channel_id=1, source_target_pairs={{0,6},{1,7},{2,4},{3,5},{4,2},{5,3},{6,0},{7,1},{8,14},{9,15},{10,... | collective-permute-start | bytes 786440 | tf_op jit(solution)/shard_map/ppermute | solution.py:162
  249.4 23.0 %collective-permute-start.8 = (f32[256,256]{1,0:T(8,128)S(1)}, f32[256,256]{1,0:T(8,128)S(1)}, u32[]{:S(2)}, u32[]{:S(2)}) collective-permute-start(f32[256,256]{1,0:T(8,128)S(1)} %add.103), channel_id=1, source_target_pairs={{0,14},{1,15},{2,12},{3,13},{4,10},{5,11},{6,8},{7,9},{8,6},{9,7},... | collective-permute-start | bytes 786440 | tf_op jit(solution)/shard_map/ppermute | solution.py:162
  272.4 14.8 %collective-permute-start.9 = (f32[256,256]{1,0:T(8,128)S(1)}, f32[256,256]{1,0:T(8,128)S(1)}, u32[]{:S(2)}, u32[]{:S(2)}) collective-permute-start(f32[256,256]{1,0:T(8,128)S(1)} %add.104), channel_id=1, source_target_pairs={{0,16},{1,17},{2,18},{3,19},{4,20},{5,21},{6,22},{7,23},{8,24},{9,... | collective-permute-start | bytes 786440 | tf_op jit(solution)/shard_map/ppermute | solution.py:162
  287.2 6.5 %collective-permute-start.10 = (f32[256,256]{1,0:T(8,128)S(1)}, f32[256,256]{1,0:T(8,128)S(1)}, u32[]{:S(2)}, u32[]{:S(2)}) collective-permute-start(f32[256,256]{1,0:T(8,128)S(1)} %add.105), channel_id=1, source_target_pairs={{0,32},{1,33},{2,34},{3,35},{4,36},{5,37},{6,38},{7,39},{8,40},{9,... | collective-permute-start | bytes 786440 | tf_op jit(solution)/shard_map/ppermute | solution.py:162
  293.8 10.6 %collective-permute-start.11 = (f32[256,256]{1,0:T(8,128)S(1)}, f32[256,256]{1,0:T(8,128)S(1)}, u32[]{:S(2)}, u32[]{:S(2)}) collective-permute-start(f32[256,256]{1,0:T(8,128)S(1)} %add.106), channel_id=1, source_target_pairs={{0,64},{1,65},{2,66},{3,67},{4,68},{5,69},{6,70},{7,71},{8,72},{9,... | collective-permute-start | bytes 786440 | tf_op jit(solution)/shard_map/ppermute | solution.py:162
  304.4 7.4 %collective-permute-start.12 = (f32[256,256]{1,0:T(8,128)S(1)}, f32[256,256]{1,0:T(8,128)S(1)}, u32[]{:S(2)}, u32[]{:S(2)}) collective-permute-start(f32[256,256]{1,0:T(8,128)S(1)} %add.107), channel_id=1, source_target_pairs={{0,128},{1,129},{2,130},{3,131},{4,132},{5,133},{6,134},{7,135},{8... | collective-permute-start | bytes 786440 | tf_op jit(solution)/shard_map/ppermute | solution.py:162
Sparse Core Ops, SparseCore 0:
  67.7 71.1 reduce-scatter.2
  159.1 39.4 all-gather.1
  227.5 60.6 reduce-scatter.4

commit v10 on v8

--- a/solution.py
+++ b/solution.py
@@ -145,9 +145,18 @@
     return (hidden, grad_pre)
 
 
-def butterfly_sum(value, axes, count, levels):
+def butterfly_sum(value, axes, count, levels, rings):
+    def partner(i, level):
+        for low_bit, ring_n in rings:
+            if low_bit <= level < low_bit + ring_n.bit_length() - 1:
+                label = [p ^ (p >> 1) for p in range(ring_n)]
+                p = (i >> low_bit) % ring_n
+                q = label.index(label[p] ^ (1 << (level - low_bit)))
+                return i + ((q - p) << low_bit)
+        return i ^ (1 << level)
+
     for level in levels:
-        pairs = [(i, i ^ (1 << level)) for i in range(count)]
+        pairs = [(i, partner(i, level)) for i in range(count)]
         value = value + lax.ppermute(value, axes, pairs)
     return value
 
@@ -228,7 +237,10 @@
     grad_agg = jnp.dot(grad_own, weight.T, preferred_element_type=jnp.float32).astype(jnp.bfloat16)
     every = ("row",) + col_axes
     levels = list(range((row_n * col_n).bit_length() - 1))
-    weight_sum = butterfly_sum(weight_part, every, row_n * col_n, levels)
+    mid_low = (core_n - 1).bit_length()
+    x_n = 4 if row_n % 4 == 0 else row_n
+    rings = ((mid_low, mid_n), ((col_n - 1).bit_length(), x_n))
+    weight_sum = butterfly_sum(weight_part, every, row_n * col_n, levels, rings)
     grad_source = pair_gather(grad_agg, "high")
     grad_source = lax.all_gather(grad_source, "mid", axis=0, tiled=True)
     grad_other = lax.ppermute(grad_source, "core", [(0, 1), (1, 0)])

time: 329 us -> 325 us (0.988); the launches traced: 328 us -> 319 us
  starting transfers between devices: 34.9 us -> 51.5 us
  waiting for transfers between devices: 215 us -> 199 us
  Pallas kernels: 43.3 us -> 34 us
    ppermute x1, starting transfers between devices: 0.09 us -> 14.8 us  [on_device(): lax.ppermute(partial_value[:half], 'core', [(0, 1), (1, 0)])]
    reduce_scatter x1, waiting for transfers between devices: 69.3 us -> 59.2 us  [on_device(): lax.psum_scatter(partial_value, 'mid', scatter_dimension=0, tiled=True)]
    ppermute x8, waiting for transfers between devices: 65.3 us -> 59.7 us  [butterfly_sum(): value = value + lax.ppermute(value, axes, pairs)]
    pallas_call x1, Pallas kernels: 23.3 us -> 18.1 us  [back_pass(): pl.pallas_call(functools.partial(back_kernel, per_block=per_block, scale=...]
    pallas_call x1, Pallas kernels: 19.9 us -> 15.9 us  [slot_pass(): pl.pallas_call(functools.partial(slot_kernel, per_block=per_block, scale=...]
where the time goes in v10:
time: 325 us; the launch traced here: 319 us
  waiting for transfers between devices  199 us (61%)
  starting transfers between devices  51.5 us (16%)
  Pallas kernels  34 us (10%)
  between operations  14.6 us (4%)
  other arithmetic  10.6 us (3%)
  local copies, waits for them, and re-layouts  7.93 us (2%)
    ppermute x8, waiting for transfers between devices, butterfly_sum(): value = value + lax.ppermute(value, axes, pairs)  59.7 us
    reduce_scatter x1, waiting for transfers between devices, on_device(): lax.psum_scatter(partial_value, 'mid', scatter_dimension=0, tiled=True)  59.2 us
    all_gather x1, waiting for transfers between devices, on_device(): grad_source = lax.all_gather(grad_source, 'mid', axis=0, tiled=True)  39.6 us
    ppermute x8, starting transfers between devices, butterfly_sum(): value = value + lax.ppermute(value, axes, pairs)  26.3 us
    pallas_call x1, Pallas kernels, back_pass(): pl.pallas_call(functools.partial(back_kernel, per_block=per_block, scale=...  18.1 us
    ppermute x3, waiting for transfers between devices, doubling_gather(): other = lax.ppermute(value, axis, pairs)  17.8 us
    pallas_call x1, Pallas kernels, slot_pass(): pl.pallas_call(functools.partial(slot_kernel, per_block=per_block, scale=...  15.9 us
    ppermute x1, starting transfers between devices, on_device(): lax.ppermute(partial_value[:half], 'core', [(0, 1), (1, 0)])  14.8 us
  transfers between devices with their start and end apart: 18, of which 17 were waited for; matrix products, arithmetic and copies ran while one was open for 1% of the time, Pallas kernels for 0%

profile of v10, /device:TPU:8, one launch (start us, length us, event | category | flops | bytes accessed | tf_op | source)
XLA Modules:
  0.0 319.2 jit_solution(14975538499138798017)
XLA Ops:
  7.2 1.6 collective-permute-start
  8.8 4.0 %collective-permute-done = bf16[256,256]{1,0:T(8,128)(2,1)S(1)} collective-permute-done((bf16[256,256]{1,0:T(8,128)(2,1)}, bf16[256,256]{1,0:T(8,128)(2,1)S(1)}, u32[]{:S(2)}, u32[]{:S(2)}) %collective-permute-start) | collective-permute-done | bytes 131104 | tf_op jit(solution)/shard_map/ppermute | solution.py:168
  13.7 3.1 collective-permute-start.1
  16.8 5.7 %collective-permute-done.1 = bf16[512,256]{1,0:T(8,128)(2,1)S(1)} collective-permute-done((bf16[512,256]{1,0:T(8,128)(2,1)S(1)}, bf16[512,256]{1,0:T(8,128)(2,1)S(1)}, u32[]{:S(2)}, u32[]{:S(2)}) %collective-permute-start.1) | collective-permute-done | bytes 262176 | tf_op jit(solution)/shard_map/ppermute | solution.py:168
  26.6 8.1 %collective-permute-done.2 = bf16[1024,256]{1,0:T(8,128)(2,1)S(1)} collective-permute-done((bf16[1024,256]{1,0:T(8,128)(2,1)S(1)}, bf16[1024,256]{1,0:T(8,128)(2,1)S(1)}, u32[]{:S(2)}, u32[]{:S(2)}) %collective-permute-start.2) | collective-permute-done | bytes 524320 | tf_op jit(solution)/shard_map/ppermute | solution.py:168
  35.0 15.9 %shard_map.94 = f32[64,128,256]{2,1,0:T(8,128)} custom-call(s32[1]{0:T(128)} %bitcast.17.live_ref, s32[176]{0:T(256)S(1)} %multiply_add_fusion.rows_ref, s32[176]{0:T(256)S(1)} %bitcast.21, s32[176,128,128]{2,1,0:T(8,128)} %bitcast.23, bf16[16,128,256]{2,1,0:T(8,128)(2,1)S(1)} %bitcast.19), custom_call_target="tpu_custom_call" | custom-call | tf_op jit(solution)/shard_map/pallas_call | solution.py:96
  50.9 4.0 %fusion.7 = (f32[32,128,256]{2,1,0:T(8,128)S(1)}, f32[32,128,256]{2,1,0:T(8,128)S(1)}) fusion(f32[64,128,256]{2,1,0:T(8,128)} %shard_map.94), kind=kLoop, calls=%fused_computation.53 | loop fusion | bytes 16777216 | tf_op jit(solution)/shard_map/slice | solution.py:227
  54.9 14.8 %collective-permute-start.3 = (f32[4096,256]{1,0:T(8,128)S(1)}, f32[4096,256]{1,0:T(8,128)S(1)}, u32[]{:S(2)}, u32[]{:S(2)}) collective-permute-start(f32[4096,256]{1,0:T(8,128)S(1)} %bitcast.25), channel_id=1, source_target_pairs={{0,1},{1,0},{2,3},{3,2},{4,5},{5,4},{6,7},{7,6},{8,9},{9,8},{10,11... | collective-permute-start | bytes 12582920 | tf_op jit(solution)/shard_map/ppermute | solution.py:227
  69.7 6.8 %collective-permute-done.3 = f32[4096,256]{1,0:T(8,128)S(1)} collective-permute-done((f32[4096,256]{1,0:T(8,128)S(1)}, f32[4096,256]{1,0:T(8,128)S(1)}, u32[]{:S(2)}, u32[]{:S(2)}) %collective-permute-start.3) | collective-permute-done | bytes 4194336 | tf_op jit(solution)/shard_map/ppermute | solution.py:227
  76.5 2.8 bitcast_add_fusion
  79.4 59.2 %reduce-scatter.3.cloned.1.call-done = f32[512,256]{1,0:T(8,128)} async-done(((f32[4096,256]{1,0:T(8,128)}), f32[512,256]{1,0:T(8,128)}) %reduce-scatter.3.cloned.1.call-update) | async-done | bytes 524304 | tf_op jit(solution)/shard_map/reduce_scatter | solution.py:230
  139.6 2.2 collective-permute-start.4
  141.8 7.4 %collective-permute-done.4 = f32[256,256]{1,0:T(8,128)S(1)} collective-permute-done((f32[256,256]{1,0:T(8,128)S(1)}, f32[256,256]{1,0:T(8,128)S(1)}, u32[]{:S(2)}, u32[]{:S(2)}) %collective-permute-start.4) | collective-permute-done | bytes 262176 | tf_op jit(solution)/shard_map/ppermute | solution.py:181
  151.3 2.2 collective-permute-start.13
  153.6 4.4 %collective-permute-done.13 = bf16[256,256]{1,0:T(8,128)(2,1)S(1)} collective-permute-done((bf16[256,256]{1,0:T(8,128)(2,1)S(1)}, bf16[256,256]{1,0:T(8,128)(2,1)S(1)}, u32[]{:S(2)}, u32[]{:S(2)}) %collective-permute-start.13) | collective-permute-done | bytes 131104 | tf_op jit(solution)/shard_map/ppermute | solution.py:186
  158.7 39.6 %all-gather.2.cloned.1.call-done = bf16[4096,256]{1,0:T(8,128)(2,1)} async-done(((bf16[512,256]{1,0:T(8,128)(2,1)}), bf16[4096,256]{1,0:T(8,128)(2,1)}) %all-gather.2.cloned.1.call-update) | async-done | bytes 2097168 | tf_op jit(solution)/shard_map/all_gather | solution.py:245
  198.3 4.4 %collective-permute-done.14 = bf16[4096,256]{1,0:T(8,128)(2,1)S(1)} collective-permute-done((bf16[4096,256]{1,0:T(8,128)(2,1)}, bf16[4096,256]{1,0:T(8,128)(2,1)S(1)}, u32[]{:S(2)}, u32[]{:S(2)}) %collective-permute-start.14) | collective-permute-done | bytes 2097184 | tf_op jit(solution)/shard_map/ppermute | solution.py:246
  202.7 1.3 copy-done.3
  204.0 1.6 copy-done.1
  205.6 18.1 %shard_map.95 = f32[16,128,256]{2,1,0:T(8,128)} custom-call(s32[1]{0:T(128)} %bitcast.18.live_ref, s32[176]{0:T(256)S(1)} %get-tuple-element.5.rows_ref, s32[176]{0:T(256)S(1)} %bitcast.22, s32[176]{0:T(256)S(1)} %get-tuple-element.3.halves_ref, s32[176,128,128]{2,1,0:T(8,128)} %bitcast.24, bf16[32,128,256]{2,1,0:T(8,128)(2,1)S(1)} %bitcast.20, ...), custom_call_target="tpu_custom_call" | custom-call | tf_op jit(solution)/shard_map/pallas_call | solution.py:128
  224.0 22.5 %collective-permute-start.5 = (f32[256,256]{1,0:T(8,128)S(1)}, f32[256,256]{1,0:T(8,128)S(1)}, u32[]{:S(2)}, u32[]{:S(2)}) collective-permute-start(f32[256,256]{1,0:T(8,128)S(1)} %fusion.8), channel_id=1, source_target_pairs={{0,1},{1,0},{2,3},{3,2},{4,5},{5,4},{6,7},{7,6},{8,9},{9,8},{10,11... | collective-permute-start | bytes 786440 | tf_op jit(solution)/shard_map/ppermute | solution.py:160
  246.5 1.2 collective-permute-done.5
  247.8 8.6 %collective-permute-done.6 = f32[256,256]{1,0:T(8,128)S(1)} collective-permute-done((f32[256,256]{1,0:T(8,128)S(1)}, f32[256,256]{1,0:T(8,128)S(1)}, u32[]{:S(2)}, u32[]{:S(2)}) %collective-permute-start.6) | collective-permute-done | bytes 262176 | tf_op jit(solution)/shard_map/ppermute | solution.py:160
  256.7 9.6 %collective-permute-done.7 = f32[256,256]{1,0:T(8,128)S(1)} collective-permute-done((f32[256,256]{1,0:T(8,128)S(1)}, f32[256,256]{1,0:T(8,128)S(1)}, u32[]{:S(2)}, u32[]{:S(2)}) %collective-permute-start.7) | collective-permute-done | bytes 262176 | tf_op jit(solution)/shard_map/ppermute | solution.py:160
  266.3 1.2 collective-permute-start.8
  267.5 12.7 %collective-permute-done.8 = f32[256,256]{1,0:T(8,128)S(1)} collective-permute-done((f32[256,256]{1,0:T(8,128)S(1)}, f32[256,256]{1,0:T(8,128)S(1)}, u32[]{:S(2)}, u32[]{:S(2)}) %collective-permute-start.8) | collective-permute-done | bytes 262176 | tf_op jit(solution)/shard_map/ppermute | solution.py:160
  280.3 9.3 %collective-permute-done.9 = f32[256,256]{1,0:T(8,128)S(1)} collective-permute-done((f32[256,256]{1,0:T(8,128)S(1)}, f32[256,256]{1,0:T(8,128)S(1)}, u32[]{:S(2)}, u32[]{:S(2)}) %collective-permute-start.9) | collective-permute-done | bytes 262176 | tf_op jit(solution)/shard_map/ppermute | solution.py:160
  289.7 6.4 %collective-permute-done.10 = f32[256,256]{1,0:T(8,128)S(1)} collective-permute-done((f32[256,256]{1,0:T(8,128)S(1)}, f32[256,256]{1,0:T(8,128)S(1)}, u32[]{:S(2)}, u32[]{:S(2)}) %collective-permute-start.10) | collective-permute-done | bytes 262176 | tf_op jit(solution)/shard_map/ppermute | solution.py:160
  296.1 2.0 collective-permute-start.11
  298.1 5.7 %collective-permute-done.11 = f32[256,256]{1,0:T(8,128)S(1)} collective-permute-done((f32[256,256]{1,0:T(8,128)S(1)}, f32[256,256]{1,0:T(8,128)S(1)}, u32[]{:S(2)}, u32[]{:S(2)}) %collective-permute-start.11) | collective-permute-done | bytes 262176 | tf_op jit(solution)/shard_map/ppermute | solution.py:160
  303.9 6.4 %collective-permute-done.12 = f32[256,256]{1,0:T(8,128)S(1)} collective-permute-done((f32[256,256]{1,0:T(8,128)S(1)}, f32[256,256]{1,0:T(8,128)S(1)}, u32[]{:S(2)}, u32[]{:S(2)}) %collective-permute-start.12) | collective-permute-done | bytes 262176 | tf_op jit(solution)/shard_map/ppermute | solution.py:160
  311.0 1.6 convert_element_type.28
  (46 shorter events, 10.5 us)
Async XLA Ops:
  7.2 143.0 %copy-start = (bf16[256,256]{1,0:T(8,128)(2,1)S(1)}, bf16[256,256]{1,0:T(8,128)(2,1)}, u32[]{:S(2)}) copy-start(bf16[256,256]{1,0:T(8,128)(2,1)} %param.8) | copy-start | bytes 393220
  7.2 27.8 %copy-start.2 = (s32[1,1,176]{2,1,0:T(1,128)S(1)}, s32[1,1,176]{2,1,0:T(1,128)}, u32[]{:S(2)}) copy-start(s32[1,1,176]{2,1,0:T(1,128)} %param.11) | copy-start | bytes 2116
  7.2 131.4 %reduce-scatter.3.cloned.1.call-start = ((), (), s32[]{:S(2)}) async-start(), calls=%async_computation.2 | async-start | bytes 4718592 | tf_op jit(solution)/shard_map/reduce_scatter | solution.py:230
  7.2 5.5 %collective-permute-start = (bf16[256,256]{1,0:T(8,128)(2,1)}, bf16[256,256]{1,0:T(8,128)(2,1)S(1)}, u32[]{:S(2)}, u32[]{:S(2)}) collective-permute-start(bf16[256,256]{1,0:T(8,128)(2,1)} %param.7), channel_id=1, source_target_pairs={{0,32},{32,0},{64,96},{96,64},{128,160},{160,128},{192,224},{224,1... | collective-permute-start | bytes 393224 | tf_op jit(solution)/shard_map/ppermute | solution.py:168
  13.7 8.8 %collective-permute-start.1 = (bf16[512,256]{1,0:T(8,128)(2,1)S(1)}, bf16[512,256]{1,0:T(8,128)(2,1)S(1)}, u32[]{:S(2)}, u32[]{:S(2)}) collective-permute-start(bf16[512,256]{1,0:T(8,128)(2,1)S(1)} %pad_maximum_fusion.2), channel_id=1, source_target_pairs={{0,64},{32,96},{64,0},{96,32},{128,192},{160,224},{192,128},{224,1... | collective-permute-start | bytes 786440 | tf_op jit(solution)/shard_map/ppermute | solution.py:168
  22.7 12.0 %collective-permute-start.2 = (bf16[1024,256]{1,0:T(8,128)(2,1)S(1)}, bf16[1024,256]{1,0:T(8,128)(2,1)S(1)}, u32[]{:S(2)}, u32[]{:S(2)}) collective-permute-start(bf16[1024,256]{1,0:T(8,128)(2,1)S(1)} %pad_maximum_fusion.1), channel_id=1, source_target_pairs={{0,128},{32,160},{64,192},{96,224},{128,0},{160,32},{192,64},{224,... | collective-permute-start | bytes 1572872 | tf_op jit(solution)/shard_map/ppermute | solution.py:168
  54.9 21.6 %collective-permute-start.3 = (f32[4096,256]{1,0:T(8,128)S(1)}, f32[4096,256]{1,0:T(8,128)S(1)}, u32[]{:S(2)}, u32[]{:S(2)}) collective-permute-start(f32[4096,256]{1,0:T(8,128)S(1)} %bitcast.25), channel_id=1, source_target_pairs={{0,1},{1,0},{2,3},{3,2},{4,5},{5,4},{6,7},{7,6},{8,9},{9,8},{10,11... | collective-permute-start | bytes 12582920 | tf_op jit(solution)/shard_map/ppermute | solution.py:227
  79.3 70.9 %copy-start.4 = (bf16[256,256]{1,0:T(8,128)(2,1)S(1)}, bf16[256,256]{1,0:T(8,128)(2,1)}, u32[]{:S(2)}) copy-start(bf16[256,256]{1,0:T(8,128)(2,1)} %param.9) | copy-start | bytes 393220
  79.3 119.0 %all-gather.2.cloned.1.call-start = ((), (), s32[]{:S(2)}) async-start(), calls=%async_computation.3 | async-start | bytes 2359296 | tf_op jit(solution)/shard_map/all_gather | solution.py:245
  139.6 9.6 %collective-permute-start.4 = (f32[256,256]{1,0:T(8,128)S(1)}, f32[256,256]{1,0:T(8,128)S(1)}, u32[]{:S(2)}, u32[]{:S(2)}) collective-permute-start(f32[256,256]{1,0:T(8,128)S(1)} %constant_dynamic-slice_fusion), channel_id=1, source_target_pairs={{0,16},{16,0},{1,17},{17,1},{2,18},{18,2},{3,19},{19,3},{4,20},{20... | collective-permute-start | bytes 786440 | tf_op jit(solution)/shard_map/ppermute | solution.py:181
  151.3 6.6 %collective-permute-start.13 = (bf16[256,256]{1,0:T(8,128)(2,1)S(1)}, bf16[256,256]{1,0:T(8,128)(2,1)S(1)}, u32[]{:S(2)}, u32[]{:S(2)}) collective-permute-start(bf16[256,256]{1,0:T(8,128)(2,1)S(1)} %convolution_convert_fusion), channel_id=1, source_target_pairs={{0,16},{16,0},{1,17},{17,1},{2,18},{18,2},{3,19},{19,3},{4,20},{20... | collective-permute-start | bytes 393224 | tf_op jit(solution)/shard_map/ppermute | solution.py:186
  158.7 152.4 %reduce-scatter.5.cloned.1.call-start = ((), (), s32[]{:S(2)}) async-start(), calls=%async_computation.4 | async-start | bytes 2359296 | tf_op jit(solution)/shard_map/reduce_scatter | solution.py:256
  198.3 4.4 %collective-permute-start.14 = (bf16[4096,256]{1,0:T(8,128)(2,1)}, bf16[4096,256]{1,0:T(8,128)(2,1)S(1)}, u32[]{:S(2)}, u32[]{:S(2)}) collective-permute-start(bf16[4096,256]{1,0:T(8,128)(2,1)} %all-gather.2.cloned.1.call-done), channel_id=1, source_target_pairs={{0,1},{1,0},{2,3},{3,2},{4,5},{5,4},{6,7},{7,6},{8,9},{9,8},{10,11... | collective-permute-start | bytes 6291464 | tf_op jit(solution)/shard_map/ppermute | solution.py:246
  202.7 1.3 copy-start.3
  204.0 1.6 copy-start.1
  224.0 23.6 %collective-permute-start.5 = (f32[256,256]{1,0:T(8,128)S(1)}, f32[256,256]{1,0:T(8,128)S(1)}, u32[]{:S(2)}, u32[]{:S(2)}) collective-permute-start(f32[256,256]{1,0:T(8,128)S(1)} %fusion.8), channel_id=1, source_target_pairs={{0,1},{1,0},{2,3},{3,2},{4,5},{5,4},{6,7},{7,6},{8,9},{9,8},{10,11... | collective-permute-start | bytes 786440 | tf_op jit(solution)/shard_map/ppermute | solution.py:160
  247.7 8.7 %collective-permute-start.6 = (f32[256,256]{1,0:T(8,128)S(1)}, f32[256,256]{1,0:T(8,128)S(1)}, u32[]{:S(2)}, u32[]{:S(2)}) collective-permute-start(f32[256,256]{1,0:T(8,128)S(1)} %add.101), channel_id=1, source_target_pairs={{0,2},{1,3},{2,0},{3,1},{4,6},{5,7},{6,4},{7,5},{8,10},{9,11},{10,... | collective-permute-start | bytes 786440 | tf_op jit(solution)/shard_map/ppermute | solution.py:160
  256.4 9.9 %collective-permute-start.7 = (f32[256,256]{1,0:T(8,128)S(1)}, f32[256,256]{1,0:T(8,128)S(1)}, u32[]{:S(2)}, u32[]{:S(2)}) collective-permute-start(f32[256,256]{1,0:T(8,128)S(1)} %add.102), channel_id=1, source_target_pairs={{0,6},{1,7},{2,4},{3,5},{4,2},{5,3},{6,0},{7,1},{8,14},{9,15},{10,... | collective-permute-start | bytes 786440 | tf_op jit(solution)/shard_map/ppermute | solution.py:160
  266.3 13.9 %collective-permute-start.8 = (f32[256,256]{1,0:T(8,128)S(1)}, f32[256,256]{1,0:T(8,128)S(1)}, u32[]{:S(2)}, u32[]{:S(2)}) collective-permute-start(f32[256,256]{1,0:T(8,128)S(1)} %add.103), channel_id=1, source_target_pairs={{0,14},{1,15},{2,12},{3,13},{4,10},{5,11},{6,8},{7,9},{8,6},{9,7},... | collective-permute-start | bytes 786440 | tf_op jit(solution)/shard_map/ppermute | solution.py:160
  280.2 9.4 %collective-permute-start.9 = (f32[256,256]{1,0:T(8,128)S(1)}, f32[256,256]{1,0:T(8,128)S(1)}, u32[]{:S(2)}, u32[]{:S(2)}) collective-permute-start(f32[256,256]{1,0:T(8,128)S(1)} %add.104), channel_id=1, source_target_pairs={{0,16},{1,17},{2,18},{3,19},{4,20},{5,21},{6,22},{7,23},{8,24},{9,... | collective-permute-start | bytes 786440 | tf_op jit(solution)/shard_map/ppermute | solution.py:160
  289.6 6.5 %collective-permute-start.10 = (f32[256,256]{1,0:T(8,128)S(1)}, f32[256,256]{1,0:T(8,128)S(1)}, u32[]{:S(2)}, u32[]{:S(2)}) collective-permute-start(f32[256,256]{1,0:T(8,128)S(1)} %add.105), channel_id=1, source_target_pairs={{0,32},{1,33},{2,34},{3,35},{4,36},{5,37},{6,38},{7,39},{8,40},{9,... | collective-permute-start | bytes 786440 | tf_op jit(solution)/shard_map/ppermute | solution.py:160
  296.1 7.7 %collective-permute-start.11 = (f32[256,256]{1,0:T(8,128)S(1)}, f32[256,256]{1,0:T(8,128)S(1)}, u32[]{:S(2)}, u32[]{:S(2)}) collective-permute-start(f32[256,256]{1,0:T(8,128)S(1)} %add.106), channel_id=1, source_target_pairs={{0,96},{1,97},{2,98},{3,99},{4,100},{5,101},{6,102},{7,103},{8,104... | collective-permute-start | bytes 786440 | tf_op jit(solution)/shard_map/ppermute | solution.py:160
  303.8 6.5 %collective-permute-start.12 = (f32[256,256]{1,0:T(8,128)S(1)}, f32[256,256]{1,0:T(8,128)S(1)}, u32[]{:S(2)}, u32[]{:S(2)}) collective-permute-start(f32[256,256]{1,0:T(8,128)S(1)} %add.107), channel_id=1, source_target_pairs={{0,128},{1,129},{2,130},{3,131},{4,132},{5,133},{6,134},{7,135},{8... | collective-permute-start | bytes 786440 | tf_op jit(solution)/shard_map/ppermute | solution.py:160
Sparse Core Ops, SparseCore 0:
  79.4 59.1 reduce-scatter.2
  158.8 39.4 all-gather.1
  223.9 64.7 reduce-scatter.4

commit v11 on v9

--- a/solution.py
+++ b/solution.py
@@ -238,7 +238,9 @@
     )
     grad_agg = jnp.dot(grad_own, weight.T, preferred_element_type=jnp.float32).astype(jnp.bfloat16)
     every = ("row",) + col_axes
-    levels = list(range((row_n * col_n).bit_length() - 1))
+    high_level = (core_n * mid_n - 1).bit_length()
+    levels = [level for level in range((row_n * col_n).bit_length() - 1) if level != high_level]
+    levels = levels + [high_level]
     weight_sum = butterfly_sum(
         weight_part, every, row_n * col_n, levels, ((core_n - 1).bit_length(), mid_n)
     )

time: 325 us -> 324 us (level)
  no operation moved by 1% of the time
where the time goes in v11:
time: 324 us; the launch traced here: 321 us
  waiting for transfers between devices  202 us (62%)
  starting transfers between devices  44.1 us (14%)
  Pallas kernels  40.9 us (13%)
  between operations  14.6 us (5%)
  other arithmetic  10.6 us (3%)
  local copies, waits for them, and re-layouts  7.93 us (2%)
    reduce_scatter x1, waiting for transfers between devices, on_device(): lax.psum_scatter(partial_value, 'mid', scatter_dimension=0, tiled=True)  71.8 us
    ppermute x8, waiting for transfers between devices, butterfly_sum(): value = value + lax.ppermute(value, axes, pairs)  49.6 us
    all_gather x1, waiting for transfers between devices, on_device(): grad_source = lax.all_gather(grad_source, 'mid', axis=0, tiled=True)  39.6 us
    ppermute x8, starting transfers between devices, butterfly_sum(): value = value + lax.ppermute(value, axes, pairs)  33.6 us
    pallas_call x1, Pallas kernels, back_pass(): pl.pallas_call(functools.partial(back_kernel, per_block=per_block, scale=...  22 us
    pallas_call x1, Pallas kernels, slot_pass(): pl.pallas_call(functools.partial(slot_kernel, per_block=per_block, scale=...  18.9 us
    ppermute x3, waiting for transfers between devices, doubling_gather(): other = lax.ppermute(value, axis, pairs)  17.8 us
    ppermute x1, waiting for transfers between devices, pair_scatter(): return keep + lax.ppermute(send, axis, [(0, 1), (1, 0)])  7.39 us
  transfers between devices with their start and end apart: 18, of which 17 were waited for; matrix products, arithmetic and copies ran while one was open for 1% of the time, Pallas kernels for 0%

profile of v11, /device:TPU:8, one launch (start us, length us, event | category | flops | bytes accessed | tf_op | source)
XLA Modules:
  0.0 321.5 jit_solution(11106434366907504953)
XLA Ops:
  7.2 1.6 collective-permute-start
  8.8 4.0 %collective-permute-done = bf16[256,256]{1,0:T(8,128)(2,1)S(1)} collective-permute-done((bf16[256,256]{1,0:T(8,128)(2,1)}, bf16[256,256]{1,0:T(8,128)(2,1)S(1)}, u32[]{:S(2)}, u32[]{:S(2)}) %collective-permute-start) | collective-permute-done | bytes 131104 | tf_op jit(solution)/shard_map/ppermute | solution.py:170
  13.7 3.1 collective-permute-start.1
  16.8 5.7 %collective-permute-done.1 = bf16[512,256]{1,0:T(8,128)(2,1)S(1)} collective-permute-done((bf16[512,256]{1,0:T(8,128)(2,1)S(1)}, bf16[512,256]{1,0:T(8,128)(2,1)S(1)}, u32[]{:S(2)}, u32[]{:S(2)}) %collective-permute-start.1) | collective-permute-done | bytes 262176 | tf_op jit(solution)/shard_map/ppermute | solution.py:170
  26.6 8.1 %collective-permute-done.2 = bf16[1024,256]{1,0:T(8,128)(2,1)S(1)} collective-permute-done((bf16[1024,256]{1,0:T(8,128)(2,1)S(1)}, bf16[1024,256]{1,0:T(8,128)(2,1)S(1)}, u32[]{:S(2)}, u32[]{:S(2)}) %collective-permute-start.2) | collective-permute-done | bytes 524320 | tf_op jit(solution)/shard_map/ppermute | solution.py:170
  35.0 18.9 %shard_map.94 = f32[64,128,256]{2,1,0:T(8,128)} custom-call(s32[1]{0:T(128)} %bitcast.17.live_ref, s32[176]{0:T(256)S(1)} %multiply_add_fusion.rows_ref, s32[176]{0:T(256)S(1)} %bitcast.21, s32[176,128,128]{2,1,0:T(8,128)} %bitcast.23, bf16[16,128,256]{2,1,0:T(8,128)(2,1)S(1)} %bitcast.19), custom_call_target="tpu_custom_call" | custom-call | tf_op jit(solution)/shard_map/pallas_call | solution.py:96
  53.9 4.0 %fusion.7 = (f32[32,128,256]{2,1,0:T(8,128)S(1)}, f32[32,128,256]{2,1,0:T(8,128)S(1)}) fusion(f32[64,128,256]{2,1,0:T(8,128)} %shard_map.94), kind=kLoop, calls=%fused_computation.53 | loop fusion | bytes 16777216 | tf_op jit(solution)/shard_map/slice | solution.py:229
  58.0 7.1 %collective-permute-done.3 = f32[4096,256]{1,0:T(8,128)S(1)} collective-permute-done((f32[4096,256]{1,0:T(8,128)S(1)}, f32[4096,256]{1,0:T(8,128)S(1)}, u32[]{:S(2)}, u32[]{:S(2)}) %collective-permute-start.3) | collective-permute-done | bytes 4194336 | tf_op jit(solution)/shard_map/ppermute | solution.py:229
  65.2 2.8 bitcast_add_fusion
  68.0 71.8 %reduce-scatter.3.cloned.1.call-done = f32[512,256]{1,0:T(8,128)} async-done(((f32[4096,256]{1,0:T(8,128)}), f32[512,256]{1,0:T(8,128)}) %reduce-scatter.3.cloned.1.call-update) | async-done | bytes 524304 | tf_op jit(solution)/shard_map/reduce_scatter | solution.py:232
  140.9 2.2 collective-permute-start.4
  143.1 7.4 %collective-permute-done.4 = f32[256,256]{1,0:T(8,128)S(1)} collective-permute-done((f32[256,256]{1,0:T(8,128)S(1)}, f32[256,256]{1,0:T(8,128)S(1)}, u32[]{:S(2)}, u32[]{:S(2)}) %collective-permute-start.4) | collective-permute-done | bytes 262176 | tf_op jit(solution)/shard_map/ppermute | solution.py:183
  152.6 2.2 collective-permute-start.13
  154.8 4.4 %collective-permute-done.13 = bf16[256,256]{1,0:T(8,128)(2,1)S(1)} collective-permute-done((bf16[256,256]{1,0:T(8,128)(2,1)S(1)}, bf16[256,256]{1,0:T(8,128)(2,1)S(1)}, u32[]{:S(2)}, u32[]{:S(2)}) %collective-permute-start.13) | collective-permute-done | bytes 131104 | tf_op jit(solution)/shard_map/ppermute | solution.py:188
  160.0 39.6 %all-gather.2.cloned.1.call-done = bf16[4096,256]{1,0:T(8,128)(2,1)} async-done(((bf16[512,256]{1,0:T(8,128)(2,1)}), bf16[4096,256]{1,0:T(8,128)(2,1)}) %all-gather.2.cloned.1.call-update) | async-done | bytes 2097168 | tf_op jit(solution)/shard_map/all_gather | solution.py:248
  199.6 4.4 %collective-permute-done.14 = bf16[4096,256]{1,0:T(8,128)(2,1)S(1)} collective-permute-done((bf16[4096,256]{1,0:T(8,128)(2,1)}, bf16[4096,256]{1,0:T(8,128)(2,1)S(1)}, u32[]{:S(2)}, u32[]{:S(2)}) %collective-permute-start.14) | collective-permute-done | bytes 2097184 | tf_op jit(solution)/shard_map/ppermute | solution.py:249
  205.3 1.6 copy-done.1
  206.9 22.0 %shard_map.95 = f32[16,128,256]{2,1,0:T(8,128)} custom-call(s32[1]{0:T(128)} %bitcast.18.live_ref, s32[176]{0:T(256)S(1)} %get-tuple-element.5.rows_ref, s32[176]{0:T(256)S(1)} %bitcast.22, s32[176]{0:T(256)S(1)} %get-tuple-element.3.halves_ref, s32[176,128,128]{2,1,0:T(8,128)} %bitcast.24, bf16[32,128,256]{2,1,0:T(8,128)(2,1)S(1)} %bitcast.20, ...), custom_call_target="tpu_custom_call" | custom-call | tf_op jit(solution)/shard_map/pallas_call | solution.py:128
  229.2 1.5 collective-permute-done.5
  230.8 1.5 collective-permute-start.6
  232.3 6.9 %collective-permute-done.6 = f32[256,256]{1,0:T(8,128)S(1)} collective-permute-done((f32[256,256]{1,0:T(8,128)S(1)}, f32[256,256]{1,0:T(8,128)S(1)}, u32[]{:S(2)}, u32[]{:S(2)}) %collective-permute-start.6) | collective-permute-done | bytes 262176 | tf_op jit(solution)/shard_map/ppermute | solution.py:162
  239.3 19.6 %collective-permute-start.7 = (f32[256,256]{1,0:T(8,128)S(1)}, f32[256,256]{1,0:T(8,128)S(1)}, u32[]{:S(2)}, u32[]{:S(2)}) collective-permute-start(f32[256,256]{1,0:T(8,128)S(1)} %add.102), channel_id=1, source_target_pairs={{0,6},{1,7},{2,4},{3,5},{4,2},{5,3},{6,0},{7,1},{8,14},{9,15},{10,... | collective-permute-start | bytes 786440 | tf_op jit(solution)/shard_map/ppermute | solution.py:162
  258.9 6.1 %collective-permute-done.7 = f32[256,256]{1,0:T(8,128)S(1)} collective-permute-done((f32[256,256]{1,0:T(8,128)S(1)}, f32[256,256]{1,0:T(8,128)S(1)}, u32[]{:S(2)}, u32[]{:S(2)}) %collective-permute-start.7) | collective-permute-done | bytes 262176 | tf_op jit(solution)/shard_map/ppermute | solution.py:162
  265.1 8.4 %collective-permute-done.8 = f32[256,256]{1,0:T(8,128)S(1)} collective-permute-done((f32[256,256]{1,0:T(8,128)S(1)}, f32[256,256]{1,0:T(8,128)S(1)}, u32[]{:S(2)}, u32[]{:S(2)}) %collective-permute-start.8) | collective-permute-done | bytes 262176 | tf_op jit(solution)/shard_map/ppermute | solution.py:162
  273.6 12.4 %collective-permute-done.9 = f32[256,256]{1,0:T(8,128)S(1)} collective-permute-done((f32[256,256]{1,0:T(8,128)S(1)}, f32[256,256]{1,0:T(8,128)S(1)}, u32[]{:S(2)}, u32[]{:S(2)}) %collective-permute-start.9) | collective-permute-done | bytes 262176 | tf_op jit(solution)/shard_map/ppermute | solution.py:162
  286.1 3.0 collective-permute-start.10
  289.0 5.5 %collective-permute-done.10 = f32[256,256]{1,0:T(8,128)S(1)} collective-permute-done((f32[256,256]{1,0:T(8,128)S(1)}, f32[256,256]{1,0:T(8,128)S(1)}, u32[]{:S(2)}, u32[]{:S(2)}) %collective-permute-start.10) | collective-permute-done | bytes 262176 | tf_op jit(solution)/shard_map/ppermute | solution.py:162
  294.6 3.1 collective-permute-start.11
  297.7 4.4 %collective-permute-done.11 = f32[256,256]{1,0:T(8,128)S(1)} collective-permute-done((f32[256,256]{1,0:T(8,128)S(1)}, f32[256,256]{1,0:T(8,128)S(1)}, u32[]{:S(2)}, u32[]{:S(2)}) %collective-permute-start.11) | collective-permute-done | bytes 262176 | tf_op jit(solution)/shard_map/ppermute | solution.py:162
  302.1 6.2 %collective-permute-start.12 = (f32[256,256]{1,0:T(8,128)S(1)}, f32[256,256]{1,0:T(8,128)S(1)}, u32[]{:S(2)}, u32[]{:S(2)}) collective-permute-start(f32[256,256]{1,0:T(8,128)S(1)} %add.107), channel_id=1, source_target_pairs={{0,16},{1,17},{2,18},{3,19},{4,20},{5,21},{6,22},{7,23},{8,24},{9,... | collective-permute-start | bytes 786440 | tf_op jit(solution)/shard_map/ppermute | solution.py:162
  308.2 4.4 %collective-permute-done.12 = f32[256,256]{1,0:T(8,128)S(1)} collective-permute-done((f32[256,256]{1,0:T(8,128)S(1)}, f32[256,256]{1,0:T(8,128)S(1)}, u32[]{:S(2)}, u32[]{:S(2)}) %collective-permute-start.12) | collective-permute-done | bytes 262176 | tf_op jit(solution)/shard_map/ppermute | solution.py:162
  313.3 1.6 convert_element_type.28
  (46 shorter events, 11.6 us)
Async XLA Ops:
  7.2 144.3 %copy-start = (bf16[256,256]{1,0:T(8,128)(2,1)S(1)}, bf16[256,256]{1,0:T(8,128)(2,1)}, u32[]{:S(2)}) copy-start(bf16[256,256]{1,0:T(8,128)(2,1)} %param.8) | copy-start | bytes 393220
  7.2 27.8 %copy-start.2 = (s32[1,1,176]{2,1,0:T(1,128)S(1)}, s32[1,1,176]{2,1,0:T(1,128)}, u32[]{:S(2)}) copy-start(s32[1,1,176]{2,1,0:T(1,128)} %param.11) | copy-start | bytes 2116
  7.2 132.7 %reduce-scatter.3.cloned.1.call-start = ((), (), s32[]{:S(2)}) async-start(), calls=%async_computation.2 | async-start | bytes 4718592 | tf_op jit(solution)/shard_map/reduce_scatter | solution.py:232
  7.2 5.5 %collective-permute-start = (bf16[256,256]{1,0:T(8,128)(2,1)}, bf16[256,256]{1,0:T(8,128)(2,1)S(1)}, u32[]{:S(2)}, u32[]{:S(2)}) collective-permute-start(bf16[256,256]{1,0:T(8,128)(2,1)} %param.7), channel_id=1, source_target_pairs={{0,32},{32,0},{64,96},{96,64},{128,160},{160,128},{192,224},{224,1... | collective-permute-start | bytes 393224 | tf_op jit(solution)/shard_map/ppermute | solution.py:170
  13.7 8.8 %collective-permute-start.1 = (bf16[512,256]{1,0:T(8,128)(2,1)S(1)}, bf16[512,256]{1,0:T(8,128)(2,1)S(1)}, u32[]{:S(2)}, u32[]{:S(2)}) collective-permute-start(bf16[512,256]{1,0:T(8,128)(2,1)S(1)} %pad_maximum_fusion.2), channel_id=1, source_target_pairs={{0,64},{32,96},{64,0},{96,32},{128,192},{160,224},{192,128},{224,1... | collective-permute-start | bytes 786440 | tf_op jit(solution)/shard_map/ppermute | solution.py:170
  22.7 12.0 %collective-permute-start.2 = (bf16[1024,256]{1,0:T(8,128)(2,1)S(1)}, bf16[1024,256]{1,0:T(8,128)(2,1)S(1)}, u32[]{:S(2)}, u32[]{:S(2)}) collective-permute-start(bf16[1024,256]{1,0:T(8,128)(2,1)S(1)} %pad_maximum_fusion.1), channel_id=1, source_target_pairs={{0,128},{32,160},{64,192},{96,224},{128,0},{160,32},{192,64},{224,... | collective-permute-start | bytes 1572872 | tf_op jit(solution)/shard_map/ppermute | solution.py:170
  57.9 7.2 %collective-permute-start.3 = (f32[4096,256]{1,0:T(8,128)S(1)}, f32[4096,256]{1,0:T(8,128)S(1)}, u32[]{:S(2)}, u32[]{:S(2)}) collective-permute-start(f32[4096,256]{1,0:T(8,128)S(1)} %bitcast.25), channel_id=1, source_target_pairs={{0,1},{1,0},{2,3},{3,2},{4,5},{5,4},{6,7},{7,6},{8,9},{9,8},{10,11... | collective-permute-start | bytes 12582920 | tf_op jit(solution)/shard_map/ppermute | solution.py:229
  68.0 83.5 %copy-start.4 = (bf16[256,256]{1,0:T(8,128)(2,1)S(1)}, bf16[256,256]{1,0:T(8,128)(2,1)}, u32[]{:S(2)}) copy-start(bf16[256,256]{1,0:T(8,128)(2,1)} %param.9) | copy-start | bytes 393220
  68.0 131.6 %all-gather.2.cloned.1.call-start = ((), (), s32[]{:S(2)}) async-start(), calls=%async_computation.3 | async-start | bytes 2359296 | tf_op jit(solution)/shard_map/all_gather | solution.py:248
  140.9 9.6 %collective-permute-start.4 = (f32[256,256]{1,0:T(8,128)S(1)}, f32[256,256]{1,0:T(8,128)S(1)}, u32[]{:S(2)}, u32[]{:S(2)}) collective-permute-start(f32[256,256]{1,0:T(8,128)S(1)} %constant_dynamic-slice_fusion), channel_id=1, source_target_pairs={{0,16},{16,0},{1,17},{17,1},{2,18},{18,2},{3,19},{19,3},{4,20},{20... | collective-permute-start | bytes 786440 | tf_op jit(solution)/shard_map/ppermute | solution.py:183
  152.6 6.6 %collective-permute-start.13 = (bf16[256,256]{1,0:T(8,128)(2,1)S(1)}, bf16[256,256]{1,0:T(8,128)(2,1)S(1)}, u32[]{:S(2)}, u32[]{:S(2)}) collective-permute-start(bf16[256,256]{1,0:T(8,128)(2,1)S(1)} %convolution_convert_fusion), channel_id=1, source_target_pairs={{0,16},{16,0},{1,17},{17,1},{2,18},{18,2},{3,19},{19,3},{4,20},{20... | collective-permute-start | bytes 393224 | tf_op jit(solution)/shard_map/ppermute | solution.py:188
  159.9 153.4 %reduce-scatter.5.cloned.1.call-start = ((), (), s32[]{:S(2)}) async-start(), calls=%async_computation.4 | async-start | bytes 2359296 | tf_op jit(solution)/shard_map/reduce_scatter | solution.py:259
  199.6 4.4 %collective-permute-start.14 = (bf16[4096,256]{1,0:T(8,128)(2,1)}, bf16[4096,256]{1,0:T(8,128)(2,1)S(1)}, u32[]{:S(2)}, u32[]{:S(2)}) collective-permute-start(bf16[4096,256]{1,0:T(8,128)(2,1)} %all-gather.2.cloned.1.call-done), channel_id=1, source_target_pairs={{0,1},{1,0},{2,3},{3,2},{4,5},{5,4},{6,7},{7,6},{8,9},{9,8},{10,11... | collective-permute-start | bytes 6291464 | tf_op jit(solution)/shard_map/ppermute | solution.py:249
  204.0 1.3 copy-start.3
  205.3 1.6 copy-start.1
  229.1 1.6 collective-permute-start.5
  230.8 8.4 %collective-permute-start.6 = (f32[256,256]{1,0:T(8,128)S(1)}, f32[256,256]{1,0:T(8,128)S(1)}, u32[]{:S(2)}, u32[]{:S(2)}) collective-permute-start(f32[256,256]{1,0:T(8,128)S(1)} %add.101), channel_id=1, source_target_pairs={{0,2},{1,3},{2,0},{3,1},{4,6},{5,7},{6,4},{7,5},{8,10},{9,11},{10,... | collective-permute-start | bytes 786440 | tf_op jit(solution)/shard_map/ppermute | solution.py:162
  239.3 25.7 %collective-permute-start.7 = (f32[256,256]{1,0:T(8,128)S(1)}, f32[256,256]{1,0:T(8,128)S(1)}, u32[]{:S(2)}, u32[]{:S(2)}) collective-permute-start(f32[256,256]{1,0:T(8,128)S(1)} %add.102), channel_id=1, source_target_pairs={{0,6},{1,7},{2,4},{3,5},{4,2},{5,3},{6,0},{7,1},{8,14},{9,15},{10,... | collective-permute-start | bytes 786440 | tf_op jit(solution)/shard_map/ppermute | solution.py:162
  265.0 8.5 %collective-permute-start.8 = (f32[256,256]{1,0:T(8,128)S(1)}, f32[256,256]{1,0:T(8,128)S(1)}, u32[]{:S(2)}, u32[]{:S(2)}) collective-permute-start(f32[256,256]{1,0:T(8,128)S(1)} %add.103), channel_id=1, source_target_pairs={{0,14},{1,15},{2,12},{3,13},{4,10},{5,11},{6,8},{7,9},{8,6},{9,7},... | collective-permute-start | bytes 786440 | tf_op jit(solution)/shard_map/ppermute | solution.py:162
  273.5 12.5 %collective-permute-start.9 = (f32[256,256]{1,0:T(8,128)S(1)}, f32[256,256]{1,0:T(8,128)S(1)}, u32[]{:S(2)}, u32[]{:S(2)}) collective-permute-start(f32[256,256]{1,0:T(8,128)S(1)} %add.104), channel_id=1, source_target_pairs={{0,32},{1,33},{2,34},{3,35},{4,36},{5,37},{6,38},{7,39},{8,40},{9,... | collective-permute-start | bytes 786440 | tf_op jit(solution)/shard_map/ppermute | solution.py:162
  286.1 8.5 %collective-permute-start.10 = (f32[256,256]{1,0:T(8,128)S(1)}, f32[256,256]{1,0:T(8,128)S(1)}, u32[]{:S(2)}, u32[]{:S(2)}) collective-permute-start(f32[256,256]{1,0:T(8,128)S(1)} %add.105), channel_id=1, source_target_pairs={{0,64},{1,65},{2,66},{3,67},{4,68},{5,69},{6,70},{7,71},{8,72},{9,... | collective-permute-start | bytes 786440 | tf_op jit(solution)/shard_map/ppermute | solution.py:162
  294.6 7.5 %collective-permute-start.11 = (f32[256,256]{1,0:T(8,128)S(1)}, f32[256,256]{1,0:T(8,128)S(1)}, u32[]{:S(2)}, u32[]{:S(2)}) collective-permute-start(f32[256,256]{1,0:T(8,128)S(1)} %add.106), channel_id=1, source_target_pairs={{0,128},{1,129},{2,130},{3,131},{4,132},{5,133},{6,134},{7,135},{8... | collective-permute-start | bytes 786440 | tf_op jit(solution)/shard_map/ppermute | solution.py:162
  302.1 10.5 %collective-permute-start.12 = (f32[256,256]{1,0:T(8,128)S(1)}, f32[256,256]{1,0:T(8,128)S(1)}, u32[]{:S(2)}, u32[]{:S(2)}) collective-permute-start(f32[256,256]{1,0:T(8,128)S(1)} %add.107), channel_id=1, source_target_pairs={{0,16},{1,17},{2,18},{3,19},{4,20},{5,21},{6,22},{7,23},{8,24},{9,... | collective-permute-start | bytes 786440 | tf_op jit(solution)/shard_map/ppermute | solution.py:162
Sparse Core Ops, SparseCore 0:
  68.1 71.7 reduce-scatter.2
  160.1 39.4 all-gather.1
  229.0 62.1 reduce-scatter.4

commit v12 on v11

--- a/solution.py
+++ b/solution.py
@@ -218,7 +218,9 @@
     core_i = chunk % core_n
     placed = (core_i * mid_n * high_n + mid_i * high_n + high_i) * per_chunk + row_ids % per_chunk
     kept = (core_i == lax.axis_index("core")).astype(jnp.int32)
-    fwd_placed = (kept * mid_n * high_n + mid_i * high_n + high_i) * per_chunk + row_ids % per_chunk
+    high_kept = (high_i == lax.axis_index("high")).astype(jnp.int32)
+    fwd_placed = (kept * mid_n * high_n + mid_i * high_n + high_kept) * per_chunk
+    fwd_placed = fwd_placed + row_ids % per_chunk
     weights_all = tile_weights[0, 0]
     live = tile_count[0, 0].reshape(1)
     source = doubling_gather(features, "row", row_n)
@@ -230,7 +232,10 @@
         partial_value[:half], "core", [(0, 1), (1, 0)]
     )
     partial_value = lax.psum_scatter(partial_value, "mid", scatter_dimension=0, tiled=True)
-    partial_value = pair_scatter(partial_value, "high")
+    half = partial_value.shape[0] // 2
+    partial_value = partial_value[half:] + lax.ppermute(
+        partial_value[:half], "high", [(0, 1), (1, 0)]
+    )
     aggregate = partial_value.astype(jnp.bfloat16)
     hidden, grad_own = dense_layer(aggregate, weight, cotangent)
     weight_part = lax.dot_general(

time: 324 us -> 326 us (level)
  waiting for transfers between devices: 202 us -> 210 us
  Pallas kernels: 40.9 us -> 34 us
    ppermute x8, waiting for transfers between devices: 49.6 us -> 54.5 us  [butterfly_sum(): value = value + lax.ppermute(value, axes, pairs)]
    pallas_call x1, Pallas kernels: 22 us -> 18.1 us  [back_pass(): pl.pallas_call(functools.partial(back_kernel, per_block=per_block, scale=...]
    reduce_scatter x1, waiting for transfers between devices: 71.8 us -> 75.7 us  [on_device(): lax.psum_scatter(partial_value, 'mid', scatter_dimension=0, tiled=True)]
where the time goes in v12:
time: 326 us; the launch traced here: 324 us
  waiting for transfers between devices  210 us (64%)
  starting transfers between devices  44.6 us (14%)
  Pallas kernels  34 us (10%)
  between operations  14.6 us (4%)
  other arithmetic  10.8 us (3%)
  local copies, waits for them, and re-layouts  7.93 us (2%)
    reduce_scatter x1, waiting for transfers between devices, on_device(): lax.psum_scatter(partial_value, 'mid', scatter_dimension=0, tiled=True)  75.7 us
    ppermute x8, waiting for transfers between devices, butterfly_sum(): value = value + lax.ppermute(value, axes, pairs)  54.5 us
    all_gather x1, waiting for transfers between devices, on_device(): grad_source = lax.all_gather(grad_source, 'mid', axis=0, tiled=True)  39.6 us
    ppermute x8, starting transfers between devices, butterfly_sum(): value = value + lax.ppermute(value, axes, pairs)  33.7 us
    pallas_call x1, Pallas kernels, back_pass(): pl.pallas_call(functools.partial(back_kernel, per_block=per_block, scale=...  18.1 us
    ppermute x3, waiting for transfers between devices, doubling_gather(): other = lax.ppermute(value, axis, pairs)  17.8 us
    pallas_call x1, Pallas kernels, slot_pass(): pl.pallas_call(functools.partial(slot_kernel, per_block=per_block, scale=...  15.9 us
    ppermute x1, waiting for transfers between devices, on_device(): lax.ppermute(partial_value[:half], 'high', [(0, 1), (1, 0)])  7.37 us
  transfers between devices with their start and end apart: 18, of which 17 were waited for; matrix products, arithmetic and copies ran while one was open for 1% of the time, Pallas kernels for 0%

profile of v12, /device:TPU:8, one launch (start us, length us, event | category | flops | bytes accessed | tf_op | source)
XLA Modules:
  0.0 323.7 jit_solution(16924654352513580301)
XLA Ops:
  7.2 1.6 collective-permute-start
  8.8 4.0 %collective-permute-done = bf16[256,256]{1,0:T(8,128)(2,1)S(1)} collective-permute-done((bf16[256,256]{1,0:T(8,128)(2,1)}, bf16[256,256]{1,0:T(8,128)(2,1)S(1)}, u32[]{:S(2)}, u32[]{:S(2)}) %collective-permute-start) | collective-permute-done | bytes 131104 | tf_op jit(solution)/shard_map/ppermute | solution.py:170
  13.7 3.1 collective-permute-start.1
  16.8 5.7 %collective-permute-done.1 = bf16[512,256]{1,0:T(8,128)(2,1)S(1)} collective-permute-done((bf16[512,256]{1,0:T(8,128)(2,1)S(1)}, bf16[512,256]{1,0:T(8,128)(2,1)S(1)}, u32[]{:S(2)}, u32[]{:S(2)}) %collective-permute-start.1) | collective-permute-done | bytes 262176 | tf_op jit(solution)/shard_map/ppermute | solution.py:170
  26.6 8.1 %collective-permute-done.2 = bf16[1024,256]{1,0:T(8,128)(2,1)S(1)} collective-permute-done((bf16[1024,256]{1,0:T(8,128)(2,1)S(1)}, bf16[1024,256]{1,0:T(8,128)(2,1)S(1)}, u32[]{:S(2)}, u32[]{:S(2)}) %collective-permute-start.2) | collective-permute-done | bytes 524320 | tf_op jit(solution)/shard_map/ppermute | solution.py:170
  35.0 15.9 %shard_map.94 = f32[64,128,256]{2,1,0:T(8,128)} custom-call(s32[1]{0:T(128)} %bitcast.17.live_ref, s32[176]{0:T(256)S(1)} %multiply_add_fusion.rows_ref, s32[176]{0:T(256)S(1)} %bitcast.21, s32[176,128,128]{2,1,0:T(8,128)} %bitcast.23, bf16[16,128,256]{2,1,0:T(8,128)(2,1)S(1)} %bitcast.19), custom_call_target="tpu_custom_call" | custom-call | tf_op jit(solution)/shard_map/pallas_call | solution.py:96
  50.9 4.0 %fusion.8 = (f32[32,128,256]{2,1,0:T(8,128)S(1)}, f32[32,128,256]{2,1,0:T(8,128)S(1)}) fusion(f32[64,128,256]{2,1,0:T(8,128)} %shard_map.94), kind=kLoop, calls=%fused_computation.54 | loop fusion | bytes 16777216 | tf_op jit(solution)/shard_map/slice | solution.py:231
  55.4 6.8 %collective-permute-done.3 = f32[4096,256]{1,0:T(8,128)S(1)} collective-permute-done((f32[4096,256]{1,0:T(8,128)S(1)}, f32[4096,256]{1,0:T(8,128)S(1)}, u32[]{:S(2)}, u32[]{:S(2)}) %collective-permute-start.3) | collective-permute-done | bytes 4194336 | tf_op jit(solution)/shard_map/ppermute | solution.py:231
  62.2 3.0 bitcast_add_fusion
  65.3 75.7 %reduce-scatter.3.cloned.1.call-done = f32[512,256]{1,0:T(8,128)} async-done(((f32[4096,256]{1,0:T(8,128)}), f32[512,256]{1,0:T(8,128)}) %reduce-scatter.3.cloned.1.call-update) | async-done | bytes 524304 | tf_op jit(solution)/shard_map/reduce_scatter | solution.py:234
  141.9 2.2 collective-permute-start.4
  144.1 7.4 %collective-permute-done.4 = f32[256,256]{1,0:T(8,128)S(1)} collective-permute-done((f32[256,256]{1,0:T(8,128)S(1)}, f32[256,256]{1,0:T(8,128)S(1)}, u32[]{:S(2)}, u32[]{:S(2)}) %collective-permute-start.4) | collective-permute-done | bytes 262176 | tf_op jit(solution)/shard_map/ppermute | solution.py:236
  153.7 2.2 collective-permute-start.13
  155.9 4.4 %collective-permute-done.13 = bf16[256,256]{1,0:T(8,128)(2,1)S(1)} collective-permute-done((bf16[256,256]{1,0:T(8,128)(2,1)S(1)}, bf16[256,256]{1,0:T(8,128)(2,1)S(1)}, u32[]{:S(2)}, u32[]{:S(2)}) %collective-permute-start.13) | collective-permute-done | bytes 131104 | tf_op jit(solution)/shard_map/ppermute | solution.py:188
  161.1 39.6 %all-gather.2.cloned.1.call-done = bf16[4096,256]{1,0:T(8,128)(2,1)} async-done(((bf16[512,256]{1,0:T(8,128)(2,1)}), bf16[4096,256]{1,0:T(8,128)(2,1)}) %all-gather.2.cloned.1.call-update) | async-done | bytes 2097168 | tf_op jit(solution)/shard_map/all_gather | solution.py:253
  200.7 4.4 %collective-permute-done.14 = bf16[4096,256]{1,0:T(8,128)(2,1)S(1)} collective-permute-done((bf16[4096,256]{1,0:T(8,128)(2,1)}, bf16[4096,256]{1,0:T(8,128)(2,1)S(1)}, u32[]{:S(2)}, u32[]{:S(2)}) %collective-permute-start.14) | collective-permute-done | bytes 2097184 | tf_op jit(solution)/shard_map/ppermute | solution.py:254
  205.0 1.3 copy-done.3
  206.4 1.6 copy-done.1
  208.0 18.1 %shard_map.95 = f32[16,128,256]{2,1,0:T(8,128)} custom-call(s32[1]{0:T(128)} %bitcast.18.live_ref, s32[176]{0:T(256)S(1)} %get-tuple-element.5.rows_ref, s32[176]{0:T(256)S(1)} %bitcast.22, s32[176]{0:T(256)S(1)} %get-tuple-element.3.halves_ref, s32[176,128,128]{2,1,0:T(8,128)} %bitcast.24, bf16[32,128,256]{2,1,0:T(8,128)(2,1)S(1)} %bitcast.20, ...), custom_call_target="tpu_custom_call" | custom-call | tf_op jit(solution)/shard_map/pallas_call | solution.py:128
  226.4 4.3 %collective-permute-start.5 = (f32[256,256]{1,0:T(8,128)S(1)}, f32[256,256]{1,0:T(8,128)S(1)}, u32[]{:S(2)}, u32[]{:S(2)}) collective-permute-start(f32[256,256]{1,0:T(8,128)S(1)} %fusion.9), channel_id=1, source_target_pairs={{0,1},{1,0},{2,3},{3,2},{4,5},{5,4},{6,7},{7,6},{8,9},{9,8},{10,11... | collective-permute-start | bytes 786440 | tf_op jit(solution)/shard_map/ppermute | solution.py:162
  231.9 8.6 %collective-permute-done.6 = f32[256,256]{1,0:T(8,128)S(1)} collective-permute-done((f32[256,256]{1,0:T(8,128)S(1)}, f32[256,256]{1,0:T(8,128)S(1)}, u32[]{:S(2)}, u32[]{:S(2)}) %collective-permute-start.6) | collective-permute-done | bytes 262176 | tf_op jit(solution)/shard_map/ppermute | solution.py:162
  241.4 9.0 %collective-permute-done.7 = f32[256,256]{1,0:T(8,128)S(1)} collective-permute-done((f32[256,256]{1,0:T(8,128)S(1)}, f32[256,256]{1,0:T(8,128)S(1)}, u32[]{:S(2)}, u32[]{:S(2)}) %collective-permute-start.7) | collective-permute-done | bytes 262176 | tf_op jit(solution)/shard_map/ppermute | solution.py:162
  250.5 20.1 %collective-permute-start.8 = (f32[256,256]{1,0:T(8,128)S(1)}, f32[256,256]{1,0:T(8,128)S(1)}, u32[]{:S(2)}, u32[]{:S(2)}) collective-permute-start(f32[256,256]{1,0:T(8,128)S(1)} %add.95), channel_id=1, source_target_pairs={{0,14},{1,15},{2,12},{3,13},{4,10},{5,11},{6,8},{7,9},{8,6},{9,7},... | collective-permute-start | bytes 786440 | tf_op jit(solution)/shard_map/ppermute | solution.py:162
  270.6 10.5 %collective-permute-done.8 = f32[256,256]{1,0:T(8,128)S(1)} collective-permute-done((f32[256,256]{1,0:T(8,128)S(1)}, f32[256,256]{1,0:T(8,128)S(1)}, u32[]{:S(2)}, u32[]{:S(2)}) %collective-permute-start.8) | collective-permute-done | bytes 262176 | tf_op jit(solution)/shard_map/ppermute | solution.py:162
  281.2 2.9 collective-permute-start.9
  284.1 6.5 %collective-permute-done.9 = f32[256,256]{1,0:T(8,128)S(1)} collective-permute-done((f32[256,256]{1,0:T(8,128)S(1)}, f32[256,256]{1,0:T(8,128)S(1)}, u32[]{:S(2)}, u32[]{:S(2)}) %collective-permute-start.9) | collective-permute-done | bytes 262176 | tf_op jit(solution)/shard_map/ppermute | solution.py:162
  291.4 7.2 %collective-permute-done.10 = f32[256,256]{1,0:T(8,128)S(1)} collective-permute-done((f32[256,256]{1,0:T(8,128)S(1)}, f32[256,256]{1,0:T(8,128)S(1)}, u32[]{:S(2)}, u32[]{:S(2)}) %collective-permute-start.10) | collective-permute-done | bytes 262176 | tf_op jit(solution)/shard_map/ppermute | solution.py:162
  298.6 1.2 collective-permute-start.11
  299.8 6.9 %collective-permute-done.11 = f32[256,256]{1,0:T(8,128)S(1)} collective-permute-done((f32[256,256]{1,0:T(8,128)S(1)}, f32[256,256]{1,0:T(8,128)S(1)}, u32[]{:S(2)}, u32[]{:S(2)}) %collective-permute-start.11) | collective-permute-done | bytes 262176 | tf_op jit(solution)/shard_map/ppermute | solution.py:162
  306.8 3.4 %collective-permute-start.12 = (f32[256,256]{1,0:T(8,128)S(1)}, f32[256,256]{1,0:T(8,128)S(1)}, u32[]{:S(2)}, u32[]{:S(2)}) collective-permute-start(f32[256,256]{1,0:T(8,128)S(1)} %add.99), channel_id=1, source_target_pairs={{0,16},{1,17},{2,18},{3,19},{4,20},{5,21},{6,22},{7,23},{8,24},{9,... | collective-permute-start | bytes 786440 | tf_op jit(solution)/shard_map/ppermute | solution.py:162
  310.2 4.6 %collective-permute-done.12 = f32[256,256]{1,0:T(8,128)S(1)} collective-permute-done((f32[256,256]{1,0:T(8,128)S(1)}, f32[256,256]{1,0:T(8,128)S(1)}, u32[]{:S(2)}, u32[]{:S(2)}) %collective-permute-start.12) | collective-permute-done | bytes 262176 | tf_op jit(solution)/shard_map/ppermute | solution.py:162
  315.5 1.6 convert_element_type.32
  (46 shorter events, 13.3 us)
Async XLA Ops:
  7.2 145.3 %copy-start = (bf16[256,256]{1,0:T(8,128)(2,1)S(1)}, bf16[256,256]{1,0:T(8,128)(2,1)}, u32[]{:S(2)}) copy-start(bf16[256,256]{1,0:T(8,128)(2,1)} %param.8) | copy-start | bytes 393220
  7.2 27.8 %copy-start.2 = (s32[1,1,176]{2,1,0:T(1,128)S(1)}, s32[1,1,176]{2,1,0:T(1,128)}, u32[]{:S(2)}) copy-start(s32[1,1,176]{2,1,0:T(1,128)} %param.11) | copy-start | bytes 2116
  7.2 133.8 %reduce-scatter.3.cloned.1.call-start = ((), (), s32[]{:S(2)}) async-start(), calls=%async_computation.2 | async-start | bytes 4718592 | tf_op jit(solution)/shard_map/reduce_scatter | solution.py:234
  7.2 5.5 %collective-permute-start = (bf16[256,256]{1,0:T(8,128)(2,1)}, bf16[256,256]{1,0:T(8,128)(2,1)S(1)}, u32[]{:S(2)}, u32[]{:S(2)}) collective-permute-start(bf16[256,256]{1,0:T(8,128)(2,1)} %param.7), channel_id=1, source_target_pairs={{0,32},{32,0},{64,96},{96,64},{128,160},{160,128},{192,224},{224,1... | collective-permute-start | bytes 393224 | tf_op jit(solution)/shard_map/ppermute | solution.py:170
  13.7 8.8 %collective-permute-start.1 = (bf16[512,256]{1,0:T(8,128)(2,1)S(1)}, bf16[512,256]{1,0:T(8,128)(2,1)S(1)}, u32[]{:S(2)}, u32[]{:S(2)}) collective-permute-start(bf16[512,256]{1,0:T(8,128)(2,1)S(1)} %pad_maximum_fusion.2), channel_id=1, source_target_pairs={{0,64},{32,96},{64,0},{96,32},{128,192},{160,224},{192,128},{224,1... | collective-permute-start | bytes 786440 | tf_op jit(solution)/shard_map/ppermute | solution.py:170
  22.7 12.0 %collective-permute-start.2 = (bf16[1024,256]{1,0:T(8,128)(2,1)S(1)}, bf16[1024,256]{1,0:T(8,128)(2,1)S(1)}, u32[]{:S(2)}, u32[]{:S(2)}) collective-permute-start(bf16[1024,256]{1,0:T(8,128)(2,1)S(1)} %pad_maximum_fusion.1), channel_id=1, source_target_pairs={{0,128},{32,160},{64,192},{96,224},{128,0},{160,32},{192,64},{224,... | collective-permute-start | bytes 1572872 | tf_op jit(solution)/shard_map/ppermute | solution.py:170
  54.9 7.3 %collective-permute-start.3 = (f32[4096,256]{1,0:T(8,128)S(1)}, f32[4096,256]{1,0:T(8,128)S(1)}, u32[]{:S(2)}, u32[]{:S(2)}) collective-permute-start(f32[4096,256]{1,0:T(8,128)S(1)} %bitcast.25), channel_id=1, source_target_pairs={{0,1},{1,0},{2,3},{3,2},{4,5},{5,4},{6,7},{7,6},{8,9},{9,8},{10,11... | collective-permute-start | bytes 12582920 | tf_op jit(solution)/shard_map/ppermute | solution.py:231
  65.2 87.3 %copy-start.4 = (bf16[256,256]{1,0:T(8,128)(2,1)S(1)}, bf16[256,256]{1,0:T(8,128)(2,1)}, u32[]{:S(2)}) copy-start(bf16[256,256]{1,0:T(8,128)(2,1)} %param.9) | copy-start | bytes 393220
  65.2 135.4 %all-gather.2.cloned.1.call-start = ((), (), s32[]{:S(2)}) async-start(), calls=%async_computation.3 | async-start | bytes 2359296 | tf_op jit(solution)/shard_map/all_gather | solution.py:253
  141.9 9.6 %collective-permute-start.4 = (f32[256,256]{1,0:T(8,128)S(1)}, f32[256,256]{1,0:T(8,128)S(1)}, u32[]{:S(2)}, u32[]{:S(2)}) collective-permute-start(f32[256,256]{1,0:T(8,128)S(1)} %slice.27), channel_id=1, source_target_pairs={{0,16},{16,0},{1,17},{17,1},{2,18},{18,2},{3,19},{19,3},{4,20},{20... | collective-permute-start | bytes 786440 | tf_op jit(solution)/shard_map/ppermute | solution.py:236
  153.7 6.6 %collective-permute-start.13 = (bf16[256,256]{1,0:T(8,128)(2,1)S(1)}, bf16[256,256]{1,0:T(8,128)(2,1)S(1)}, u32[]{:S(2)}, u32[]{:S(2)}) collective-permute-start(bf16[256,256]{1,0:T(8,128)(2,1)S(1)} %convolution_convert_fusion), channel_id=1, source_target_pairs={{0,16},{16,0},{1,17},{17,1},{2,18},{18,2},{3,19},{19,3},{4,20},{20... | collective-permute-start | bytes 393224 | tf_op jit(solution)/shard_map/ppermute | solution.py:188
  161.0 154.5 %reduce-scatter.5.cloned.1.call-start = ((), (), s32[]{:S(2)}) async-start(), calls=%async_computation.4 | async-start | bytes 2359296 | tf_op jit(solution)/shard_map/reduce_scatter | solution.py:264
  200.7 4.4 %collective-permute-start.14 = (bf16[4096,256]{1,0:T(8,128)(2,1)}, bf16[4096,256]{1,0:T(8,128)(2,1)S(1)}, u32[]{:S(2)}, u32[]{:S(2)}) collective-permute-start(bf16[4096,256]{1,0:T(8,128)(2,1)} %all-gather.2.cloned.1.call-done), channel_id=1, source_target_pairs={{0,1},{1,0},{2,3},{3,2},{4,5},{5,4},{6,7},{7,6},{8,9},{9,8},{10,11... | collective-permute-start | bytes 6291464 | tf_op jit(solution)/shard_map/ppermute | solution.py:254
  205.0 1.3 copy-start.3
  206.4 1.6 copy-start.1
  226.4 5.4 %collective-permute-start.5 = (f32[256,256]{1,0:T(8,128)S(1)}, f32[256,256]{1,0:T(8,128)S(1)}, u32[]{:S(2)}, u32[]{:S(2)}) collective-permute-start(f32[256,256]{1,0:T(8,128)S(1)} %fusion.9), channel_id=1, source_target_pairs={{0,1},{1,0},{2,3},{3,2},{4,5},{5,4},{6,7},{7,6},{8,9},{9,8},{10,11... | collective-permute-start | bytes 786440 | tf_op jit(solution)/shard_map/ppermute | solution.py:162
  231.8 8.7 %collective-permute-start.6 = (f32[256,256]{1,0:T(8,128)S(1)}, f32[256,256]{1,0:T(8,128)S(1)}, u32[]{:S(2)}, u32[]{:S(2)}) collective-permute-start(f32[256,256]{1,0:T(8,128)S(1)} %add.93), channel_id=1, source_target_pairs={{0,2},{1,3},{2,0},{3,1},{4,6},{5,7},{6,4},{7,5},{8,10},{9,11},{10,... | collective-permute-start | bytes 786440 | tf_op jit(solution)/shard_map/ppermute | solution.py:162
  240.6 9.9 %collective-permute-start.7 = (f32[256,256]{1,0:T(8,128)S(1)}, f32[256,256]{1,0:T(8,128)S(1)}, u32[]{:S(2)}, u32[]{:S(2)}) collective-permute-start(f32[256,256]{1,0:T(8,128)S(1)} %add.94), channel_id=1, source_target_pairs={{0,6},{1,7},{2,4},{3,5},{4,2},{5,3},{6,0},{7,1},{8,14},{9,15},{10,... | collective-permute-start | bytes 786440 | tf_op jit(solution)/shard_map/ppermute | solution.py:162
  250.5 30.6 %collective-permute-start.8 = (f32[256,256]{1,0:T(8,128)S(1)}, f32[256,256]{1,0:T(8,128)S(1)}, u32[]{:S(2)}, u32[]{:S(2)}) collective-permute-start(f32[256,256]{1,0:T(8,128)S(1)} %add.95), channel_id=1, source_target_pairs={{0,14},{1,15},{2,12},{3,13},{4,10},{5,11},{6,8},{7,9},{8,6},{9,7},... | collective-permute-start | bytes 786440 | tf_op jit(solution)/shard_map/ppermute | solution.py:162
  281.2 9.4 %collective-permute-start.9 = (f32[256,256]{1,0:T(8,128)S(1)}, f32[256,256]{1,0:T(8,128)S(1)}, u32[]{:S(2)}, u32[]{:S(2)}) collective-permute-start(f32[256,256]{1,0:T(8,128)S(1)} %add.96), channel_id=1, source_target_pairs={{0,32},{1,33},{2,34},{3,35},{4,36},{5,37},{6,38},{7,39},{8,40},{9,... | collective-permute-start | bytes 786440 | tf_op jit(solution)/shard_map/ppermute | solution.py:162
  290.6 8.0 %collective-permute-start.10 = (f32[256,256]{1,0:T(8,128)S(1)}, f32[256,256]{1,0:T(8,128)S(1)}, u32[]{:S(2)}, u32[]{:S(2)}) collective-permute-start(f32[256,256]{1,0:T(8,128)S(1)} %add.97), channel_id=1, source_target_pairs={{0,64},{1,65},{2,66},{3,67},{4,68},{5,69},{6,70},{7,71},{8,72},{9,... | collective-permute-start | bytes 786440 | tf_op jit(solution)/shard_map/ppermute | solution.py:162
  298.6 8.1 %collective-permute-start.11 = (f32[256,256]{1,0:T(8,128)S(1)}, f32[256,256]{1,0:T(8,128)S(1)}, u32[]{:S(2)}, u32[]{:S(2)}) collective-permute-start(f32[256,256]{1,0:T(8,128)S(1)} %add.98), channel_id=1, source_target_pairs={{0,128},{1,129},{2,130},{3,131},{4,132},{5,133},{6,134},{7,135},{8... | collective-permute-start | bytes 786440 | tf_op jit(solution)/shard_map/ppermute | solution.py:162
  306.8 8.0 %collective-permute-start.12 = (f32[256,256]{1,0:T(8,128)S(1)}, f32[256,256]{1,0:T(8,128)S(1)}, u32[]{:S(2)}, u32[]{:S(2)}) collective-permute-start(f32[256,256]{1,0:T(8,128)S(1)} %add.99), channel_id=1, source_target_pairs={{0,16},{1,17},{2,18},{3,19},{4,20},{5,21},{6,22},{7,23},{8,24},{9,... | collective-permute-start | bytes 786440 | tf_op jit(solution)/shard_map/ppermute | solution.py:162
Sparse Core Ops, SparseCore 0:
  65.3 75.5 reduce-scatter.2
  161.1 39.4 all-gather.1
  226.3 65.6 reduce-scatter.4
